TPU v7x, 256 devices: a whole 4x4x8 slice. The times are simulated.
256 devices in a mesh: row: 16 (over z_hi, y, core), col: 4 (over z_lo), pblk: 4 (over x).
Axes of the slice: x: 4, y: 4, z: 8 (z_hi: 2, z_lo: 4; z = z_hi * 4 + z_lo), core: 2. Of those that a mesh axis runs over, the one named last changes fastest.
Arguments:
- left_feat: int32 [2048, 256], P(('row', 'col', 'pblk')), may hold values from 0 to 255
- right_feat: int32 [4, 4, 64, 256], P('col', 'pblk', 'row'), may hold values from 0 to 255
- embed: bfloat16 [1024, 256], replicated, may hold values from -12 to 12
- conv_w: bfloat16 [8, 768, 256], replicated, may hold values from -0.01953125 to 0.01953125
- head: float32 [256], replicated, may hold values from -0.078125 to 0.078125
- assign: int32 [8], replicated, may hold values from 0 to 3, as said below
- proj_delta: bfloat16 [4, 256, 128], replicated, may hold values from -0.375 to 0.375
- proj_input: bfloat16 [4, 768, 128], replicated, may hold values from -0.21875 to 0.21875
Outputs:
- kernel: float32 [2048, 1024], P('row', ('col', 'pblk'))
Inputs may be any that keep to these rules, and one draw needn't show every extreme that they name: `assign`: every one of the 4 blocks is named by exactly 2 layers.
All inputs are finite; a program needn't handle non-finite values.
Results may differ from a plain program's by a relative error of at most 0.00036.
Values may be sent and summed in bfloat16 or wider, within the bound.
No kernel may reach another device: no remote copies, remote signals or barrier semaphores. Data moves between devices by JAX's collectives and lax.ppermute only.
A program may use at most 128 MiB of HBM per device.

v0:
```python
import jax
import jax.numpy as jnp
from jax import lax
from jax.sharding import PartitionSpec as P

SEQ = 64
NFEAT = 4
VOCAB = 256
LAYERS = 8
PR = 128
PS = 128


def shift_wide(inputs):
    blank = jnp.zeros_like(inputs[:, :1])
    earlier = jnp.concatenate([blank, inputs[:, :-1]], 1)
    later_cells = jnp.concatenate([inputs[:, 1:], blank], 1)
    return jnp.concatenate([earlier, inputs, later_cells], 2)


def panels(features, embed, conv_w, head, assign, proj_delta, proj_input):
    examples = features.shape[0]
    blocks_here = proj_delta.shape[0]
    offsets = jnp.arange(NFEAT, dtype=jnp.int32) * VOCAB
    table_rows = features.reshape(examples, SEQ, NFEAT) + offsets
    table_ids = jnp.arange(NFEAT * VOCAB, dtype=jnp.int32)
    onehot = (table_rows[:, :, 0:1] == table_ids).astype(jnp.bfloat16)
    for field in range(1, NFEAT):
        onehot = onehot + (table_rows[:, :, field : field + 1] == table_ids).astype(jnp.bfloat16)
    hidden = jnp.einsum("esv,vc->esc", onehot, embed, preferred_element_type=jnp.float32)
    wides = []
    pres = []
    for layer in range(LAYERS):
        wide_input = shift_wide(hidden.astype(jnp.bfloat16))
        pre_act = jnp.einsum(
            "esk,kc->esc", wide_input, conv_w[layer], preferred_element_type=jnp.float32
        )
        wides.append(wide_input)
        pres.append(pre_act)
        hidden = hidden + jax.nn.silu(pre_act)
    grad_h = jnp.broadcast_to(head / SEQ, hidden.shape)
    block_ids = jnp.arange(blocks_here, dtype=jnp.int32)
    panel = jnp.zeros((examples, blocks_here, PR, PS), jnp.float32)
    for layer in range(LAYERS - 1, -1, -1):
        pre_act = pres[layer]
        sigmoid_z = jax.nn.sigmoid(pre_act)
        delta_low = (grad_h * sigmoid_z * (1.0 + pre_act * (1.0 - sigmoid_z))).astype(jnp.bfloat16)
        block_pick = (assign[layer] == block_ids).astype(jnp.float32)
        rows_table = jnp.einsum("b,bcr->cr", block_pick, proj_delta.astype(jnp.float32)).astype(
            jnp.bfloat16
        )
        cols_table = jnp.einsum("b,bkt->kt", block_pick, proj_input.astype(jnp.float32)).astype(
            jnp.bfloat16
        )
        left_side = jnp.einsum(
            "esc,cr->esr", delta_low, rows_table, preferred_element_type=jnp.float32
        )
        right_side = jnp.einsum(
            "esk,kt->est", wides[layer], cols_table, preferred_element_type=jnp.float32
        )
        projected = jnp.einsum(
            "esr,est->ert", left_side, right_side, precision=lax.Precision.HIGHEST
        )
        panel = panel + block_pick[None, :, None, None] * projected[:, None]
        if layer > 0:
            back_wide = jnp.einsum(
                "esc,kc->esk", delta_low, conv_w[layer], preferred_element_type=jnp.float32
            )
            width = grad_h.shape[2]
            first_third = back_wide[:, :, :width]
            last_third = back_wide[:, :, 2 * width :]
            blank = jnp.zeros_like(first_third[:, :1])
            grad_input = back_wide[:, :, width : 2 * width]
            grad_input = grad_input + jnp.concatenate([first_third[:, 1:], blank], 1)
            grad_input = grad_input + jnp.concatenate([blank, last_third[:, :-1]], 1)
            grad_h = grad_h + grad_input
    return panel.reshape(examples, blocks_here, PR * PS).astype(jnp.bfloat16)


def on_device(left_feat, right_feat, embed, conv_w, head, assign, proj_delta, proj_input):
    row_count = lax.axis_size("row")
    blk_count = lax.axis_size("pblk")
    left_each = left_feat.shape[0]
    right_each = right_feat.shape[2]
    right_local = right_feat.reshape(right_each, right_feat.shape[3])
    own_features = jnp.concatenate([left_feat, right_local], 0)
    panel = panels(own_features, embed, conv_w, head, assign, proj_delta, proj_input)
    left_part = panel[:left_each]
    right_part = panel[left_each:]
    left_one, right_one = (
        lax.all_to_all(left_part, "pblk", split_axis=1, concat_axis=0, tiled=True),
        lax.all_to_all(right_part, "pblk", split_axis=1, concat_axis=0, tiled=True),
    )
    left_panel = lax.all_gather(left_one[:, 0], "col", axis=0, tiled=True)
    partial_tile = jnp.einsum(
        "lq,rq->lr",
        left_panel,
        lax.all_gather(right_one[:, 0], "row", axis=0, tiled=True),
        preferred_element_type=jnp.float32,
    )
    tile_rows = partial_tile.shape[0]
    reordered = partial_tile.reshape(tile_rows, row_count, blk_count, right_each)
    reordered = jnp.transpose(reordered, (0, 2, 1, 3)).reshape(
        tile_rows, row_count * blk_count * right_each
    )
    return lax.psum_scatter(reordered, "pblk", scatter_dimension=1, tiled=True)


def solution(mesh):
    placed = (
        P(("row", "col", "pblk"), None),
        P("col", "pblk", "row", None),
        P(),
        P(),
        P(),
        P(),
        P(),
        P(),
    )
    return jax.shard_map(
        on_device, mesh=mesh, in_specs=placed, out_specs=P("row", ("col", "pblk")), check_vma=False
    )
```

profile of v0, /device:TPU:8, one launch (start us, length us, event | category | flops | bytes accessed | tf_op | source)
XLA Modules:
  0.0 330.6 jit_solution(17172536809581401327)
XLA Ops:
  6.5 1.6 fusion.261
  8.2 1.2 copy.39
  9.3 1.3 fusion.191
  10.7 1.6 fusion.161
  12.2 1.0 fusion.165
  13.2 0.9 fusion.169
  14.1 1.2 fusion.193
  15.4 0.9 fusion.173
  16.3 0.9 fusion.177
  17.2 1.2 fusion.195
  18.4 0.9 fusion.181
  19.4 0.9 fusion.185
  20.3 1.3 fusion.197
  21.5 0.9 fusion.189
  22.5 0.6 copy.41
  23.1 2.0 fusion.159
  25.1 2.0 fusion.163
  27.1 1.9 fusion.167
  29.0 2.0 fusion.171
  31.0 1.9 fusion.175
  32.9 1.2 fusion.179
  34.1 1.2 fusion.183
  35.3 1.2 fusion.187
  37.4 3.1 fusion.262
  41.1 1.4 copy-done.2
  42.5 0.5 fusion.233
  44.0 0.7 fusion.244
  45.5 0.5 fusion.234
  47.0 0.7 fusion.243
  48.4 0.5 fusion.235
  49.6 0.7 fusion.242
  50.9 0.5 add_convert_fusion.1
  52.1 0.6 multiply_convert_fusion.6
  53.4 1.4 fusion.263
  55.0 0.6 copy.59
  56.1 0.7 fusion.69
  57.1 1.4 fusion.264
  58.6 0.6 copy.60
  59.9 0.5 fusion.73
  60.7 1.4 fusion.265
  62.2 0.6 copy.61
  63.4 0.5 fusion.77
  64.2 1.4 fusion.266
  65.7 0.6 copy.62
  67.8 1.4 fusion.267
  69.3 0.6 copy.63
  70.1 0.7 multiply_convert_fusion.1
  71.5 1.4 fusion.268
  73.1 0.6 copy.64
  74.3 0.5 fusion.89
  75.1 1.4 fusion.269
  76.6 0.6 copy.65
  77.5 0.5 fusion.96
  78.0 1.4 fusion.270
  79.6 0.6 copy.66
  80.2 2.3 add_convert_fusion
  82.6 19.3 %all_to_all.30 = bf16[8,4,16384]{2,0,1:T(8,128)(2,1)} all-to-all(bf16[8,4,16384]{2,0,1:T(8,128)(2,1)S(1)} %slice.312), channel_id=1, replica_groups=mesh['row'=16,'col'=4,'pblk'=4] {'pblk'}, dimensions={1} | all-to-all | bytes 2097152 | tf_op jit(solution)/shard_map/all_to_all | solution.py:91
  102.1 11.0 %all_to_all.31 = bf16[4,4,16384]{2,0,1:T(4,128)(2,1)S(1)} all-to-all(bf16[4,4,16384]{2,0,1:T(4,128)(2,1)S(1)} %slice.313), channel_id=1, replica_groups=mesh['row'=16,'col'=4,'pblk'=4] {'pblk'}, dimensions={1} | all-to-all | bytes 1048576 | tf_op jit(solution)/shard_map/all_to_all | solution.py:92
  113.1 0.9 squeeze.78
  114.1 72.9 %all-gather.3.cloned.1.call-done = bf16[128,16384]{1,0:T(8,128)(2,1)} async-done(((bf16[32,16384]{1,0:T(8,128)(2,1)}), bf16[128,16384]{1,0:T(8,128)(2,1)}) %all-gather.3.cloned.1.call-update) | async-done | bytes 4194320 | tf_op jit(solution)/shard_map/all_gather | solution.py:94
  186.9 110.0 %all-gather.5.cloned.1.call-done = bf16[256,16384]{1,0:T(8,128)(2,1)} async-done(((bf16[16,16384]{1,0:T(8,128)(2,1)}), bf16[256,16384]{1,0:T(8,128)(2,1)}) %all-gather.5.cloned.1.call-update) | async-done | bytes 8388624 | tf_op jit(solution)/shard_map/all_gather | solution.py:98
  296.9 7.0 %fusion.271 = f32[128,256]{0,1:T(8,128)S(1)} fusion(bf16[128,16384]{1,0:T(8,128)(2,1)} %all-gather.3.cloned.1.call-done, bf16[256,16384]{1,0:T(8,128)(2,1)} %all-gather.5.cloned.1.call-done), kind=kOutput, calls=%fused_computation.290 | convolution fusion | flops 1073741824 | bytes 12713984 | tf_op jit(solution)/shard_map/lq,rq->lr/dot_general | solution.py:95
  303.9 0.7 copy.38
  304.6 19.2 %reduce-scatter.2.cloned.1.call-done = f32[128,64]{0,1:T(8,128)} async-done(((f32[128,256]{0,1:T(8,128)}), f32[128,64]{0,1:T(8,128)}) %reduce-scatter.2.cloned.1.call-update) | async-done | bytes 32784 | tf_op jit(solution)/shard_map/reduce_scatter | solution.py:106
  (89 shorter events, 14.6 us)
Async XLA Ops:
  6.5 30.8 %copy-start = (bf16[1024,256]{1,0:T(8,128)(2,1)S(1)}, bf16[1024,256]{1,0:T(8,128)(2,1)}, u32[]{:S(2)}) copy-start(bf16[1024,256]{1,0:T(8,128)(2,1)} %param.10) | copy-start | bytes 1572868
  6.5 15.9 %copy-start.3 = (bf16[4,768,128]{2,1,0:T(8,128)(2,1)S(1)}, bf16[4,768,128]{2,1,0:T(8,128)(2,1)}, u32[]{:S(2)}) copy-start(bf16[4,768,128]{2,1,0:T(8,128)(2,1)} %param.15) | copy-start | bytes 2359300
  6.5 180.4 %all-gather.3.cloned.1.call-start = ((), (), s32[]{:S(2)}) async-start(), calls=%async_computation.3 | async-start | bytes 5242880 | tf_op jit(solution)/shard_map/all_gather | solution.py:94
  32.9 3.6 %copy-start.6 = (f32[256]{0:T(256)S(1)}, f32[256]{0:T(256)}, u32[]{:S(2)}) copy-start(f32[256]{0:T(256)} %param.12) | copy-start | bytes 3076
  32.9 3.6 %copy-start.4 = (s32[8,256]{1,0:T(8,128)S(1)}, s32[8,256]{1,0:T(8,128)}, u32[]{:S(2)}) copy-start(s32[8,256]{1,0:T(8,128)} %param.8) | copy-start | bytes 24580
  32.9 3.8 %copy-start.5 = (s32[1,1,4,256]{3,2,1,0:T(4,128)S(1)}, s32[1,1,4,256]{3,2,1,0:T(4,128)}, u32[]{:S(2)}) copy-start(s32[1,1,4,256]{3,2,1,0:T(4,128)} %param.9) | copy-start | bytes 12292
  37.4 3.2 copy-start.11
  40.6 1.9 copy-start.2
  42.5 1.0 copy-start.10
  44.0 1.0 copy-start.9
  45.5 1.0 copy-start.8
  46.9 1.0 copy-start.7
  76.6 0.9 copy-start.12
  101.9 195.0 %all-gather.5.cloned.1.call-start = ((), (), s32[]{:S(2)}) async-start(), calls=%async_computation.4 | async-start | bytes 8912896 | tf_op jit(solution)/shard_map/all_gather | solution.py:98
  114.0 209.8 %reduce-scatter.2.cloned.1.call-start = ((), (), s32[]{:S(2)}) async-start(), calls=%async_computation.5 | async-start | bytes 163840 | tf_op jit(solution)/shard_map/reduce_scatter | solution.py:106
  296.9 26.9 %copy-start.1 = (bf16[1024,256]{1,0:T(8,128)(2,1)S(1)}, bf16[1024,256]{1,0:T(8,128)(2,1)}, u32[]{:S(2)}) copy-start(bf16[1024,256]{1,0:T(8,128)(2,1)} %param.10) | copy-start | bytes 1572868
Sparse Core Ops, SparseCore 0:
  102.0 84.9 all-gather.2
  189.7 107.1 all-gather.4
  304.8 18.9 reduce-scatter.1
where the time goes:
time: 337 us; the launch traced here: 331 us
  waiting for transfers between devices  202 us (60%)
  matrix products  57.4 us (17%)
  blocking collectives  30.3 us (9%)
  local copies, waits for them, and re-layouts  16.3 us (5%)
  between operations  14.1 us (4%)
  other arithmetic  10.4 us (3%)
    all_gather x1, waiting for transfers between devices, on_device(): lax.all_gather(right_one[:, 0], 'row', axis=0, tiled=True)  110 us
    all_gather x1, waiting for transfers between devices, on_device(): left_panel = lax.all_gather(left_one[:, 0], 'col', axis=0, tiled=True)  72.9 us
    all_to_all x1, blocking collectives, on_device(): lax.all_to_all(left_part, 'pblk', split_axis=1, concat_axis=0, tiled=True)  19.3 us
    reduce_scatter x1, waiting for transfers between devices, on_device(): return lax.psum_scatter(reordered, 'pblk', scatter_dimension=1, tiled=True)  19.2 us
    dot_general x8, matrix products, panels(): jnp.einsum('b,bkt->kt', block_pick, proj_input.astype(jnp.float32))  13.4 us
    dot_general x8, matrix products, panels(): jnp.einsum('esr,est->ert', left_side, right_side, precision=lax.Precision...  11.5 us
    all_to_all x1, blocking collectives, on_device(): lax.all_to_all(right_part, 'pblk', split_axis=1, concat_axis=0, tiled=True)  11 us
    unnamed x45, local copies, waits for them, and re-layouts  10 us
  transfers between devices with their start and end apart: 3, of which 3 were waited for; matrix products, arithmetic and copies ran while one was open for 0% of the time, Pallas kernels for 0%

commit v1 on v0

--- a/solution.py
+++ b/solution.py
@@ -1,7 +1,7 @@
 import jax
 import jax.numpy as jnp
 from jax import lax
-from jax.sharding import PartitionSpec as P
+from jax.sharding import Mesh, PartitionSpec as P
 
 SEQ = 64
 NFEAT = 4
@@ -78,38 +78,47 @@
 
 
 def on_device(left_feat, right_feat, embed, conv_w, head, assign, proj_delta, proj_input):
-    row_count = lax.axis_size("row")
-    blk_count = lax.axis_size("pblk")
+    group = ("zh", "core", "col")
+    n_group = lax.axis_size(group)
+    n_zh = lax.axis_size("zh")
+    n_core = lax.axis_size("core")
+    n_col = lax.axis_size("col")
+    n_y = lax.axis_size("y")
+    n_blk = lax.axis_size("pblk")
     left_each = left_feat.shape[0]
     right_each = right_feat.shape[2]
     right_local = right_feat.reshape(right_each, right_feat.shape[3])
     own_features = jnp.concatenate([left_feat, right_local], 0)
     panel = panels(own_features, embed, conv_w, head, assign, proj_delta, proj_input)
-    left_part = panel[:left_each]
-    right_part = panel[left_each:]
-    left_one, right_one = (
-        lax.all_to_all(left_part, "pblk", split_axis=1, concat_axis=0, tiled=True),
-        lax.all_to_all(right_part, "pblk", split_axis=1, concat_axis=0, tiled=True),
+    own = panel.shape[0]
+    width = panel.shape[1] * panel.shape[2] // n_group
+    sliced = panel.reshape(own, n_group, width)
+    spread = lax.all_to_all(sliced, group, split_axis=1, concat_axis=0, tiled=True)
+    spread = spread.reshape(n_group, own, width)
+    left_part = spread[:, :left_each].reshape(n_group * left_each, width)
+    right_part = spread[:, left_each:].reshape(n_group * right_each, width)
+    left_tile = lax.all_gather(left_part, "pblk", axis=0, tiled=True)
+    right_tile = lax.all_gather(right_part, "y", axis=0, tiled=True)
+    partial_tile = jnp.einsum("lk,rk->lr", left_tile, right_tile, preferred_element_type=jnp.float32)
+    partial_tile = partial_tile.reshape(
+        n_blk, n_zh, n_core, n_col, left_each, n_y, n_zh, n_core, n_col, right_each
     )
-    left_panel = lax.all_gather(left_one[:, 0], "col", axis=0, tiled=True)
-    partial_tile = jnp.einsum(
-        "lq,rq->lr",
-        left_panel,
-        lax.all_gather(right_one[:, 0], "row", axis=0, tiled=True),
-        preferred_element_type=jnp.float32,
-    )
-    tile_rows = partial_tile.shape[0]
-    reordered = partial_tile.reshape(tile_rows, row_count, blk_count, right_each)
-    reordered = jnp.transpose(reordered, (0, 2, 1, 3)).reshape(
-        tile_rows, row_count * blk_count * right_each
-    )
-    return lax.psum_scatter(reordered, "pblk", scatter_dimension=1, tiled=True)
+    chunks = jnp.transpose(partial_tile, (1, 2, 8, 3, 0, 4, 6, 5, 7, 9))
+    chunks = chunks.reshape(n_group, n_col * n_blk * left_each, n_zh * n_y * n_core * right_each)
+    block = lax.psum_scatter(chunks, group, scatter_dimension=0, tiled=True)
+    return block.reshape(block.shape[1], block.shape[2])
 
 
 def solution(mesh):
+    n_row = mesh.shape["row"]
+    fine = Mesh(
+        mesh.devices.reshape(2, 4, n_row // 8, mesh.shape["col"], mesh.shape["pblk"]),
+        ("zh", "y", "core", "col", "pblk"),
+    )
+    rows = ("zh", "y", "core")
     placed = (
-        P(("row", "col", "pblk"), None),
-        P("col", "pblk", "row", None),
+        P((*rows, "col", "pblk"), None),
+        P("col", "pblk", rows, None),
         P(),
         P(),
         P(),
@@ -118,5 +127,5 @@
         P(),
     )
     return jax.shard_map(
-        on_device, mesh=mesh, in_specs=placed, out_specs=P("row", ("col", "pblk")), check_vma=False
+        on_device, mesh=fine, in_specs=placed, out_specs=P(rows, ("col", "pblk")), check_vma=False
     )

time: 337 us -> 422 us (1.25)
  the two profiles are of different devices: /device:TPU:8 before, /device:TPU:1 now
where the time goes in v1:
time: 422 us; the launch traced here: 415 us
  waiting for transfers between devices  148 us (35%)
  local copies, waits for them, and re-layouts  124 us (29%)
  blocking collectives  57.9 us (14%)
  matrix products  53.7 us (13%)
  other arithmetic  17.5 us (4%)
  between operations  14.3 us (3%)
    mul x32, local copies, waits for them, and re-layouts, panels(): panel = panel + block_pick[None, :, None, None] * projected[:, None]  68.9 us
    reduce_scatter x1, waiting for transfers between devices, on_device(): block = lax.psum_scatter(chunks, group, scatter_dimension=0, tiled=True)  63.3 us
    all_to_all x1, blocking collectives, on_device(): lax.all_to_all(sliced, group, split_axis=1, concat_axis=0, tiled=True)  57.9 us
    all_gather x1, waiting for transfers between devices, on_device(): left_tile = lax.all_gather(left_part, 'pblk', axis=0, tiled=True)  52.6 us
    all_gather x1, waiting for transfers between devices, on_device(): right_tile = lax.all_gather(right_part, 'y', axis=0, tiled=True)  31.7 us
    unnamed x43, local copies, waits for them, and re-layouts  14.8 us
    dot_general x8, matrix products, panels(): jnp.einsum('b,bkt->kt', block_pick, proj_input.astype(jnp.float32))  13.3 us
    reshape x1, local copies, waits for them, and re-layouts, on_device(): partial_tile.reshape(n_blk, n_zh, n_core, n_col, left_each, n_y, n_zh, n_...  11.5 us
  transfers between devices with their start and end apart: 3, of which 3 were waited for; matrix products, arithmetic and copies ran while one was open for 0% of the time, Pallas kernels for 0%

profile of v1, /device:TPU:1, one launch (start us, length us, event | category | flops | bytes accessed | tf_op | source)
XLA Modules:
  0.0 414.9 jit_solution(5127504593989071444)
XLA Ops:
  6.5 1.6 fusion.261
  9.4 1.2 copy.43
  10.6 0.8 fusion.161
  11.4 1.0 fusion.165
  13.0 0.8 fusion.169
  13.8 0.7 fusion.194
  14.5 1.0 fusion.173
  15.5 0.7 fusion.195
  16.2 1.0 fusion.177
  17.8 0.9 fusion.181
  19.3 0.9 fusion.185
  20.8 0.9 fusion.189
  22.4 1.9 fusion.159
  24.2 2.0 fusion.163
  26.2 1.9 fusion.167
  28.1 2.0 fusion.171
  30.1 2.0 fusion.175
  32.1 1.2 fusion.179
  33.3 1.2 fusion.183
  34.5 1.2 fusion.187
  37.8 2.8 fusion.262
  41.3 1.4 copy-done.2
  53.6 1.4 fusion.263
  56.3 0.9 fusion.69
  57.5 1.4 fusion.264
  61.1 1.4 fusion.265
  62.6 1.6 copy.65
  65.6 1.4 fusion.266
  67.1 1.6 copy.66
  70.0 1.4 fusion.267
  71.6 1.6 copy.67
  74.7 1.4 fusion.268
  76.2 1.6 copy.68
  79.2 1.4 fusion.269
  80.7 1.6 copy.69
  83.0 1.4 fusion.270
  85.2 2.4 mul.370
  87.6 5.2 %mul.371 = f32[12,16,4096]{2,1,0:T(8,128)} reshape(f32[12,4,16384]{2,1,0:T(4,128)} %mul.370) | data formatting | bytes 6291456 | tf_op jit(solution)/shard_map/mul | solution.py:64
  92.8 3.7 mul.360
  96.5 5.2 %mul.361 = f32[12,16,4096]{2,1,0:T(8,128)} reshape(f32[12,4,16384]{2,1,0:T(4,128)} %mul.360) | data formatting | bytes 6291456 | tf_op jit(solution)/shard_map/mul | solution.py:64
  101.7 3.7 mul.350
  105.4 5.4 %mul.351 = f32[12,16,4096]{2,1,0:T(8,128)} reshape(f32[12,4,16384]{2,1,0:T(4,128)} %mul.350) | data formatting | bytes 6291456 | tf_op jit(solution)/shard_map/mul | solution.py:64
  110.8 3.6 mul.340
  114.4 5.3 %mul.341 = f32[12,16,4096]{2,1,0:T(8,128)} reshape(f32[12,4,16384]{2,1,0:T(4,128)} %mul.340) | data formatting | bytes 6291456 | tf_op jit(solution)/shard_map/mul | solution.py:64
  119.7 3.6 mul.330
  123.3 5.3 %mul.331 = f32[12,16,4096]{2,1,0:T(8,128)} reshape(f32[12,4,16384]{2,1,0:T(4,128)} %mul.330) | data formatting | bytes 6291456 | tf_op jit(solution)/shard_map/mul | solution.py:64
  128.6 3.7 mul.320
  132.2 5.2 %mul.321 = f32[12,16,4096]{2,1,0:T(8,128)} reshape(f32[12,4,16384]{2,1,0:T(4,128)} %mul.320) | data formatting | bytes 6291456 | tf_op jit(solution)/shard_map/mul | solution.py:64
  137.5 2.4 mul.310
  139.9 5.2 %mul.311 = f32[12,16,4096]{2,1,0:T(8,128)} reshape(f32[12,4,16384]{2,1,0:T(4,128)} %mul.310) | data formatting | bytes 6291456 | tf_op jit(solution)/shard_map/mul | solution.py:64
  145.2 2.4 mul.300
  147.5 5.3 %mul.301 = f32[12,16,4096]{2,1,0:T(8,128)} reshape(f32[12,4,16384]{2,1,0:T(4,128)} %mul.300) | data formatting | bytes 6291456 | tf_op jit(solution)/shard_map/mul | solution.py:64
  152.8 9.6 %add_convert_fusion = bf16[12,16,4096]{2,1,0:T(8,128)(2,1)S(1)} fusion(f32[12,16,4096]{2,1,0:T(8,128)} %mul.371, f32[12,16,4096]{2,1,0:T(8,128)} %mul.361, f32[12,16,4096]{2,1,0:T(8,128)} %mul.351, f32[12,16,4096]{2,1,0:T(8,128)} %mul.341, f32[12,16,4096]{2,1,0:T(8,128)} %mul.331, f32[12,16,4096]{2,1,0:T(8,128)} %mul.321, f32[12,16,4096]{2,1,0:T(8,128)} %mul.311, ...), kind=kLoop, calls=%fused_computation | loop fusion | flops 12582912 | bytes 26739200 | tf_op jit(solution)/shard_map/convert_element_type | solution.py:77
  162.4 0.9 copy.40
  163.3 57.9 %all_to_all.15 = bf16[12,16,4096]{2,0,1:T(8,128)(2,1)S(1)} all-to-all(bf16[12,16,4096]{2,0,1:T(8,128)(2,1)S(1)} %copy.40), channel_id=1, replica_groups=mesh['zh'=2,'y'=4,'core'=2,'col'=4,'pblk'=4] {'zh','core','col'}, dimensions={1} | all-to-all | bytes 3145728 | tf_op jit(solution)/shard_map/all_to_all | solution.py:96
  221.5 1.0 reshape.112
  222.5 1.0 slice_bitcast_fusion
  223.6 31.7 %all-gather.5.cloned.1.call-done = bf16[256,4096]{1,0:T(8,128)(2,1)} async-done(((bf16[64,4096]{1,0:T(8,128)(2,1)}), bf16[256,4096]{1,0:T(8,128)(2,1)}) %all-gather.5.cloned.1.call-update) | async-done | bytes 2097168 | tf_op jit(solution)/shard_map/all_gather | solution.py:101
  255.3 52.6 %all-gather.3.cloned.1.call-done = bf16[512,4096]{1,0:T(8,128)(2,1)} async-done(((bf16[128,4096]{1,0:T(8,128)(2,1)}), bf16[512,4096]{1,0:T(8,128)(2,1)}) %all-gather.3.cloned.1.call-update) | async-done | bytes 4194320 | tf_op jit(solution)/shard_map/all_gather | solution.py:100
  307.9 4.2 %fusion.271 = f32[512,256]{0,1:T(8,128)S(1)} fusion(bf16[512,4096]{1,0:T(8,128)(2,1)} %all-gather.3.cloned.1.call-done, bf16[256,4096]{1,0:T(8,128)(2,1)} %all-gather.5.cloned.1.call-done), kind=kOutput, calls=%fused_computation.291 | convolution fusion | flops 1073741824 | bytes 6815744 | tf_op jit(solution)/shard_map/lk,rk->lr/dot_general | solution.py:102
  312.1 11.5 %reshape.113 = f32[4,2,2,4,8,4,2,2,4,4]{4,3,2,1,0,9,8,7,6,5:T(4,128)} reshape(f32[512,256]{0,1:T(8,128)S(1)} %fusion.271) | data formatting | bytes 1048576 | tf_op jit(solution)/shard_map/reshape | solution.py:103
  323.6 9.9 %copy.42 = f32[2,2,4,4,4,8,2,4,2,4]{5,4,3,9,8,7,6,2,1,0:T(4,128)} copy(f32[2,2,4,4,4,8,2,4,2,4]{5,3,1,0,4,9,2,8,6,7:T(4,128)} %bitcast.292) | data formatting | bytes 1048576 | tf_op jit(solution)/shard_map/transpose | solution.py:106
  333.5 11.1 %reshape.114 = f32[16,128,64]{1,2,0:T(8,128)} reshape(f32[2,2,4,4,4,8,2,4,2,4]{5,4,3,9,8,7,6,2,1,0:T(4,128)} %copy.42) | data formatting | bytes 1048576 | tf_op jit(solution)/shard_map/reshape | solution.py:107
  344.6 63.3 %reduce-scatter.2.cloned.1.call-done = f32[1,128,64]{1,2,0:T(8,128)} async-done(((f32[16,128,64]{1,2,0:T(8,128)}), f32[1,128,64]{1,2,0:T(8,128)}) %reduce-scatter.2.cloned.1.call-update) | async-done | bytes 32784 | tf_op jit(solution)/shard_map/reduce_scatter | solution.py:108
  (125 shorter events, 29.1 us)
Async XLA Ops:
  6.5 31.3 %copy-start = (bf16[1024,256]{1,0:T(8,128)(2,1)S(1)}, bf16[1024,256]{1,0:T(8,128)(2,1)}, u32[]{:S(2)}) copy-start(bf16[1024,256]{1,0:T(8,128)(2,1)} %param.10) | copy-start | bytes 1572868
  6.5 15.2 %copy-start.3 = (bf16[4,768,128]{2,1,0:T(8,128)(2,1)S(1)}, bf16[4,768,128]{2,1,0:T(8,128)(2,1)}, u32[]{:S(2)}) copy-start(bf16[4,768,128]{2,1,0:T(8,128)(2,1)} %param.15) | copy-start | bytes 2359300
  6.5 248.8 %all-gather.5.cloned.1.call-start = ((), (), s32[]{:S(2)}) async-start(), calls=%async_computation.3 | async-start | bytes 2621440 | tf_op jit(solution)/shard_map/all_gather | solution.py:101
  32.1 3.6 copy-start.6
  32.1 4.8 %copy-start.4 = (s32[8,256]{1,0:T(8,128)S(1)}, s32[8,256]{1,0:T(8,128)}, u32[]{:S(2)}) copy-start(s32[8,256]{1,0:T(8,128)} %param.8) | copy-start | bytes 24580
  32.1 5.0 %copy-start.5 = (s32[1,1,4,256]{3,2,1,0:T(4,128)S(1)}, s32[1,1,4,256]{3,2,1,0:T(4,128)}, u32[]{:S(2)}) copy-start(s32[1,1,4,256]{3,2,1,0:T(4,128)} %param.9) | copy-start | bytes 12292
  37.8 3.0 copy-start.11
  40.8 1.9 copy-start.2
  42.7 1.0 copy-start.10
  44.2 1.0 copy-start.9
  45.6 1.0 copy-start.8
  47.1 1.0 copy-start.7
  222.5 85.5 %all-gather.3.cloned.1.call-start = ((), (), s32[]{:S(2)}) async-start(), calls=%async_computation.2 | async-start | bytes 5242880 | tf_op jit(solution)/shard_map/all_gather | solution.py:100
  223.6 184.3 %reduce-scatter.2.cloned.1.call-start = ((), (), s32[]{:S(2)}) async-start(), calls=%async_computation.4 | async-start | bytes 557056 | tf_op jit(solution)/shard_map/reduce_scatter | solution.py:108
  333.5 74.4 %copy-start.1 = (bf16[1024,256]{1,0:T(8,128)(2,1)S(1)}, bf16[1024,256]{1,0:T(8,128)(2,1)}, u32[]{:S(2)}) copy-start(bf16[1024,256]{1,0:T(8,128)(2,1)} %param.10) | copy-start | bytes 1572868
Sparse Core Ops, SparseCore 0:
  222.6 32.7 all-gather.4
  257.1 50.7 all-gather.2
  344.8 63.1 reduce-scatter.1

commit v2 on v1

--- a/solution.py
+++ b/solution.py
@@ -39,29 +39,18 @@
         pres.append(pre_act)
         hidden = hidden + jax.nn.silu(pre_act)
     grad_h = jnp.broadcast_to(head / SEQ, hidden.shape)
-    block_ids = jnp.arange(blocks_here, dtype=jnp.int32)
-    panel = jnp.zeros((examples, blocks_here, PR, PS), jnp.float32)
+    delta_sides = [None] * LAYERS
+    input_sides = [None] * LAYERS
     for layer in range(LAYERS - 1, -1, -1):
         pre_act = pres[layer]
         sigmoid_z = jax.nn.sigmoid(pre_act)
         delta_low = (grad_h * sigmoid_z * (1.0 + pre_act * (1.0 - sigmoid_z))).astype(jnp.bfloat16)
-        block_pick = (assign[layer] == block_ids).astype(jnp.float32)
-        rows_table = jnp.einsum("b,bcr->cr", block_pick, proj_delta.astype(jnp.float32)).astype(
-            jnp.bfloat16
+        delta_sides[layer] = jnp.einsum(
+            "esc,cr->esr", delta_low, proj_delta[assign[layer]], preferred_element_type=jnp.float32
         )
-        cols_table = jnp.einsum("b,bkt->kt", block_pick, proj_input.astype(jnp.float32)).astype(
-            jnp.bfloat16
+        input_sides[layer] = jnp.einsum(
+            "esk,kt->est", wides[layer], proj_input[assign[layer]], preferred_element_type=jnp.float32
         )
-        left_side = jnp.einsum(
-            "esc,cr->esr", delta_low, rows_table, preferred_element_type=jnp.float32
-        )
-        right_side = jnp.einsum(
-            "esk,kt->est", wides[layer], cols_table, preferred_element_type=jnp.float32
-        )
-        projected = jnp.einsum(
-            "esr,est->ert", left_side, right_side, precision=lax.Precision.HIGHEST
-        )
-        panel = panel + block_pick[None, :, None, None] * projected[:, None]
         if layer > 0:
             back_wide = jnp.einsum(
                 "esc,kc->esk", delta_low, conv_w[layer], preferred_element_type=jnp.float32
@@ -74,7 +63,23 @@
             grad_input = grad_input + jnp.concatenate([first_third[:, 1:], blank], 1)
             grad_input = grad_input + jnp.concatenate([blank, last_third[:, :-1]], 1)
             grad_h = grad_h + grad_input
-    return panel.reshape(examples, blocks_here, PR * PS).astype(jnp.bfloat16)
+    layer_ids = jnp.arange(LAYERS, dtype=jnp.int32)
+    same_before = jnp.sum(
+        (assign[None, :] == assign[:, None]) & (layer_ids[None, :] < layer_ids[:, None]), axis=1
+    )
+    slot = assign * (LAYERS // blocks_here) + same_before
+    order = jnp.sum(
+        jnp.where(slot[None, :] == layer_ids[:, None], layer_ids[None, :], 0), axis=1
+    )
+    delta_stack = jnp.stack(delta_sides)[order]
+    input_stack = jnp.stack(input_sides)[order]
+    per_block = LAYERS // blocks_here
+    delta_stack = delta_stack.reshape(blocks_here, per_block, examples, SEQ, PR)
+    input_stack = input_stack.reshape(blocks_here, per_block, examples, SEQ, PS)
+    panel = jnp.einsum(
+        "bjesr,bjest->ebrt", delta_stack, input_stack, precision=lax.Precision.HIGHEST
+    )
+    return panel.reshape(examples, blocks_here * PR * PS).astype(jnp.bfloat16)
 
 
 def on_device(left_feat, right_feat, embed, conv_w, head, assign, proj_delta, proj_input):
@@ -91,7 +96,7 @@
     own_features = jnp.concatenate([left_feat, right_local], 0)
     panel = panels(own_features, embed, conv_w, head, assign, proj_delta, proj_input)
     own = panel.shape[0]
-    width = panel.shape[1] * panel.shape[2] // n_group
+    width = panel.shape[1] // n_group
     sliced = panel.reshape(own, n_group, width)
     spread = lax.all_to_all(sliced, group, split_axis=1, concat_axis=0, tiled=True)
     spread = spread.reshape(n_group, own, width)
@@ -99,14 +104,15 @@
     right_part = spread[:, left_each:].reshape(n_group * right_each, width)
     left_tile = lax.all_gather(left_part, "pblk", axis=0, tiled=True)
     right_tile = lax.all_gather(right_part, "y", axis=0, tiled=True)
-    partial_tile = jnp.einsum("lk,rk->lr", left_tile, right_tile, preferred_element_type=jnp.float32)
-    partial_tile = partial_tile.reshape(
-        n_blk, n_zh, n_core, n_col, left_each, n_y, n_zh, n_core, n_col, right_each
-    )
-    chunks = jnp.transpose(partial_tile, (1, 2, 8, 3, 0, 4, 6, 5, 7, 9))
-    chunks = chunks.reshape(n_group, n_col * n_blk * left_each, n_zh * n_y * n_core * right_each)
+    left_tile = left_tile.reshape(n_blk, n_zh * n_core, n_col, left_each, width)
+    left_tile = jnp.transpose(left_tile, (1, 2, 0, 3, 4)).reshape(-1, width)
+    right_tile = right_tile.reshape(n_y, n_zh, n_core, n_col, right_each, width)
+    right_tile = jnp.transpose(right_tile, (3, 1, 0, 2, 4, 5)).reshape(-1, width)
+    partial_t = jnp.einsum("rk,lk->rl", right_tile, left_tile, preferred_element_type=jnp.float32)
+    chunks = partial_t.reshape(n_col, partial_t.shape[0] // n_col, n_zh * n_core, -1)
+    chunks = jnp.transpose(chunks, (2, 0, 1, 3)).reshape(n_group, chunks.shape[1], chunks.shape[3])
     block = lax.psum_scatter(chunks, group, scatter_dimension=0, tiled=True)
-    return block.reshape(block.shape[1], block.shape[2])
+    return block[0].T
 
 
 def solution(mesh):

time: 422 us -> 315 us (0.75); the launches traced: 415 us -> 314 us
  local copies, waits for them, and re-layouts: 124 us -> 35.7 us
  between operations: 14.3 us -> 29.5 us
  other arithmetic: 17.5 us -> 4.78 us
  waiting for transfers between devices: 148 us -> 140 us
  matrix products: 53.7 us -> 46.3 us
    mul x32 -> x0, local copies, waits for them, and re-layouts: 68.9 us -> none  [panels(): panel = panel + block_pick[None, :, None, None] * projected[:, None]]
    reshape x2 -> x1, local copies, waits for them, and re-layouts: 22.6 us -> 2.73 us  [on_device(): right_tile = right_tile.reshape(n_y, n_zh, n_core, n_col, right_each, width)]
    convert_element_type x9 -> x0, other arithmetic: 14.6 us -> none  [the longest x1 9.6 us: panels(): return panel.reshape(examples, blocks_here, PR * PS).astype(jnp.bfloat16)]
    unnamed x43 -> x121, local copies, waits for them, and re-layouts: 14.8 us -> 4.31 us
    gather x0 -> x2, local copies, waits for them, and re-layouts: none -> 8.56 us  [the longest x1 4.31 us: panels(): input_stack = jnp.stack(input_sides)[order]]
    all_gather x1, waiting for transfers between devices: 52.6 us -> 45 us  [on_device(): left_tile = lax.all_gather(left_part, 'pblk', axis=0, tiled=True)]
    dot_general x41 -> x18, matrix products: 42.3 us -> 35.2 us  [the longest x8 16.1 us: panels(): jnp.einsum('esk,kt->est', wides[layer], proj_input[assign[layer]], prefer...]
    transpose x1 -> x3, local copies, waits for them, and re-layouts: 9.9 us -> 5.61 us  [the longest x1 2.46 us: on_device(): left_tile = jnp.transpose(left_tile, (1, 2, 0, 3, 4)).reshape(-1, width)]
  transfers between devices with their start and end apart: 3 -> 3, of which waited for: 3 -> 3; matrix products, arithmetic and copies ran while one was open for 0% -> 3% of each run, Pallas kernels for 0% -> 0%
where the time goes in v2:
time: 315 us; the launch traced here: 314 us
  waiting for transfers between devices  140 us (44%)
  blocking collectives  57.9 us (18%)
  matrix products  46.3 us (15%)
  local copies, waits for them, and re-layouts  35.7 us (11%)
  between operations  29.5 us (9%)
  other arithmetic  4.78 us (2%)
    reduce_scatter x1, waiting for transfers between devices, on_device(): block = lax.psum_scatter(chunks, group, scatter_dimension=0, tiled=True)  63.2 us
    all_to_all x1, blocking collectives, on_device(): lax.all_to_all(sliced, group, split_axis=1, concat_axis=0, tiled=True)  57.9 us
    all_gather x1, waiting for transfers between devices, on_device(): left_tile = lax.all_gather(left_part, 'pblk', axis=0, tiled=True)  45 us
    all_gather x1, waiting for transfers between devices, on_device(): right_tile = lax.all_gather(right_part, 'y', axis=0, tiled=True)  31.7 us
    dot_general x8, matrix products, panels(): jnp.einsum('esk,kt->est', wides[layer], proj_input[assign[layer]], prefer...  16.1 us
    dot_general x1, matrix products, panels(): jnp.einsum('bjesr,bjest->ebrt', delta_stack, input_stack, precision=lax.P...  9.38 us
    dot_general x8, matrix products, panels(): jnp.einsum('esc,cr->esr', delta_low, proj_delta[assign[layer]], preferred...  8.37 us
  transfers between devices with their start and end apart: 3, of which 3 were waited for; matrix products, arithmetic and copies ran while one was open for 3% of the time, Pallas kernels for 0%

profile of v2, /device:TPU:1, one launch (start us, length us, event | category | flops | bytes accessed | tf_op | source)
XLA Modules:
  0.0 314.4 jit_solution(11110350899090717740)
XLA Ops:
  6.5 1.6 fusion.236
  18.5 0.9 convert_reduce_fusion
  19.4 0.8 copy.47
  20.2 0.8 copy.33
  21.6 2.9 fusion.237
  24.6 0.5 fusion.208
  25.7 0.7 fusion.219
  26.4 0.2 copy-done.58
  26.9 0.5 fusion.209
  28.0 0.7 fusion.218
  29.0 0.5 fusion.210
  30.1 0.7 fusion.217
  31.1 0.5 add_convert_fusion
  32.3 0.6 multiply_convert_fusion.6
  33.0 0.5 fusion.95
  33.5 0.2 fusion.226
  33.8 0.4 multiply_convert_fusion.5
  34.2 0.5 fusion.98
  34.9 0.4 multiply_convert_fusion.4
  35.3 0.5 fusion.102
  36.1 0.4 multiply_convert_fusion.3
  36.6 0.5 fusion.106
  37.3 0.4 multiply_convert_fusion.2
  37.7 0.5 fusion.110
  38.5 0.6 multiply_convert_fusion.1
  39.1 0.5 fusion.114
  39.8 1.3 multiply_convert_fusion
  41.1 0.8 copy-done.9
  41.9 0.5 fusion.118
  42.4 1.3 fusion.220
  44.3 2.5 fusion.51
  47.5 2.6 fusion.50
  50.2 1.3 fusion.59
  51.4 1.0 fusion.58
  53.2 2.6 fusion.49
  55.8 1.0 fusion.57
  57.5 1.3 fusion.48
  58.7 1.0 fusion.56
  60.5 2.4 fusion.47
  62.9 1.0 fusion.55
  64.6 1.2 fusion.46
  65.9 1.0 fusion.54
  67.5 2.3 fusion.45
  69.9 1.0 fusion.53
  71.6 1.2 fusion.44
  72.8 1.0 fusion.52
  73.8 4.3 %gather_fusion.1 = f32[8,12,64,128]{3,2,1,0:T(8,128)} fusion(f32[8,12,64,128]{3,2,1,0:T(8,128)} %fusion.44, s32[1024]{0:T(1024)S(1)} %pad_clamp_fusion), kind=kCustom, calls=%fused_computation.1 | custom fusion | bytes 6291488 | tf_op jit(solution)/shard_map/gather | solution.py:75
  78.1 4.3 %gather_fusion = f32[8,12,64,128]{3,2,1,0:T(8,128)} fusion(f32[8,12,64,128]{3,2,1,0:T(8,128)} %fusion.52, s32[1024]{0:T(1024)S(1)} %pad_clamp_fusion), kind=kCustom, calls=%fused_computation | custom fusion | bytes 6291488 | tf_op jit(solution)/shard_map/gather | solution.py:74
  82.4 9.4 %bitcast_convert_fusion = bf16[12,4,128,128]{3,2,1,0:T(8,128)(2,1)} fusion(f32[4,2,12,64,128]{4,3,2,1,0:T(8,128)} %bitcast.258, f32[4,2,12,64,128]{4,3,2,1,0:T(8,128)} %bitcast.259), kind=kOutput, calls=%fused_computation.2 | convolution fusion | flops 1208745984 | bytes 7864320 | tf_op jit(solution)/shard_map/bjesr,bjest->ebrt/dot_general | solution.py:79
  91.8 2.5 convert_element_type.92
  94.3 0.9 copy.41
  95.2 57.9 %all_to_all.15 = bf16[12,16,4096]{2,0,1:T(8,128)(2,1)S(1)} all-to-all(bf16[12,16,4096]{2,0,1:T(8,128)(2,1)S(1)} %copy.41), channel_id=1, replica_groups=mesh['zh'=2,'y'=4,'core'=2,'col'=4,'pblk'=4] {'zh','core','col'}, dimensions={1} | all-to-all | bytes 3145728 | tf_op jit(solution)/shard_map/all_to_all | solution.py:101
  153.2 0.2 slice.324
  153.4 1.0 reshape.64
  154.5 1.0 slice_bitcast_fusion
  155.6 31.7 %all-gather.3.cloned.1.call-done = bf16[256,4096]{1,0:T(8,128)(2,1)} async-done(((bf16[64,4096]{1,0:T(8,128)(2,1)}), bf16[256,4096]{1,0:T(8,128)(2,1)}) %all-gather.3.cloned.1.call-update) | async-done | bytes 2097168 | tf_op jit(solution)/shard_map/all_gather | solution.py:106
  187.3 2.7 reshape.65
  190.1 2.3 copy.42
  192.4 2.5 reshape.111
  194.9 45.0 %all-gather.5.cloned.1.call-done = bf16[512,4096]{1,0:T(8,128)(2,1)} async-done(((bf16[128,4096]{1,0:T(8,128)(2,1)}), bf16[512,4096]{1,0:T(8,128)(2,1)}) %all-gather.5.cloned.1.call-update) | async-done | bytes 4194320 | tf_op jit(solution)/shard_map/all_gather | solution.py:105
  239.9 2.5 copy.43
  242.4 1.3 fusion.41
  243.7 0.8 copy.44
  244.6 63.2 %reduce-scatter.2.cloned.1.call-done = f32[1,64,128]{2,1,0:T(8,128)} async-done(((f32[16,64,128]{2,1,0:T(8,128)}), f32[1,64,128]{2,1,0:T(8,128)}) %reduce-scatter.2.cloned.1.call-update) | async-done | bytes 32784 | tf_op jit(solution)/shard_map/reduce_scatter | solution.py:114
  (149 shorter events, 5.3 us)
Async XLA Ops:
  6.5 37.8 %copy-start = (bf16[4,768,128]{2,1,0:T(8,128)(2,1)S(1)}, bf16[4,768,128]{2,1,0:T(8,128)(2,1)}, u32[]{:S(2)}) copy-start(bf16[4,768,128]{2,1,0:T(8,128)(2,1)} %param.15) | copy-start | bytes 2359300
  6.5 180.8 %all-gather.3.cloned.1.call-start = ((), (), s32[]{:S(2)}) async-start(), calls=%async_computation.2 | async-start | bytes 2621440 | tf_op jit(solution)/shard_map/all_gather | solution.py:106
  21.6 3.1 copy-start.11
  24.5 0.8 copy-start.25
  24.6 0.8 copy-start.52
  24.6 0.9 copy-start.53
  25.5 0.8 copy-start.26
  25.5 1.0 copy-start.58
  25.7 1.0 copy-start.54
  25.7 1.1 copy-start.55
  26.8 0.8 copy-start.24
  26.9 0.8 copy-start.50
  26.9 0.9 copy-start.51
  27.8 0.8 copy-start.22
  28.0 0.7 copy-start.46
  28.0 0.9 copy-start.48
  28.9 0.8 copy-start.20
  29.0 0.8 copy-start.43
  29.0 0.9 copy-start.45
  29.9 0.8 copy-start.16
  30.0 0.8 copy-start.39
  30.0 0.9 copy-start.41
  30.9 0.8 copy-start.14
  31.1 0.8 copy-start.36
  31.1 0.9 copy-start.38
  31.1 1.0 copy-start.56
  31.1 1.2 copy-start.57
  32.0 0.9 copy-start.12
  32.1 0.8 copy-start.32
  32.1 0.9 copy-start.34
  33.0 0.7 copy-start.18
  35.3 0.8 copy-start.1
  36.5 0.7 copy-start.3
  37.7 0.8 copy-start.5
  39.1 0.7 copy-start.7
  41.1 0.8 copy-start.9
  47.5 2.7 copy-start.27
  47.5 2.7 copy-start.29
  47.5 2.7 copy-start.30
  47.5 2.7 copy-start.31
  47.5 2.7 copy-start.59
  50.2 1.3 copy-start.10
  53.1 2.7 copy-start.8
  53.2 2.7 copy-start.28
  53.2 4.3 %copy-start.23 = (bf16[12,64,256]{2,1,0:T(8,128)(2,1)S(1)}, bf16[12,64,256]{2,1,0:T(8,128)(2,1)}, u32[]{:S(2)}) copy-start(bf16[12,64,256]{2,1,0:T(8,128)(2,1)} %copy-done.22) | copy-start | bytes 1179652
  53.2 4.3 %copy-start.47 = (bf16[12,63,256]{2,1,0:T(8,128)(2,1)S(1)}, bf16[12,63,256]{2,1,0:T(8,128)(2,1)}, u32[]{:S(2)}) copy-start(bf16[12,63,256]{2,1,0:T(8,128)(2,1)} %copy-done.46) | copy-start | bytes 1161220
  53.2 4.3 %copy-start.49 = (bf16[12,63,256]{2,1,0:T(8,128)(2,1)S(1)}, bf16[12,63,256]{2,1,0:T(8,128)(2,1)}, u32[]{:S(2)}) copy-start(bf16[12,63,256]{2,1,0:T(8,128)(2,1)} %copy-done.48) | copy-start | bytes 1161220
  57.5 1.3 copy-start.6
  57.5 3.0 copy-start.21
  57.5 3.0 copy-start.44
  60.5 2.4 copy-start.4
  60.5 4.0 %copy-start.17 = (bf16[12,64,256]{2,1,0:T(8,128)(2,1)S(1)}, bf16[12,64,256]{2,1,0:T(8,128)(2,1)}, u32[]{:S(2)}) copy-start(bf16[12,64,256]{2,1,0:T(8,128)(2,1)} %copy-done.16) | copy-start | bytes 1179652
  60.5 4.0 %copy-start.40 = (bf16[12,63,256]{2,1,0:T(8,128)(2,1)S(1)}, bf16[12,63,256]{2,1,0:T(8,128)(2,1)}, u32[]{:S(2)}) copy-start(bf16[12,63,256]{2,1,0:T(8,128)(2,1)} %copy-done.39) | copy-start | bytes 1161220
  60.5 4.0 %copy-start.42 = (bf16[12,63,256]{2,1,0:T(8,128)(2,1)S(1)}, bf16[12,63,256]{2,1,0:T(8,128)(2,1)}, u32[]{:S(2)}) copy-start(bf16[12,63,256]{2,1,0:T(8,128)(2,1)} %copy-done.41) | copy-start | bytes 1161220
  64.6 1.3 copy-start.2
  64.6 2.9 copy-start.15
  64.6 2.9 copy-start.37
  67.5 4.0 %copy-start.13 = (bf16[12,64,256]{2,1,0:T(8,128)(2,1)S(1)}, bf16[12,64,256]{2,1,0:T(8,128)(2,1)}, u32[]{:S(2)}) copy-start(bf16[12,64,256]{2,1,0:T(8,128)(2,1)} %copy-done.12) | copy-start | bytes 1179652
  67.5 4.0 %copy-start.33 = (bf16[12,63,256]{2,1,0:T(8,128)(2,1)S(1)}, bf16[12,63,256]{2,1,0:T(8,128)(2,1)}, u32[]{:S(2)}) copy-start(bf16[12,63,256]{2,1,0:T(8,128)(2,1)} %copy-done.32) | copy-start | bytes 1161220
  67.5 4.0 %copy-start.35 = (bf16[12,63,256]{2,1,0:T(8,128)(2,1)S(1)}, bf16[12,63,256]{2,1,0:T(8,128)(2,1)}, u32[]{:S(2)}) copy-start(bf16[12,63,256]{2,1,0:T(8,128)(2,1)} %copy-done.34) | copy-start | bytes 1161220
  71.6 1.3 copy-start.19
  154.4 85.5 %all-gather.5.cloned.1.call-start = ((), (), s32[]{:S(2)}) async-start(), calls=%async_computation.3 | async-start | bytes 5242880 | tf_op jit(solution)/shard_map/all_gather | solution.py:105
  155.5 152.3 %reduce-scatter.2.cloned.1.call-start = ((), (), s32[]{:S(2)}) async-start(), calls=%async_computation.4 | async-start | bytes 557056 | tf_op jit(solution)/shard_map/reduce_scatter | solution.py:114
Sparse Core Ops, SparseCore 0:
  154.5 32.7 all-gather.2
  189.1 50.7 all-gather.4
  244.7 63.0 reduce-scatter.1

commit v3 on v2

--- a/solution.py
+++ b/solution.py
@@ -77,7 +77,7 @@
     delta_stack = delta_stack.reshape(blocks_here, per_block, examples, SEQ, PR)
     input_stack = input_stack.reshape(blocks_here, per_block, examples, SEQ, PS)
     panel = jnp.einsum(
-        "bjesr,bjest->ebrt", delta_stack, input_stack, precision=lax.Precision.HIGHEST
+        "bjesr,bjest->ebrt", delta_stack, input_stack, precision=lax.Precision.HIGH
     )
     return panel.reshape(examples, blocks_here * PR * PS).astype(jnp.bfloat16)
 
@@ -98,10 +98,10 @@
     own = panel.shape[0]
     width = panel.shape[1] // n_group
     sliced = panel.reshape(own, n_group, width)
-    spread = lax.all_to_all(sliced, group, split_axis=1, concat_axis=0, tiled=True)
-    spread = spread.reshape(n_group, own, width)
-    left_part = spread[:, :left_each].reshape(n_group * left_each, width)
-    right_part = spread[:, left_each:].reshape(n_group * right_each, width)
+    right_part = lax.all_to_all(sliced[left_each:], group, split_axis=1, concat_axis=0, tiled=True)
+    right_part = right_part.reshape(n_group * right_each, width)
+    left_part = lax.all_to_all(sliced[:left_each], group, split_axis=1, concat_axis=0, tiled=True)
+    left_part = left_part.reshape(n_group * left_each, width)
     left_tile = lax.all_gather(left_part, "pblk", axis=0, tiled=True)
     right_tile = lax.all_gather(right_part, "y", axis=0, tiled=True)
     left_tile = left_tile.reshape(n_blk, n_zh * n_core, n_col, left_each, width)
@@ -111,8 +111,8 @@
     partial_t = jnp.einsum("rk,lk->rl", right_tile, left_tile, preferred_element_type=jnp.float32)
     chunks = partial_t.reshape(n_col, partial_t.shape[0] // n_col, n_zh * n_core, -1)
     chunks = jnp.transpose(chunks, (2, 0, 1, 3)).reshape(n_group, chunks.shape[1], chunks.shape[3])
-    block = lax.psum_scatter(chunks, group, scatter_dimension=0, tiled=True)
-    return block[0].T
+    received = lax.all_to_all(chunks, group, split_axis=0, concat_axis=0, tiled=True)
+    return jnp.sum(received, axis=0).T
 
 
 def solution(mesh):

time: 315 us -> 234 us (0.74)
  waiting for transfers between devices: 140 us -> 45.1 us
  blocking collectives: 57.9 us -> 77.7 us
  matrix products: 46.3 us -> 42.4 us
  local copies, waits for them, and re-layouts: 35.7 us -> 32.1 us
    reduce_scatter x1 -> x0, waiting for transfers between devices: 63.2 us -> none  [on_device(): block = lax.psum_scatter(chunks, group, scatter_dimension=0, tiled=True)]
    all_gather x1, waiting for transfers between devices: 31.7 us -> 0.06 us  [on_device(): right_tile = lax.all_gather(right_part, 'y', axis=0, tiled=True)]
    all_to_all x1 -> x3, blocking collectives: 57.9 us -> 77.7 us  [the longest x1 31.3 us: on_device(): lax.all_to_all(sliced[:left_each], group, split_axis=1, concat_axis=0, ti...]
    dot_general x1, matrix products: 9.38 us -> 5.48 us  [panels(): jnp.einsum('bjesr,bjest->ebrt', delta_stack, input_stack, precision=lax.P...]
    convert_element_type x2 -> x0, local copies, waits for them, and re-layouts: 3.44 us -> none  [panels(): return panel.reshape(examples, blocks_here * PR * PS).astype(jnp.bfloat16)]
  transfers between devices with their start and end apart: 3 -> 2, of which waited for: 3 -> 2; matrix products, arithmetic and copies ran while one was open for 3% -> 4% of each run, Pallas kernels for 0% -> 0%
where the time goes in v3:
time: 234 us; the launch traced here: 233 us
  blocking collectives  77.7 us (33%)
  waiting for transfers between devices  45.1 us (19%)
  matrix products  42.4 us (18%)
  local copies, waits for them, and re-layouts  32.1 us (14%)
  between operations  29.7 us (13%)
  other arithmetic  5.42 us (2%)
    all_gather x1, waiting for transfers between devices, on_device(): left_tile = lax.all_gather(left_part, 'pblk', axis=0, tiled=True)  45 us
    all_to_all x1, blocking collectives, on_device(): lax.all_to_all(sliced[:left_each], group, split_axis=1, concat_axis=0, ti...  31.3 us
    all_to_all x1, blocking collectives, on_device(): lax.all_to_all(sliced[left_each:], group, split_axis=1, concat_axis=0, ti...  24.2 us
    all_to_all x1, blocking collectives, on_device(): lax.all_to_all(chunks, group, split_axis=0, concat_axis=0, tiled=True)  22.1 us
    dot_general x8, matrix products, panels(): jnp.einsum('esk,kt->est', wides[layer], proj_input[assign[layer]], prefer...  16.1 us
    dot_general x8, matrix products, panels(): jnp.einsum('esc,cr->esr', delta_low, proj_delta[assign[layer]], preferred...  8.4 us
    dot_general x1, matrix products, panels(): jnp.einsum('bjesr,bjest->ebrt', delta_stack, input_stack, precision=lax.P...  5.48 us
  transfers between devices with their start and end apart: 2, of which 2 were waited for; matrix products, arithmetic and copies ran while one was open for 4% of the time, Pallas kernels for 0%

profile of v3, /device:TPU:1, one launch (start us, length us, event | category | flops | bytes accessed | tf_op | source)
XLA Modules:
  0.0 232.7 jit_solution(8108243440997385240)
XLA Ops:
  6.5 1.6 fusion.236
  18.4 0.9 convert_reduce_fusion
  19.3 0.8 copy.50
  20.1 0.8 copy.35
  21.5 2.9 %fusion.237 = (bf16[12,64,256]{2,1,0:T(8,128)(2,1)S(1)}, f32[12,64,256]{2,1,0:T(8,128)S(1)}) fusion(bf16[1024,256]{1,0:T(8,128)(2,1)} %param.10, s32[12,64]{1,0:T(8,128)S(1)} %bitcast.271, s32[12,64]{1,0:T(8,128)S(1)} %bitcast.272, s32[12,64]{1,0:T(8,128)S(1)} %bitcast.273, s32[12,64]{1,0:T(8,128)S(1)} %bitcast.274), kind=kOutput, calls=%fused_computation.267 | convolution fusion | flops 415432704 | bytes 1716224 | tf_op jit(solution)/shard_map/esv,vc->esc/dot_general | solution.py:30
  24.6 0.5 fusion.208
  25.6 0.7 fusion.219
  26.9 0.5 fusion.209
  27.9 0.7 fusion.218
  28.9 0.5 fusion.210
  29.9 0.7 fusion.217
  31.0 0.5 add_convert_fusion
  32.2 0.6 multiply_convert_fusion.6
  32.9 0.5 fusion.95
  33.7 0.4 multiply_convert_fusion.5
  34.1 0.5 fusion.98
  34.8 0.4 multiply_convert_fusion.4
  35.2 0.5 fusion.102
  36.0 0.4 multiply_convert_fusion.3
  36.4 0.5 fusion.106
  37.0 0.2 fusion.223
  37.2 0.4 multiply_convert_fusion.2
  37.6 0.5 fusion.110
  38.4 0.6 multiply_convert_fusion.1
  39.0 0.5 fusion.114
  39.7 1.3 multiply_convert_fusion
  41.0 0.8 copy-done.9
  41.8 0.5 fusion.118
  42.3 1.4 fusion.220
  44.3 2.5 %fusion.51 = f32[8,12,64,128]{3,2,1,0:T(8,128)} fusion(bf16[4,768,128]{2,1,0:T(8,128)(2,1)S(1)} %copy-done, s32[]{:T(128)S(6)} %select_n.47, bf16[12,63,256]{2,1,0:T(8,128)(2,1)} %copy-done.53, bf16[12,63,256]{2,1,0:T(8,128)(2,1)} %copy-done.52, bf16[12,64,256]{2,1,0:T(8,128)(2,1)} %copy-done.25), kind=kOutput, calls=%fused_computation.58 | convolution fusion | flops 156893184 | bytes 1757188 | tf_op jit(solution)/shard_map/esk,kt->est/dot_general | solution.py:51
  47.5 2.6 %fusion.50 = f32[8,12,64,128]{3,2,1,0:T(8,128)} fusion(f32[8,12,64,128]{3,2,1,0:T(8,128)} %fusion.51, bf16[4,768,128]{2,1,0:T(8,128)(2,1)S(1)} %copy-done, s32[]{:T(128)S(6)} %select_n.48, bf16[12,63,256]{2,1,0:T(8,128)(2,1)} %copy-done.55, bf16[12,63,256]{2,1,0:T(8,128)(2,1)} %copy-done.54, bf16[12,64,256]{2,1,0:T(8,128)(2,1)} %copy-done.26), kind=kOutput, calls=%fused_computation.56 | convolution fusion | flops 156893184 | bytes 1769476 | tf_op jit(solution)/shard_map/esk,kt->est/dot_general | solution.py:51
  50.2 1.3 fusion.59
  51.4 1.0 fusion.58
  53.1 2.6 %fusion.49 = f32[8,12,64,128]{3,2,1,0:T(8,128)} fusion(f32[8,12,64,128]{3,2,1,0:T(8,128)} %fusion.50, bf16[4,768,128]{2,1,0:T(8,128)(2,1)S(1)} %copy-done, s32[]{:T(128)S(6)} %select_n.49, bf16[12,63,256]{2,1,0:T(8,128)(2,1)} %copy-done.51, bf16[12,63,256]{2,1,0:T(8,128)(2,1)} %copy-done.50, bf16[12,64,256]{2,1,0:T(8,128)(2,1)} %copy-done.24), kind=kOutput, calls=%fused_computation.54 | convolution fusion | flops 156893184 | bytes 1769476 | tf_op jit(solution)/shard_map/esk,kt->est/dot_general | solution.py:51
  55.7 1.0 fusion.57
  57.4 1.2 fusion.48
  58.7 1.0 fusion.56
  60.4 2.3 %fusion.47 = f32[8,12,64,128]{3,2,1,0:T(8,128)} fusion(f32[8,12,64,128]{3,2,1,0:T(8,128)} %fusion.48, bf16[4,768,128]{2,1,0:T(8,128)(2,1)S(1)} %copy-done, s32[]{:T(128)S(6)} %select_n.51, bf16[12,63,256]{2,1,0:T(8,128)(2,1)} %copy-done.45, bf16[12,63,256]{2,1,0:T(8,128)(2,1)S(1)} %copy-done.44, bf16[12,64,256]{2,1,0:T(8,128)(2,1)S(1)} %copy-done.21), kind=kOutput, calls=%fused_computation.50 | convolution fusion | flops 156893184 | bytes 1769476 | tf_op jit(solution)/shard_map/esk,kt->est/dot_general | solution.py:51
  62.8 1.0 fusion.55
  64.5 1.3 fusion.46
  65.7 1.0 fusion.54
  67.5 2.3 fusion.45
  69.8 1.0 fusion.53
  71.5 1.2 fusion.44
  72.7 1.0 fusion.52
  73.7 4.3 %gather_fusion.1 = f32[8,12,64,128]{3,2,1,0:T(8,128)} fusion(f32[8,12,64,128]{3,2,1,0:T(8,128)} %fusion.44, s32[1024]{0:T(1024)S(1)} %pad_clamp_fusion), kind=kCustom, calls=%fused_computation.1 | custom fusion | bytes 6291488 | tf_op jit(solution)/shard_map/gather | solution.py:75
  78.0 4.3 %gather_fusion = f32[8,12,64,128]{3,2,1,0:T(8,128)} fusion(f32[8,12,64,128]{3,2,1,0:T(8,128)} %fusion.52, s32[1024]{0:T(1024)S(1)} %pad_clamp_fusion), kind=kCustom, calls=%fused_computation | custom fusion | bytes 6291488 | tf_op jit(solution)/shard_map/gather | solution.py:74
  82.3 5.5 %bitcast_convert_fusion = bf16[12,4,128,128]{3,2,1,0:T(8,128)(2,1)S(1)} fusion(f32[4,2,12,64,128]{4,3,2,1,0:T(8,128)} %bitcast.261, f32[4,2,12,64,128]{4,3,2,1,0:T(8,128)} %bitcast.262), kind=kOutput, calls=%fused_computation.2 | convolution fusion | flops 604766208 | bytes 7864320 | tf_op jit(solution)/shard_map/bjesr,bjest->ebrt/dot_general | solution.py:79
  87.9 0.2 slice.286
  88.1 0.4 copy.43
  88.5 24.2 %all_to_all.35 = bf16[4,16,4096]{2,0,1:T(4,128)(2,1)S(1)} all-to-all(bf16[4,16,4096]{2,0,1:T(4,128)(2,1)S(1)} %copy.43), channel_id=1, replica_groups=mesh['zh'=2,'y'=4,'core'=2,'col'=4,'pblk'=4] {'zh','core','col'}, dimensions={1} | all-to-all | bytes 1048576 | tf_op jit(solution)/shard_map/all_to_all | solution.py:101
  112.7 1.0 reshape.66
  113.7 0.3 all-gather.5.cloned.1.call-start
  114.1 0.5 slice.288
  114.6 0.6 copy.45
  115.2 31.3 %all_to_all.36 = bf16[8,16,4096]{2,0,1:T(8,128)(2,1)} all-to-all(bf16[8,16,4096]{2,0,1:T(8,128)(2,1)S(1)} %copy.45), channel_id=1, replica_groups=mesh['zh'=2,'y'=4,'core'=2,'col'=4,'pblk'=4] {'zh','core','col'}, dimensions={1} | all-to-all | bytes 2097152 | tf_op jit(solution)/shard_map/all_to_all | solution.py:103
  146.6 2.7 %reshape.67 = bf16[4,2,2,4,4,4096]{5,4,3,2,1,0:T(4,128)(2,1)S(1)} reshape(bf16[256,4096]{1,0:T(8,128)(2,1)} %all-gather.3.cloned.1.call-done) | data formatting | bytes 4194304 | tf_op jit(solution)/shard_map/reshape | solution.py:109
  149.4 2.3 copy.44
  151.6 2.5 %reshape.113 = bf16[4,64,4096,1]{2,1,0,3:T(8,128)(2,1)S(1)} reshape(bf16[4,2,4,2,4,4096]{5,4,3,2,1,0:T(4,128)(2,1)} %copy.44) | data formatting | bytes 4194304 | tf_op jit(solution)/shard_map/rk,lk->rl/dot_general | solution.py:111
  154.2 45.0 %all-gather.5.cloned.1.call-done = bf16[512,4096]{1,0:T(8,128)(2,1)} async-done(((bf16[128,4096]{1,0:T(8,128)(2,1)}), bf16[512,4096]{1,0:T(8,128)(2,1)}) %all-gather.5.cloned.1.call-update) | async-done | bytes 4194320 | tf_op jit(solution)/shard_map/all_gather | solution.py:105
  199.2 2.5 %copy.46 = bf16[4,4,4,8,4096]{4,3,2,1,0:T(8,128)(2,1)S(1)} copy(bf16[4,4,4,8,4096]{4,3,1,0,2:T(8,128)(2,1)} %bitcast.264) | data formatting | bytes 8388608 | tf_op jit(solution)/shard_map/transpose | solution.py:108
  201.7 1.3 fusion.41
  203.0 22.1 %all_to_all.37 = f32[16,64,128]{2,1,0:T(8,128)S(1)} all-to-all(f32[16,64,128]{2,1,0:T(8,128)S(1)} %bitcast.268), channel_id=1, replica_groups=mesh['zh'=2,'y'=4,'core'=2,'col'=4,'pblk'=4] {'zh','core','col'}, dimensions={0} | all-to-all | bytes 1048576 | tf_op jit(solution)/shard_map/all_to_all | solution.py:114
  225.2 0.6 reduce_sum.32
  (151 shorter events, 5.6 us)
Async XLA Ops:
  6.5 37.7 %copy-start = (bf16[4,768,128]{2,1,0:T(8,128)(2,1)S(1)}, bf16[4,768,128]{2,1,0:T(8,128)(2,1)}, u32[]{:S(2)}) copy-start(bf16[4,768,128]{2,1,0:T(8,128)(2,1)} %param.15) | copy-start | bytes 2359300
  6.5 140.1 %all-gather.3.cloned.1.call-start = ((), (), s32[]{:S(2)}) async-start(), calls=%async_computation.3 | async-start | bytes 2621440 | tf_op jit(solution)/shard_map/all_gather | solution.py:106
  21.5 3.1 %copy-start.11 = (bf16[8,768,256]{2,1,0:T(8,128)(2,1)S(1)}, bf16[8,768,256]{2,1,0:T(8,128)(2,1)}, u32[]{:S(2)}) copy-start(bf16[8,768,256]{2,1,0:T(8,128)(2,1)} %param.11) | copy-start | bytes 9437188
  24.4 0.8 copy-start.25
  24.5 0.7 copy-start.52
  24.5 0.9 copy-start.53
  25.4 0.8 copy-start.26
  25.4 1.0 copy-start.58
  25.6 1.0 copy-start.54
  25.6 1.1 copy-start.55
  26.7 0.8 copy-start.24
  26.8 0.8 copy-start.50
  26.8 0.9 copy-start.51
  27.7 0.8 copy-start.22
  27.9 0.7 copy-start.46
  27.9 0.9 copy-start.48
  28.8 0.8 copy-start.20
  28.9 0.8 copy-start.43
  28.9 0.9 copy-start.45
  29.8 0.8 copy-start.16
  29.9 0.8 copy-start.39
  29.9 0.9 copy-start.41
  30.8 0.8 copy-start.14
  31.0 0.8 copy-start.36
  31.0 0.9 copy-start.38
  31.0 1.0 copy-start.56
  31.0 1.2 copy-start.57
  31.9 0.9 copy-start.12
  32.0 0.8 copy-start.32
  32.0 0.9 copy-start.34
  32.9 0.7 copy-start.18
  35.2 0.8 copy-start.1
  36.4 0.7 copy-start.3
  37.6 0.8 copy-start.5
  39.0 0.7 copy-start.7
  41.0 0.8 copy-start.9
  47.4 2.7 %copy-start.27 = (bf16[4,256,128]{2,1,0:T(8,128)(2,1)S(1)}, bf16[4,256,128]{2,1,0:T(8,128)(2,1)}, u32[]{:S(2)}) copy-start(bf16[4,256,128]{2,1,0:T(8,128)(2,1)} %param.14) | copy-start | bytes 786436
  47.5 2.7 %copy-start.29 = (f32[12,64,256]{2,1,0:T(8,128)S(1)}, f32[12,64,256]{2,1,0:T(8,128)}, u32[]{:S(2)}) copy-start(f32[12,64,256]{2,1,0:T(8,128)} %get-tuple-element.6) | copy-start | bytes 2359300
  47.5 2.7 %copy-start.30 = (f32[12,63,256]{2,1,0:T(8,128)S(1)}, f32[12,63,256]{2,1,0:T(8,128)}, u32[]{:S(2)}) copy-start(f32[12,63,256]{2,1,0:T(8,128)} %get-tuple-element.23) | copy-start | bytes 2322436
  47.5 2.7 %copy-start.31 = (f32[12,63,256]{2,1,0:T(8,128)S(1)}, f32[12,63,256]{2,1,0:T(8,128)}, u32[]{:S(2)}) copy-start(f32[12,63,256]{2,1,0:T(8,128)} %get-tuple-element.24) | copy-start | bytes 2322436
  47.5 2.7 %copy-start.59 = (f32[12,64,256]{2,1,0:T(8,128)S(1)}, f32[12,64,256]{2,1,0:T(8,128)}, u32[]{:S(2)}) copy-start(f32[12,64,256]{2,1,0:T(8,128)} %copy-done.58) | copy-start | bytes 2359300
  50.1 1.3 copy-start.10
  53.1 2.7 %copy-start.8 = (bf16[12,64,256]{2,1,0:T(8,128)(2,1)S(1)}, bf16[12,64,256]{2,1,0:T(8,128)(2,1)}, u32[]{:S(2)}) copy-start(bf16[12,64,256]{2,1,0:T(8,128)(2,1)} %copy-done.7) | copy-start | bytes 1179652
  53.1 2.6 %copy-start.28 = (bf16[4,256,128]{2,1,0:T(8,128)(2,1)S(1)}, bf16[4,256,128]{2,1,0:T(8,128)(2,1)}, u32[]{:S(2)}) copy-start(bf16[4,256,128]{2,1,0:T(8,128)(2,1)} %param.14) | copy-start | bytes 786436
  53.1 4.3 %copy-start.23 = (bf16[12,64,256]{2,1,0:T(8,128)(2,1)S(1)}, bf16[12,64,256]{2,1,0:T(8,128)(2,1)}, u32[]{:S(2)}) copy-start(bf16[12,64,256]{2,1,0:T(8,128)(2,1)} %copy-done.22) | copy-start | bytes 1179652
  53.1 4.3 %copy-start.47 = (bf16[12,63,256]{2,1,0:T(8,128)(2,1)S(1)}, bf16[12,63,256]{2,1,0:T(8,128)(2,1)}, u32[]{:S(2)}) copy-start(bf16[12,63,256]{2,1,0:T(8,128)(2,1)} %copy-done.46) | copy-start | bytes 1161220
  53.1 4.3 %copy-start.49 = (bf16[12,63,256]{2,1,0:T(8,128)(2,1)S(1)}, bf16[12,63,256]{2,1,0:T(8,128)(2,1)}, u32[]{:S(2)}) copy-start(bf16[12,63,256]{2,1,0:T(8,128)(2,1)} %copy-done.48) | copy-start | bytes 1161220
  57.4 1.3 copy-start.6
  57.4 3.0 %copy-start.21 = (bf16[12,64,256]{2,1,0:T(8,128)(2,1)S(1)}, bf16[12,64,256]{2,1,0:T(8,128)(2,1)}, u32[]{:S(2)}) copy-start(bf16[12,64,256]{2,1,0:T(8,128)(2,1)} %copy-done.20) | copy-start | bytes 1179652
  57.4 3.0 %copy-start.44 = (bf16[12,63,256]{2,1,0:T(8,128)(2,1)S(1)}, bf16[12,63,256]{2,1,0:T(8,128)(2,1)}, u32[]{:S(2)}) copy-start(bf16[12,63,256]{2,1,0:T(8,128)(2,1)} %copy-done.43) | copy-start | bytes 1161220
  60.4 2.4 %copy-start.4 = (bf16[12,64,256]{2,1,0:T(8,128)(2,1)S(1)}, bf16[12,64,256]{2,1,0:T(8,128)(2,1)}, u32[]{:S(2)}) copy-start(bf16[12,64,256]{2,1,0:T(8,128)(2,1)} %copy-done.3) | copy-start | bytes 1179652
  60.4 4.0 %copy-start.17 = (bf16[12,64,256]{2,1,0:T(8,128)(2,1)S(1)}, bf16[12,64,256]{2,1,0:T(8,128)(2,1)}, u32[]{:S(2)}) copy-start(bf16[12,64,256]{2,1,0:T(8,128)(2,1)} %copy-done.16) | copy-start | bytes 1179652
  60.4 4.0 %copy-start.40 = (bf16[12,63,256]{2,1,0:T(8,128)(2,1)S(1)}, bf16[12,63,256]{2,1,0:T(8,128)(2,1)}, u32[]{:S(2)}) copy-start(bf16[12,63,256]{2,1,0:T(8,128)(2,1)} %copy-done.39) | copy-start | bytes 1161220
  60.4 4.0 %copy-start.42 = (bf16[12,63,256]{2,1,0:T(8,128)(2,1)S(1)}, bf16[12,63,256]{2,1,0:T(8,128)(2,1)}, u32[]{:S(2)}) copy-start(bf16[12,63,256]{2,1,0:T(8,128)(2,1)} %copy-done.41) | copy-start | bytes 1161220
  64.5 1.3 copy-start.2
  64.5 2.9 %copy-start.15 = (bf16[12,64,256]{2,1,0:T(8,128)(2,1)S(1)}, bf16[12,64,256]{2,1,0:T(8,128)(2,1)}, u32[]{:S(2)}) copy-start(bf16[12,64,256]{2,1,0:T(8,128)(2,1)} %copy-done.14) | copy-start | bytes 1179652
  64.5 2.9 %copy-start.37 = (bf16[12,63,256]{2,1,0:T(8,128)(2,1)S(1)}, bf16[12,63,256]{2,1,0:T(8,128)(2,1)}, u32[]{:S(2)}) copy-start(bf16[12,63,256]{2,1,0:T(8,128)(2,1)} %copy-done.36) | copy-start | bytes 1161220
  67.4 4.0 %copy-start.13 = (bf16[12,64,256]{2,1,0:T(8,128)(2,1)S(1)}, bf16[12,64,256]{2,1,0:T(8,128)(2,1)}, u32[]{:S(2)}) copy-start(bf16[12,64,256]{2,1,0:T(8,128)(2,1)} %copy-done.12) | copy-start | bytes 1179652
  67.4 4.0 %copy-start.33 = (bf16[12,63,256]{2,1,0:T(8,128)(2,1)S(1)}, bf16[12,63,256]{2,1,0:T(8,128)(2,1)}, u32[]{:S(2)}) copy-start(bf16[12,63,256]{2,1,0:T(8,128)(2,1)} %copy-done.32) | copy-start | bytes 1161220
  67.4 4.0 %copy-start.35 = (bf16[12,63,256]{2,1,0:T(8,128)(2,1)S(1)}, bf16[12,63,256]{2,1,0:T(8,128)(2,1)}, u32[]{:S(2)}) copy-start(bf16[12,63,256]{2,1,0:T(8,128)(2,1)} %copy-done.34) | copy-start | bytes 1161220
  71.5 1.3 copy-start.19
  113.7 85.5 %all-gather.5.cloned.1.call-start = ((), (), s32[]{:S(2)}) async-start(), calls=%async_computation.4 | async-start | bytes 5242880 | tf_op jit(solution)/shard_map/all_gather | solution.py:105
Sparse Core Ops, SparseCore 0:
  113.8 32.7 all-gather.2
  148.4 50.7 all-gather.4

commit v4 on v2

--- a/solution.py
+++ b/solution.py
@@ -71,13 +71,24 @@
     order = jnp.sum(
         jnp.where(slot[None, :] == layer_ids[:, None], layer_ids[None, :], 0), axis=1
     )
-    delta_stack = jnp.stack(delta_sides)[order]
-    input_stack = jnp.stack(input_sides)[order]
+    delta_slots = []
+    input_slots = []
+    for slot_id in range(LAYERS):
+        picked_delta = delta_sides[0]
+        picked_input = input_sides[0]
+        for layer in range(1, LAYERS):
+            hit = order[slot_id] == layer
+            picked_delta = jnp.where(hit, delta_sides[layer], picked_delta)
+            picked_input = jnp.where(hit, input_sides[layer], picked_input)
+        delta_slots.append(picked_delta)
+        input_slots.append(picked_input)
+    delta_stack = jnp.stack(delta_slots)
+    input_stack = jnp.stack(input_slots)
     per_block = LAYERS // blocks_here
     delta_stack = delta_stack.reshape(blocks_here, per_block, examples, SEQ, PR)
     input_stack = input_stack.reshape(blocks_here, per_block, examples, SEQ, PS)
     panel = jnp.einsum(
-        "bjesr,bjest->ebrt", delta_stack, input_stack, precision=lax.Precision.HIGHEST
+        "bjesr,bjest->ebrt", delta_stack, input_stack, precision=lax.Precision.HIGH
     )
     return panel.reshape(examples, blocks_here * PR * PS).astype(jnp.bfloat16)
 
@@ -102,8 +113,16 @@
     spread = spread.reshape(n_group, own, width)
     left_part = spread[:, :left_each].reshape(n_group * left_each, width)
     right_part = spread[:, left_each:].reshape(n_group * right_each, width)
-    left_tile = lax.all_gather(left_part, "pblk", axis=0, tiled=True)
     right_tile = lax.all_gather(right_part, "y", axis=0, tiled=True)
+    up = [(j, (j + 1) % n_blk) for j in range(n_blk)]
+    down = [(j, (j - 1) % n_blk) for j in range(n_blk)]
+    from_below = lax.ppermute(left_part, "pblk", up)
+    from_above = lax.ppermute(left_part, "pblk", down)
+    half = left_part.shape[0] // 2
+    far_low = lax.ppermute(from_below[:half], "pblk", up)
+    far_high = lax.ppermute(from_above[half:], "pblk", down)
+    far = jnp.concatenate([far_low, far_high], 0)
+    left_tile = jnp.stack([far, from_below, left_part, from_above])
     left_tile = left_tile.reshape(n_blk, n_zh * n_core, n_col, left_each, width)
     left_tile = jnp.transpose(left_tile, (1, 2, 0, 3, 4)).reshape(-1, width)
     right_tile = right_tile.reshape(n_y, n_zh, n_core, n_col, right_each, width)
@@ -111,8 +130,11 @@
     partial_t = jnp.einsum("rk,lk->rl", right_tile, left_tile, preferred_element_type=jnp.float32)
     chunks = partial_t.reshape(n_col, partial_t.shape[0] // n_col, n_zh * n_core, -1)
     chunks = jnp.transpose(chunks, (2, 0, 1, 3)).reshape(n_group, chunks.shape[1], chunks.shape[3])
-    block = lax.psum_scatter(chunks, group, scatter_dimension=0, tiled=True)
-    return block[0].T
+    received = lax.all_to_all(chunks, group, split_axis=0, concat_axis=0, tiled=True)
+    block = jnp.sum(received, axis=0).T
+    block = block.reshape(n_col, n_blk, left_each, block.shape[1])
+    block = jnp.roll(block, lax.axis_index("pblk") - 2, axis=1)
+    return block.reshape(-1, block.shape[3])
 
 
 def solution(mesh):

time: 315 us -> 294 us (0.933)
  waiting for transfers between devices: 140 us -> 49.9 us
  between operations: 29.5 us -> 64.5 us
  starting transfers between devices: 0.09 us -> 14.3 us
  matrix products: 46.3 us -> 58.3 us
  other arithmetic: 4.78 us -> 15.4 us
  local copies, waits for them, and re-layouts: 35.7 us -> 30.8 us
    reduce_scatter x1 -> x0, waiting for transfers between devices: 63.2 us -> none  [on_device(): block = lax.psum_scatter(chunks, group, scatter_dimension=0, tiled=True)]
    all_gather x1 -> x0, waiting for transfers between devices: 45 us -> none  [on_device(): left_tile = lax.all_gather(left_part, 'pblk', axis=0, tiled=True)]
    ppermute x0 -> x4, waiting for transfers between devices: none -> 35.4 us  [the longest x1 22.1 us: on_device(): from_above = lax.ppermute(left_part, 'pblk', down)]
    all_gather x1, waiting for transfers between devices: 31.7 us -> 0.01 us  [on_device(): right_tile = lax.all_gather(right_part, 'y', axis=0, tiled=True)]
    all_to_all x0 -> x1, waiting for transfers between devices: none -> 14.5 us  [on_device(): lax.all_to_all(chunks, group, split_axis=0, concat_axis=0, tiled=True)]
    dot_general x7, matrix products: 3.54 us -> 14.5 us  [panels(): jnp.einsum('esc,kc->esk', delta_low, conv_w[layer], preferred_element_typ...]
    gather x2 -> x0, local copies, waits for them, and re-layouts: 8.56 us -> none  [the longest x1 4.31 us: panels(): input_stack = jnp.stack(input_sides)[order]]
    all_to_all x0 -> x1, starting transfers between devices: none -> 8.04 us  [on_device(): lax.all_to_all(chunks, group, split_axis=0, concat_axis=0, tiled=True)]
  transfers between devices with their start and end apart: 3 -> 6, of which waited for: 3 -> 4; matrix products, arithmetic and copies ran while one was open for 3% -> 1% of each run, Pallas kernels for 0% -> 0%
where the time goes in v4:
time: 294 us; the launch traced here: 291 us
  between operations  64.5 us (22%)
  matrix products  58.3 us (20%)
  blocking collectives  58 us (20%)
  waiting for transfers between devices  49.9 us (17%)
  local copies, waits for them, and re-layouts  30.8 us (10%)
  other arithmetic  15.4 us (5%)
  starting transfers between devices  14.3 us (5%)
    all_to_all x1, blocking collectives, on_device(): lax.all_to_all(sliced, group, split_axis=1, concat_axis=0, tiled=True)  58 us
    ppermute x1, waiting for transfers between devices, on_device(): from_above = lax.ppermute(left_part, 'pblk', down)  22.1 us
    dot_general x8, matrix products, panels(): jnp.einsum('esk,kt->est', wides[layer], proj_input[assign[layer]], prefer...  16 us
    dot_general x7, matrix products, panels(): jnp.einsum('esc,kc->esk', delta_low, conv_w[layer], preferred_element_typ...  14.5 us
    all_to_all x1, waiting for transfers between devices, on_device(): lax.all_to_all(chunks, group, split_axis=0, concat_axis=0, tiled=True)  14.5 us
    ppermute x1, waiting for transfers between devices, on_device(): far_high = lax.ppermute(from_above[half:], 'pblk', down)  10 us
    unnamed x109, local copies, waits for them, and re-layouts  9.75 us
    dot_general x8, matrix products, panels(): jnp.einsum('esc,cr->esr', delta_low, proj_delta[assign[layer]], preferred...  8.8 us
  transfers between devices with their start and end apart: 6, of which 4 were waited for; matrix products, arithmetic and copies ran while one was open for 1% of the time, Pallas kernels for 0%

profile of v4, /device:TPU:1, one launch (start us, length us, event | category | flops | bytes accessed | tf_op | source)
XLA Modules:
  0.0 291.2 jit_solution(8556908525575054601)
XLA Ops:
  6.5 0.9 convert_reduce_fusion
  7.5 0.7 multiply_add_fusion.6
  8.2 0.7 fusion.236
  43.7 1.6 fusion.237
  55.7 0.7 broadcast_multiply_fusion
  56.4 0.8 copy.43
  57.2 0.8 copy.62
  58.6 2.9 fusion.238
  61.6 0.5 fusion.207
  62.7 1.5 fusion.218
  65.4 1.5 fusion.217
  67.1 0.5 fusion.209
  68.1 1.7 fusion.216
  71.3 1.6 fusion.134
  72.9 1.2 fusion.136
  74.2 0.8 copy-done.16
  75.1 1.6 add_convert_fusion
  76.9 0.6 multiply_convert_fusion.6
  80.3 0.7 copy-done.32
  81.0 1.3 multiply_convert_fusion.4
  82.6 1.9 fusion.85
  85.2 2.4 fusion.132
  87.8 0.9 copy-done.13
  89.4 1.1 fusion.156
  90.5 2.9 fusion.89
  94.0 2.6 fusion.130
  96.8 0.9 copy-done.29
  97.8 1.3 multiply_convert_fusion.2
  99.1 1.1 fusion.154
  100.3 2.9 fusion.93
  103.9 2.5 fusion.128
  106.6 0.9 copy-done.14
  107.8 1.3 multiply_convert_fusion.1
  109.1 1.1 fusion.152
  110.2 2.9 fusion.97
  113.8 2.5 fusion.126
  116.5 0.9 copy-done.12
  117.7 1.3 multiply_convert_fusion
  119.0 1.1 fusion.150
  120.1 2.9 fusion.101
  123.6 2.6 fusion.124
  126.3 1.4 fusion.219
  128.4 2.7 fusion.108
  131.5 0.5 bitcast_dynamic-update-slice_fusion.7
  132.5 1.1 bitcast_dynamic-update-slice_fusion.15
  138.0 4.2 %bitcast_convert_fusion = bf16[12,4,128,128]{3,2,1,0:T(8,128)(2,1)} fusion(f32[4,2,12,64,128]{4,3,2,1,0:T(8,128)S(1)} %bitcast.300, f32[4,2,12,64,128]{4,3,2,1,0:T(8,128)S(1)} %bitcast.299), kind=kOutput, calls=%fused_computation.1 | convolution fusion | flops 604766208 | bytes 7864320 | tf_op jit(solution)/shard_map/bjesr,bjest->ebrt/dot_general | solution.py:90
  142.2 2.5 convert_element_type.92
  144.7 0.9 copy.51
  145.6 58.0 %all_to_all.20 = bf16[12,16,4096]{2,0,1:T(8,128)(2,1)S(1)} all-to-all(bf16[12,16,4096]{2,0,1:T(8,128)(2,1)S(1)} %copy.51), channel_id=1, replica_groups=mesh['zh'=2,'y'=4,'core'=2,'col'=4,'pblk'=4] {'zh','core','col'}, dimensions={1} | all-to-all | bytes 3145728 | tf_op jit(solution)/shard_map/all_to_all | solution.py:112
  203.8 0.9 reshape.175
  205.0 2.5 collective-permute-start.2
  207.5 22.1 %collective-permute-done.2 = bf16[128,4096]{1,0:T(8,128)(2,1)S(1)} collective-permute-done((bf16[128,4096]{1,0:T(8,128)(2,1)S(1)}, bf16[128,4096]{1,0:T(8,128)(2,1)S(1)}, u32[]{:S(2)}, u32[]{:S(2)}) %collective-permute-start.2) | collective-permute-done | bytes 1048608 | tf_op jit(solution)/shard_map/ppermute | solution.py:120
  229.7 3.6 %collective-permute-start.3 = (bf16[64,4096]{1,0:T(8,128)(2,1)S(1)}, bf16[64,4096]{1,0:T(8,128)(2,1)S(1)}, u32[]{:S(2)}, u32[]{:S(2)}) collective-permute-start(bf16[64,4096]{1,0:T(8,128)(2,1)S(1)} %slice.411), channel_id=1, source_target_pairs={{0,3},{1,0},{2,1},{3,2},{4,7},{5,4},{6,5},{7,6},{8,11},{9,8},{10,9... | collective-permute-start | bytes 1572872 | tf_op jit(solution)/shard_map/ppermute | solution.py:123
  233.4 10.0 %collective-permute-done.3 = bf16[64,4096]{1,0:T(8,128)(2,1)S(1)} collective-permute-done((bf16[64,4096]{1,0:T(8,128)(2,1)S(1)}, bf16[64,4096]{1,0:T(8,128)(2,1)S(1)}, u32[]{:S(2)}, u32[]{:S(2)}) %collective-permute-start.3) | collective-permute-done | bytes 524320 | tf_op jit(solution)/shard_map/ppermute | solution.py:123
  243.4 3.2 %collective-permute-done.1 = bf16[64,4096]{1,0:T(8,128)(2,1)S(1)} collective-permute-done((bf16[64,4096]{1,0:T(8,128)(2,1)S(1)}, bf16[64,4096]{1,0:T(8,128)(2,1)S(1)}, u32[]{:S(2)}, u32[]{:S(2)}) %collective-permute-start.1) | collective-permute-done | bytes 524320 | tf_op jit(solution)/shard_map/ppermute | solution.py:122
  246.7 2.3 pad_maximum_fusion
  249.1 2.7 reshape.176
  251.8 2.2 copy.52
  254.1 2.5 reshape.207
  256.6 3.5 %fusion.41 = f32[4,4,64,128]{3,2,0,1:T(8,128)S(1)} fusion(bf16[4,128,4096,1]{2,1,0,3:T(8,128)(2,1)} %bitcast.296, bf16[4,64,4096,1]{2,1,0,3:T(8,128)(2,1)S(1)} %reshape.207), kind=kOutput, calls=%fused_computation.41 | convolution fusion | flops 1073741824 | bytes 6815744 | tf_op jit(solution)/shard_map/rk,lk->rl/dot_general | solution.py:130
  260.1 0.8 copy.57
  260.9 8.0 %all-to-all-start.1 = ((f32[16,64,128]{2,1,0:T(8,128)}), f32[16,64,128]{2,1,0:T(8,128)S(1)}, u32[]{:S(2)}, u32[]{:S(2)}) async-start(f32[16,64,128]{2,1,0:T(8,128)} %bitcast.159), calls=%async_computation.1 | async-start | bytes 1048576 | tf_op jit(solution)/shard_map/all_to_all | solution.py:133
  269.0 14.5 %all-to-all-done.1 = f32[16,64,128]{2,1,0:T(8,128)S(1)} async-done(((f32[16,64,128]{2,1,0:T(8,128)}), f32[16,64,128]{2,1,0:T(8,128)S(1)}, u32[]{:S(2)}, u32[]{:S(2)}) %all-to-all-start.1) | async-done | bytes 524320 | tf_op jit(solution)/shard_map/all_to_all | solution.py:133
  283.6 0.7 copy.59
  (159 shorter events, 14.5 us)
Async XLA Ops:
  6.5 64.8 %copy-start = (bf16[4,768,128]{2,1,0:T(8,128)(2,1)S(1)}, bf16[4,768,128]{2,1,0:T(8,128)(2,1)}, u32[]{:S(2)}) copy-start(bf16[4,768,128]{2,1,0:T(8,128)(2,1)} %param.15) | copy-start | bytes 2359300
  6.5 242.5 %all-gather.2.cloned.1.call-start = ((), (), s32[]{:S(2)}) async-start(), calls=%async_computation.2 | async-start | bytes 2621440 | tf_op jit(solution)/shard_map/all_gather | solution.py:116
  58.6 3.1 %copy-start.15 = (bf16[8,768,256]{2,1,0:T(8,128)(2,1)S(1)}, bf16[8,768,256]{2,1,0:T(8,128)(2,1)}, u32[]{:S(2)}) copy-start(bf16[8,768,256]{2,1,0:T(8,128)(2,1)} %param.11) | copy-start | bytes 9437188
  61.4 0.8 copy-start.19
  61.6 0.8 copy-start.33
  61.6 0.9 copy-start.34
  62.5 1.6 copy-start.52
  62.7 1.5 copy-start.35
  62.7 1.5 copy-start.36
  64.2 0.8 copy-start.22
  64.3 0.8 copy-start.41
  64.3 0.9 copy-start.42
  65.2 1.7 copy-start.24
  65.3 1.7 copy-start.27
  65.4 1.5 copy-start.43
  65.4 1.5 copy-start.44
  67.1 0.7 copy-start.45
  67.1 0.9 copy-start.47
  68.0 1.9 copy-start.30
  68.1 1.7 copy-start.48
  68.1 1.7 copy-start.49
  70.0 2.9 %copy-start.50 = (bf16[12,63,256]{2,1,0:T(8,128)(2,1)}, bf16[12,63,256]{2,1,0:T(8,128)(2,1)S(1)}, u32[]{:S(2)}) copy-start(bf16[12,63,256]{2,1,0:T(8,128)(2,1)S(1)} %get-tuple-element.41) | copy-start | bytes 1161220
  70.0 2.9 %copy-start.51 = (bf16[12,63,256]{2,1,0:T(8,128)(2,1)}, bf16[12,63,256]{2,1,0:T(8,128)(2,1)S(1)}, u32[]{:S(2)}) copy-start(bf16[12,63,256]{2,1,0:T(8,128)(2,1)S(1)} %get-tuple-element.42) | copy-start | bytes 1161220
  72.9 2.0 copy-start.16
  72.9 2.2 copy-start.53
  76.8 0.8 copy-start.20
  76.9 0.8 copy-start.37
  76.9 0.9 copy-start.39
  77.8 0.7 copy-start.17
  78.9 1.0 copy-start.25
  79.9 1.1 copy-start.32
  82.4 2.8 copy-start.46
  85.2 2.4 copy-start.9
  87.6 1.1 copy-start.13
  87.6 1.4 copy-start.31
  94.0 2.7 copy-start.7
  96.7 1.1 copy-start.29
  99.1 4.8 %copy-start.23 = (bf16[12,64,256]{2,1,0:T(8,128)(2,1)S(1)}, bf16[12,64,256]{2,1,0:T(8,128)(2,1)}, u32[]{:S(2)}) copy-start(bf16[12,64,256]{2,1,0:T(8,128)(2,1)} %copy-done.22) | copy-start | bytes 1179652
  103.9 2.5 copy-start.10
  106.4 1.1 copy-start.14
  106.4 1.4 copy-start.28
  113.8 2.5 copy-start.8
  116.3 1.1 copy-start.12
  116.3 1.4 copy-start.26
  123.6 2.7 copy-start.11
  128.3 2.8 copy-start.1
  128.3 2.8 copy-start.2
  128.3 2.8 copy-start.3
  128.3 2.8 copy-start.4
  128.3 2.8 copy-start.5
  128.4 2.8 copy-start.6
  128.4 2.9 copy-start.21
  128.4 3.0 %copy-start.38 = (bf16[12,63,256]{2,1,0:T(8,128)(2,1)S(1)}, bf16[12,63,256]{2,1,0:T(8,128)(2,1)}, u32[]{:S(2)}) copy-start(bf16[12,63,256]{2,1,0:T(8,128)(2,1)} %copy-done.37) | copy-start | bytes 1161220
  128.4 3.1 %copy-start.40 = (bf16[12,63,256]{2,1,0:T(8,128)(2,1)S(1)}, bf16[12,63,256]{2,1,0:T(8,128)(2,1)}, u32[]{:S(2)}) copy-start(bf16[12,63,256]{2,1,0:T(8,128)(2,1)} %copy-done.39) | copy-start | bytes 1161220
  131.5 1.0 copy-start.18
  205.0 24.7 %collective-permute-start.2 = (bf16[128,4096]{1,0:T(8,128)(2,1)S(1)}, bf16[128,4096]{1,0:T(8,128)(2,1)S(1)}, u32[]{:S(2)}, u32[]{:S(2)}) collective-permute-start(bf16[128,4096]{1,0:T(8,128)(2,1)S(1)} %get-tuple-element.38), channel_id=1, source_target_pairs={{0,3},{1,0},{2,1},{3,2},{4,7},{5,4},{6,5},{7,6},{8,11},{9,8},{10,9... | collective-permute-start | bytes 3145736 | tf_op jit(solution)/shard_map/ppermute | solution.py:120
  207.5 25.8 %collective-permute-start = (bf16[128,4096]{1,0:T(8,128)(2,1)S(1)}, bf16[128,4096]{1,0:T(8,128)(2,1)S(1)}, u32[]{:S(2)}, u32[]{:S(2)}) collective-permute-start(bf16[128,4096]{1,0:T(8,128)(2,1)S(1)} %get-tuple-element.38), channel_id=1, source_target_pairs={{0,1},{1,2},{2,3},{3,0},{4,5},{5,6},{6,7},{7,4},{8,9},{9,10},{10,1... | collective-permute-start | bytes 3145736 | tf_op jit(solution)/shard_map/ppermute | solution.py:119
  229.7 13.7 %collective-permute-start.3 = (bf16[64,4096]{1,0:T(8,128)(2,1)S(1)}, bf16[64,4096]{1,0:T(8,128)(2,1)S(1)}, u32[]{:S(2)}, u32[]{:S(2)}) collective-permute-start(bf16[64,4096]{1,0:T(8,128)(2,1)S(1)} %slice.411), channel_id=1, source_target_pairs={{0,3},{1,0},{2,1},{3,2},{4,7},{5,4},{6,5},{7,6},{8,11},{9,8},{10,9... | collective-permute-start | bytes 1572872 | tf_op jit(solution)/shard_map/ppermute | solution.py:123
  233.3 13.4 %collective-permute-start.1 = (bf16[64,4096]{1,0:T(8,128)(2,1)S(1)}, bf16[64,4096]{1,0:T(8,128)(2,1)S(1)}, u32[]{:S(2)}, u32[]{:S(2)}) collective-permute-start(bf16[64,4096]{1,0:T(8,128)(2,1)S(1)} %slice.410), channel_id=1, source_target_pairs={{0,1},{1,2},{2,3},{3,0},{4,5},{5,6},{6,7},{7,4},{8,9},{9,10},{10,1... | collective-permute-start | bytes 1572872 | tf_op jit(solution)/shard_map/ppermute | solution.py:122
  260.9 22.5 %all-to-all-start.1 = ((f32[16,64,128]{2,1,0:T(8,128)}), f32[16,64,128]{2,1,0:T(8,128)S(1)}, u32[]{:S(2)}, u32[]{:S(2)}) async-start(f32[16,64,128]{2,1,0:T(8,128)} %bitcast.159), calls=%async_computation.1 | async-start | bytes 1048576 | tf_op jit(solution)/shard_map/all_to_all | solution.py:133
Sparse Core Ops, SparseCore 0:
  204.8 32.7 all-gather.1

commit v5 on v3

--- a/solution.py
+++ b/solution.py
@@ -98,12 +98,20 @@
     own = panel.shape[0]
     width = panel.shape[1] // n_group
     sliced = panel.reshape(own, n_group, width)
+    left_part = lax.all_to_all(sliced[:left_each], group, split_axis=1, concat_axis=0, tiled=True)
+    left_part = left_part.reshape(n_group * left_each, width)
+    up = [(j, (j + 1) % n_blk) for j in range(n_blk)]
+    down = [(j, (j - 1) % n_blk) for j in range(n_blk)]
+    from_below = lax.ppermute(left_part, "pblk", up)
+    from_above = lax.ppermute(left_part, "pblk", down)
+    half = left_part.shape[0] // 2
+    far_low = lax.ppermute(from_below[:half], "pblk", up)
+    far_high = lax.ppermute(from_above[half:], "pblk", down)
+    far = jnp.concatenate([far_low, far_high], 0)
     right_part = lax.all_to_all(sliced[left_each:], group, split_axis=1, concat_axis=0, tiled=True)
     right_part = right_part.reshape(n_group * right_each, width)
-    left_part = lax.all_to_all(sliced[:left_each], group, split_axis=1, concat_axis=0, tiled=True)
-    left_part = left_part.reshape(n_group * left_each, width)
-    left_tile = lax.all_gather(left_part, "pblk", axis=0, tiled=True)
     right_tile = lax.all_gather(right_part, "y", axis=0, tiled=True)
+    left_tile = jnp.stack([far, from_below, left_part, from_above])
     left_tile = left_tile.reshape(n_blk, n_zh * n_core, n_col, left_each, width)
     left_tile = jnp.transpose(left_tile, (1, 2, 0, 3, 4)).reshape(-1, width)
     right_tile = right_tile.reshape(n_y, n_zh, n_core, n_col, right_each, width)
@@ -112,7 +120,10 @@
     chunks = partial_t.reshape(n_col, partial_t.shape[0] // n_col, n_zh * n_core, -1)
     chunks = jnp.transpose(chunks, (2, 0, 1, 3)).reshape(n_group, chunks.shape[1], chunks.shape[3])
     received = lax.all_to_all(chunks, group, split_axis=0, concat_axis=0, tiled=True)
-    return jnp.sum(received, axis=0).T
+    block = jnp.sum(received, axis=0).T
+    block = block.reshape(n_col, n_blk, left_each, block.shape[1])
+    block = jnp.roll(block, lax.axis_index("pblk") - 2, axis=1)
+    return block.reshape(-1, block.shape[3])
 
 
 def solution(mesh):

time: 234 us -> 233 us (level)
  blocking collectives: 77.7 us -> 0 us
  waiting for transfers between devices: 45.1 us -> 82.8 us
  starting transfers between devices: 0.26 us -> 33.4 us
    all_to_all x3 -> x0, blocking collectives: 77.7 us -> none  [the longest x1 31.3 us: on_device(): lax.all_to_all(sliced[:left_each], group, split_axis=1, concat_axis=0, ti...]
    all_to_all x0 -> x3, waiting for transfers between devices: none -> 50 us  [the longest x1 23.1 us: on_device(): lax.all_to_all(sliced[:left_each], group, split_axis=1, concat_axis=0, ti...]
    all_gather x1 -> x0, waiting for transfers between devices: 45 us -> none  [on_device(): left_tile = lax.all_gather(left_part, 'pblk', axis=0, tiled=True)]
    ppermute x0 -> x4, waiting for transfers between devices: none -> 32.7 us  [the longest x1 20.9 us: on_device(): from_above = lax.ppermute(left_part, 'pblk', down)]
    all_to_all x0 -> x3, starting transfers between devices: none -> 27.3 us  [the longest x1 11.3 us: on_device(): lax.all_to_all(chunks, group, split_axis=0, concat_axis=0, tiled=True)]
    ppermute x0 -> x4, starting transfers between devices: none -> 6.05 us  [the longest x1 3.49 us: on_device(): far_high = lax.ppermute(from_above[half:], 'pblk', down)]
    transpose x1, local copies, waits for them, and re-layouts: 2.46 us -> 0.09 us  [on_device(): block = jnp.sum(received, axis=0).T]
  transfers between devices with their start and end apart: 2 -> 8, of which waited for: 2 -> 6; matrix products, arithmetic and copies ran while one was open for 4% -> 3% of each run, Pallas kernels for 0% -> 0%
where the time goes in v5:
time: 233 us; the launch traced here: 231 us
  waiting for transfers between devices  82.8 us (36%)
  matrix products  44.6 us (19%)
  local copies, waits for them, and re-layouts  34.1 us (15%)
  starting transfers between devices  33.4 us (14%)
  between operations  29.6 us (13%)
  other arithmetic  7.08 us (3%)
    all_to_all x1, waiting for transfers between devices, on_device(): lax.all_to_all(sliced[:left_each], group, split_axis=1, concat_axis=0, ti...  23.1 us
    ppermute x1, waiting for transfers between devices, on_device(): from_above = lax.ppermute(left_part, 'pblk', down)  20.9 us
    dot_general x8, matrix products, panels(): jnp.einsum('esk,kt->est', wides[layer], proj_input[assign[layer]], prefer...  16.1 us
    all_to_all x1, waiting for transfers between devices, on_device(): lax.all_to_all(chunks, group, split_axis=0, concat_axis=0, tiled=True)  14.5 us
    all_to_all x1, waiting for transfers between devices, on_device(): lax.all_to_all(sliced[left_each:], group, split_axis=1, concat_axis=0, ti...  12.4 us
    all_to_all x1, starting transfers between devices, on_device(): lax.all_to_all(chunks, group, split_axis=0, concat_axis=0, tiled=True)  11.3 us
    all_to_all x1, starting transfers between devices, on_device(): lax.all_to_all(sliced[left_each:], group, split_axis=1, concat_axis=0, ti...  9.99 us
    ppermute x1, waiting for transfers between devices, on_device(): far_high = lax.ppermute(from_above[half:], 'pblk', down)  8.63 us
  transfers between devices with their start and end apart: 8, of which 6 were waited for; matrix products, arithmetic and copies ran while one was open for 3% of the time, Pallas kernels for 0%

profile of v5, /device:TPU:1, one launch (start us, length us, event | category | flops | bytes accessed | tf_op | source)
XLA Modules:
  0.0 231.5 jit_solution(2988020424608891672)
XLA Ops:
  6.5 1.6 fusion.237
  18.3 0.9 convert_reduce_fusion
  19.2 0.8 copy.65
  20.0 0.8 copy.45
  21.4 2.9 %fusion.238 = (bf16[12,64,256]{2,1,0:T(8,128)(2,1)S(1)}, f32[12,64,256]{2,1,0:T(8,128)S(1)}) fusion(bf16[1024,256]{1,0:T(8,128)(2,1)} %param.10, s32[12,64]{1,0:T(8,128)S(1)} %bitcast.290, s32[12,64]{1,0:T(8,128)S(1)} %bitcast.291, s32[12,64]{1,0:T(8,128)S(1)} %bitcast.292, s32[12,64]{1,0:T(8,128)S(1)} %bitcast.293), kind=kOutput, calls=%fused_computation.272 | convolution fusion | flops 415432704 | bytes 1716224 | tf_op jit(solution)/shard_map/esv,vc->esc/dot_general | solution.py:30
  24.5 0.5 fusion.209
  25.5 0.7 fusion.220
  26.8 0.5 fusion.210
  27.8 0.7 fusion.219
  28.8 0.5 fusion.211
  29.9 0.7 fusion.218
  31.0 0.5 add_convert_fusion
  32.2 0.6 multiply_convert_fusion.6
  32.9 0.5 fusion.95
  34.1 0.5 fusion.98
  35.2 0.5 fusion.102
  36.4 0.5 fusion.106
  37.6 0.5 fusion.110
  38.9 0.5 fusion.114
  39.7 1.3 multiply_convert_fusion
  41.0 0.7 copy-done.9
  41.7 0.5 fusion.118
  42.3 1.3 fusion.221
  44.2 2.5 %fusion.51 = f32[8,12,64,128]{3,2,1,0:T(8,128)} fusion(bf16[4,768,128]{2,1,0:T(8,128)(2,1)S(1)} %copy-done, s32[]{:T(128)S(6)} %select_n.60, bf16[12,63,256]{2,1,0:T(8,128)(2,1)} %copy-done.53, bf16[12,63,256]{2,1,0:T(8,128)(2,1)} %copy-done.52, bf16[12,64,256]{2,1,0:T(8,128)(2,1)} %copy-done.25), kind=kOutput, calls=%fused_computation.59 | convolution fusion | flops 156893184 | bytes 1757188 | tf_op jit(solution)/shard_map/esk,kt->est/dot_general | solution.py:51
  47.4 2.6 %fusion.50 = f32[8,12,64,128]{3,2,1,0:T(8,128)} fusion(f32[8,12,64,128]{3,2,1,0:T(8,128)} %fusion.51, bf16[4,768,128]{2,1,0:T(8,128)(2,1)S(1)} %copy-done, s32[]{:T(128)S(6)} %select_n.61, bf16[12,63,256]{2,1,0:T(8,128)(2,1)} %copy-done.55, bf16[12,63,256]{2,1,0:T(8,128)(2,1)} %copy-done.54, bf16[12,64,256]{2,1,0:T(8,128)(2,1)} %copy-done.26), kind=kOutput, calls=%fused_computation.57 | convolution fusion | flops 156893184 | bytes 1769476 | tf_op jit(solution)/shard_map/esk,kt->est/dot_general | solution.py:51
  50.0 1.3 fusion.59
  51.3 1.0 fusion.58
  53.0 2.6 %fusion.49 = f32[8,12,64,128]{3,2,1,0:T(8,128)} fusion(f32[8,12,64,128]{3,2,1,0:T(8,128)} %fusion.50, bf16[4,768,128]{2,1,0:T(8,128)(2,1)S(1)} %copy-done, s32[]{:T(128)S(6)} %select_n.62, bf16[12,63,256]{2,1,0:T(8,128)(2,1)} %copy-done.51, bf16[12,63,256]{2,1,0:T(8,128)(2,1)} %copy-done.50, bf16[12,64,256]{2,1,0:T(8,128)(2,1)} %copy-done.24), kind=kOutput, calls=%fused_computation.55 | convolution fusion | flops 156893184 | bytes 1769476 | tf_op jit(solution)/shard_map/esk,kt->est/dot_general | solution.py:51
  55.6 1.0 fusion.57
  57.3 1.2 fusion.48
  58.5 1.0 fusion.56
  60.3 2.4 %fusion.47 = f32[8,12,64,128]{3,2,1,0:T(8,128)} fusion(f32[8,12,64,128]{3,2,1,0:T(8,128)} %fusion.48, bf16[4,768,128]{2,1,0:T(8,128)(2,1)S(1)} %copy-done, s32[]{:T(128)S(6)} %select_n.64, bf16[12,63,256]{2,1,0:T(8,128)(2,1)} %copy-done.45, bf16[12,63,256]{2,1,0:T(8,128)(2,1)S(1)} %copy-done.44, bf16[12,64,256]{2,1,0:T(8,128)(2,1)S(1)} %copy-done.21), kind=kOutput, calls=%fused_computation.51 | convolution fusion | flops 156893184 | bytes 1769476 | tf_op jit(solution)/shard_map/esk,kt->est/dot_general | solution.py:51
  62.7 1.0 fusion.55
  64.4 1.3 fusion.46
  65.7 1.0 fusion.54
  67.4 2.3 %fusion.45 = f32[8,12,64,128]{3,2,1,0:T(8,128)} fusion(f32[8,12,64,128]{3,2,1,0:T(8,128)} %fusion.46, bf16[4,768,128]{2,1,0:T(8,128)(2,1)S(1)} %copy-done, s32[]{:T(128)S(6)} %select_n.66, bf16[12,63,256]{2,1,0:T(8,128)(2,1)} %copy-done.38, bf16[12,63,256]{2,1,0:T(8,128)(2,1)S(1)} %copy-done.37, bf16[12,64,256]{2,1,0:T(8,128)(2,1)S(1)} %copy-done.15), kind=kOutput, calls=%fused_computation.47 | convolution fusion | flops 156893184 | bytes 1769476 | tf_op jit(solution)/shard_map/esk,kt->est/dot_general | solution.py:51
  69.7 1.0 fusion.53
  71.4 1.2 fusion.44
  72.6 1.0 fusion.52
  73.7 4.3 %gather_fusion.1 = f32[8,12,64,128]{3,2,1,0:T(8,128)} fusion(f32[8,12,64,128]{3,2,1,0:T(8,128)} %fusion.44, s32[1024]{0:T(1024)S(1)} %pad_clamp_fusion), kind=kCustom, calls=%fused_computation.1 | custom fusion | bytes 6291488 | tf_op jit(solution)/shard_map/gather | solution.py:75
  77.9 4.3 %gather_fusion = f32[8,12,64,128]{3,2,1,0:T(8,128)} fusion(f32[8,12,64,128]{3,2,1,0:T(8,128)} %fusion.52, s32[1024]{0:T(1024)S(1)} %pad_clamp_fusion), kind=kCustom, calls=%fused_computation | custom fusion | bytes 6291488 | tf_op jit(solution)/shard_map/gather | solution.py:74
  82.2 5.5 %bitcast_convert_fusion = bf16[12,4,128,128]{3,2,1,0:T(8,128)(2,1)S(1)} fusion(f32[4,2,12,64,128]{4,3,2,1,0:T(8,128)} %bitcast.275, f32[4,2,12,64,128]{4,3,2,1,0:T(8,128)} %bitcast.276), kind=kOutput, calls=%fused_computation.3 | convolution fusion | flops 604766208 | bytes 7864320 | tf_op jit(solution)/shard_map/bjesr,bjest->ebrt/dot_general | solution.py:79
  88.0 1.2 copy.53
  89.2 10.0 %all-to-all-start = ((bf16[4,16,4096]{2,0,1:T(4,128)(2,1)}), bf16[4,16,4096]{2,0,1:T(4,128)(2,1)}, u32[]{:S(2)}, u32[]{:S(2)}) async-start(bf16[4,16,4096]{2,0,1:T(4,128)(2,1)} %copy.53), calls=%async_computation | async-start | bytes 1048576 | tf_op jit(solution)/shard_map/all_to_all | solution.py:111
  99.3 0.5 slice.294
  99.8 1.5 copy.55
  101.3 12.4 %all-to-all-done = bf16[4,16,4096]{2,0,1:T(4,128)(2,1)} async-done(((bf16[4,16,4096]{2,0,1:T(4,128)(2,1)}), bf16[4,16,4096]{2,0,1:T(4,128)(2,1)}, u32[]{:S(2)}, u32[]{:S(2)}) %all-to-all-start) | async-done | bytes 524320 | tf_op jit(solution)/shard_map/all_to_all | solution.py:111
  113.7 5.9 %all-to-all-start.1 = ((bf16[8,16,4096]{2,0,1:T(8,128)(2,1)}), bf16[8,16,4096]{2,0,1:T(8,128)(2,1)S(1)}, u32[]{:S(2)}, u32[]{:S(2)}) async-start(bf16[8,16,4096]{2,0,1:T(8,128)(2,1)} %copy.55), calls=%async_computation.1 | async-start | bytes 2097152 | tf_op jit(solution)/shard_map/all_to_all | solution.py:101
  119.7 2.0 reshape.79
  121.7 23.1 %all-to-all-done.1 = bf16[8,16,4096]{2,0,1:T(8,128)(2,1)S(1)} async-done(((bf16[8,16,4096]{2,0,1:T(8,128)(2,1)}), bf16[8,16,4096]{2,0,1:T(8,128)(2,1)S(1)}, u32[]{:S(2)}, u32[]{:S(2)}) %all-to-all-start.1) | async-done | bytes 1048608 | tf_op jit(solution)/shard_map/all_to_all | solution.py:101
  144.8 2.5 %collective-permute-start.2 = (bf16[128,4096]{1,0:T(8,128)(2,1)S(1)}, bf16[128,4096]{1,0:T(8,128)(2,1)S(1)}, u32[]{:S(2)}, u32[]{:S(2)}) collective-permute-start(bf16[128,4096]{1,0:T(8,128)(2,1)S(1)} %bitcast.279), channel_id=1, source_target_pairs={{0,3},{1,0},{2,1},{3,2},{4,7},{5,4},{6,5},{7,6},{8,11},{9,8},{10,9... | collective-permute-start | bytes 3145736 | tf_op jit(solution)/shard_map/ppermute | solution.py:106
  147.3 20.9 %collective-permute-done.2 = bf16[128,4096]{1,0:T(8,128)(2,1)S(1)} collective-permute-done((bf16[128,4096]{1,0:T(8,128)(2,1)S(1)}, bf16[128,4096]{1,0:T(8,128)(2,1)S(1)}, u32[]{:S(2)}, u32[]{:S(2)}) %collective-permute-start.2) | collective-permute-done | bytes 1048608 | tf_op jit(solution)/shard_map/ppermute | solution.py:106
  168.2 3.5 %collective-permute-start.3 = (bf16[64,4096]{1,0:T(8,128)(2,1)S(1)}, bf16[64,4096]{1,0:T(8,128)(2,1)S(1)}, u32[]{:S(2)}, u32[]{:S(2)}) collective-permute-start(bf16[64,4096]{1,0:T(8,128)(2,1)S(1)} %slice.345), channel_id=1, source_target_pairs={{0,3},{1,0},{2,1},{3,2},{4,7},{5,4},{6,5},{7,6},{8,11},{9,8},{10,9... | collective-permute-start | bytes 1572872 | tf_op jit(solution)/shard_map/ppermute | solution.py:109
  171.8 8.6 %collective-permute-done.3 = bf16[64,4096]{1,0:T(8,128)(2,1)S(1)} collective-permute-done((bf16[64,4096]{1,0:T(8,128)(2,1)S(1)}, bf16[64,4096]{1,0:T(8,128)(2,1)S(1)}, u32[]{:S(2)}, u32[]{:S(2)}) %collective-permute-start.3) | collective-permute-done | bytes 524320 | tf_op jit(solution)/shard_map/ppermute | solution.py:109
  180.5 3.3 %collective-permute-done.1 = bf16[64,4096]{1,0:T(8,128)(2,1)S(1)} collective-permute-done((bf16[64,4096]{1,0:T(8,128)(2,1)S(1)}, bf16[64,4096]{1,0:T(8,128)(2,1)S(1)}, u32[]{:S(2)}, u32[]{:S(2)}) %collective-permute-start.1) | collective-permute-done | bytes 524320 | tf_op jit(solution)/shard_map/ppermute | solution.py:108
  183.8 2.3 pad_maximum_fusion
  186.1 2.7 %reshape.80 = bf16[4,2,2,4,4,4096]{5,4,3,2,1,0:T(4,128)(2,1)S(1)} reshape(bf16[256,4096]{1,0:T(8,128)(2,1)} %all-gather.2.cloned.1.call-done) | data formatting | bytes 4194304 | tf_op jit(solution)/shard_map/reshape | solution.py:117
  188.8 2.2 copy.54
  191.1 2.5 %reshape.127 = bf16[4,64,4096,1]{2,1,0,3:T(8,128)(2,1)S(1)} reshape(bf16[4,2,4,2,4,4096]{5,4,3,2,1,0:T(4,128)(2,1)} %copy.54) | data formatting | bytes 4194304 | tf_op jit(solution)/shard_map/rk,lk->rl/dot_general | solution.py:119
  193.6 3.5 %fusion.41 = f32[4,4,64,128]{3,2,0,1:T(8,128)S(1)} fusion(bf16[4,128,4096,1]{2,1,0,3:T(8,128)(2,1)} %bitcast.278, bf16[4,64,4096,1]{2,1,0,3:T(8,128)(2,1)S(1)} %reshape.127), kind=kOutput, calls=%fused_computation.43 | convolution fusion | flops 1073741824 | bytes 6815744 | tf_op jit(solution)/shard_map/rk,lk->rl/dot_general | solution.py:119
  197.1 0.9 copy.60
  198.0 11.3 %all-to-all-start.2 = ((f32[16,64,128]{2,1,0:T(8,128)}), f32[16,64,128]{2,1,0:T(8,128)S(1)}, u32[]{:S(2)}, u32[]{:S(2)}) async-start(f32[16,64,128]{2,1,0:T(8,128)} %bitcast.106), calls=%async_computation.2 | async-start | bytes 1048576 | tf_op jit(solution)/shard_map/all_to_all | solution.py:122
  209.3 14.5 %all-to-all-done.2 = f32[16,64,128]{2,1,0:T(8,128)S(1)} async-done(((f32[16,64,128]{2,1,0:T(8,128)}), f32[16,64,128]{2,1,0:T(8,128)S(1)}, u32[]{:S(2)}, u32[]{:S(2)}) %all-to-all-start.2) | async-done | bytes 524320 | tf_op jit(solution)/shard_map/all_to_all | solution.py:122
  223.9 0.7 copy.62
  (165 shorter events, 8.7 us)
Async XLA Ops:
  6.5 37.7 %copy-start = (bf16[4,768,128]{2,1,0:T(8,128)(2,1)S(1)}, bf16[4,768,128]{2,1,0:T(8,128)(2,1)}, u32[]{:S(2)}) copy-start(bf16[4,768,128]{2,1,0:T(8,128)(2,1)} %param.15) | copy-start | bytes 2359300
  21.4 3.1 %copy-start.11 = (bf16[8,768,256]{2,1,0:T(8,128)(2,1)S(1)}, bf16[8,768,256]{2,1,0:T(8,128)(2,1)}, u32[]{:S(2)}) copy-start(bf16[8,768,256]{2,1,0:T(8,128)(2,1)} %param.11) | copy-start | bytes 9437188
  24.3 0.8 copy-start.25
  24.4 0.8 copy-start.52
  24.4 0.9 copy-start.53
  25.3 0.8 copy-start.26
  25.3 1.0 copy-start.58
  25.5 1.0 copy-start.54
  25.5 1.1 copy-start.55
  26.7 0.8 copy-start.50
  26.8 0.9 copy-start.51
  27.6 0.8 copy-start.22
  27.8 0.9 copy-start.48
  28.7 0.8 copy-start.20
  28.8 0.8 copy-start.43
  28.8 0.9 copy-start.45
  29.7 0.9 copy-start.16
  29.9 0.8 copy-start.39
  29.9 0.9 copy-start.41
  30.8 0.8 copy-start.14
  30.9 0.8 copy-start.36
  31.0 0.9 copy-start.38
  31.0 1.0 copy-start.56
  31.0 1.2 copy-start.57
  31.8 0.9 copy-start.12
  32.0 0.8 copy-start.32
  32.0 0.9 copy-start.34
  35.2 0.8 copy-start.1
  36.4 0.8 copy-start.3
  37.6 0.9 copy-start.5
  38.9 0.8 copy-start.7
  47.3 2.7 %copy-start.27 = (bf16[4,256,128]{2,1,0:T(8,128)(2,1)S(1)}, bf16[4,256,128]{2,1,0:T(8,128)(2,1)}, u32[]{:S(2)}) copy-start(bf16[4,256,128]{2,1,0:T(8,128)(2,1)} %param.14) | copy-start | bytes 786436
  47.3 2.7 %copy-start.29 = (f32[12,64,256]{2,1,0:T(8,128)S(1)}, f32[12,64,256]{2,1,0:T(8,128)}, u32[]{:S(2)}) copy-start(f32[12,64,256]{2,1,0:T(8,128)} %get-tuple-element.6) | copy-start | bytes 2359300
  47.3 2.7 %copy-start.30 = (f32[12,63,256]{2,1,0:T(8,128)S(1)}, f32[12,63,256]{2,1,0:T(8,128)}, u32[]{:S(2)}) copy-start(f32[12,63,256]{2,1,0:T(8,128)} %get-tuple-element.23) | copy-start | bytes 2322436
  47.4 2.7 %copy-start.31 = (f32[12,63,256]{2,1,0:T(8,128)S(1)}, f32[12,63,256]{2,1,0:T(8,128)}, u32[]{:S(2)}) copy-start(f32[12,63,256]{2,1,0:T(8,128)} %get-tuple-element.24) | copy-start | bytes 2322436
  47.4 2.7 %copy-start.59 = (f32[12,64,256]{2,1,0:T(8,128)S(1)}, f32[12,64,256]{2,1,0:T(8,128)}, u32[]{:S(2)}) copy-start(f32[12,64,256]{2,1,0:T(8,128)} %copy-done.58) | copy-start | bytes 2359300
  50.0 1.3 copy-start.10
  53.0 2.7 %copy-start.8 = (bf16[12,64,256]{2,1,0:T(8,128)(2,1)S(1)}, bf16[12,64,256]{2,1,0:T(8,128)(2,1)}, u32[]{:S(2)}) copy-start(bf16[12,64,256]{2,1,0:T(8,128)(2,1)} %copy-done.7) | copy-start | bytes 1179652
  53.0 2.6 %copy-start.28 = (bf16[4,256,128]{2,1,0:T(8,128)(2,1)S(1)}, bf16[4,256,128]{2,1,0:T(8,128)(2,1)}, u32[]{:S(2)}) copy-start(bf16[4,256,128]{2,1,0:T(8,128)(2,1)} %param.14) | copy-start | bytes 786436
  53.0 4.3 %copy-start.23 = (bf16[12,64,256]{2,1,0:T(8,128)(2,1)S(1)}, bf16[12,64,256]{2,1,0:T(8,128)(2,1)}, u32[]{:S(2)}) copy-start(bf16[12,64,256]{2,1,0:T(8,128)(2,1)} %copy-done.22) | copy-start | bytes 1179652
  53.0 4.3 %copy-start.47 = (bf16[12,63,256]{2,1,0:T(8,128)(2,1)S(1)}, bf16[12,63,256]{2,1,0:T(8,128)(2,1)}, u32[]{:S(2)}) copy-start(bf16[12,63,256]{2,1,0:T(8,128)(2,1)} %copy-done.46) | copy-start | bytes 1161220
  53.0 4.3 %copy-start.49 = (bf16[12,63,256]{2,1,0:T(8,128)(2,1)S(1)}, bf16[12,63,256]{2,1,0:T(8,128)(2,1)}, u32[]{:S(2)}) copy-start(bf16[12,63,256]{2,1,0:T(8,128)(2,1)} %copy-done.48) | copy-start | bytes 1161220
  57.3 1.3 copy-start.6
  57.3 3.0 %copy-start.21 = (bf16[12,64,256]{2,1,0:T(8,128)(2,1)S(1)}, bf16[12,64,256]{2,1,0:T(8,128)(2,1)}, u32[]{:S(2)}) copy-start(bf16[12,64,256]{2,1,0:T(8,128)(2,1)} %copy-done.20) | copy-start | bytes 1179652
  57.3 3.0 %copy-start.44 = (bf16[12,63,256]{2,1,0:T(8,128)(2,1)S(1)}, bf16[12,63,256]{2,1,0:T(8,128)(2,1)}, u32[]{:S(2)}) copy-start(bf16[12,63,256]{2,1,0:T(8,128)(2,1)} %copy-done.43) | copy-start | bytes 1161220
  60.3 2.4 %copy-start.4 = (bf16[12,64,256]{2,1,0:T(8,128)(2,1)S(1)}, bf16[12,64,256]{2,1,0:T(8,128)(2,1)}, u32[]{:S(2)}) copy-start(bf16[12,64,256]{2,1,0:T(8,128)(2,1)} %copy-done.3) | copy-start | bytes 1179652
  60.3 4.1 %copy-start.17 = (bf16[12,64,256]{2,1,0:T(8,128)(2,1)S(1)}, bf16[12,64,256]{2,1,0:T(8,128)(2,1)}, u32[]{:S(2)}) copy-start(bf16[12,64,256]{2,1,0:T(8,128)(2,1)} %copy-done.16) | copy-start | bytes 1179652
  60.3 4.1 %copy-start.40 = (bf16[12,63,256]{2,1,0:T(8,128)(2,1)S(1)}, bf16[12,63,256]{2,1,0:T(8,128)(2,1)}, u32[]{:S(2)}) copy-start(bf16[12,63,256]{2,1,0:T(8,128)(2,1)} %copy-done.39) | copy-start | bytes 1161220
  60.3 4.1 %copy-start.42 = (bf16[12,63,256]{2,1,0:T(8,128)(2,1)S(1)}, bf16[12,63,256]{2,1,0:T(8,128)(2,1)}, u32[]{:S(2)}) copy-start(bf16[12,63,256]{2,1,0:T(8,128)(2,1)} %copy-done.41) | copy-start | bytes 1161220
  64.4 1.3 copy-start.2
  64.4 2.9 %copy-start.15 = (bf16[12,64,256]{2,1,0:T(8,128)(2,1)S(1)}, bf16[12,64,256]{2,1,0:T(8,128)(2,1)}, u32[]{:S(2)}) copy-start(bf16[12,64,256]{2,1,0:T(8,128)(2,1)} %copy-done.14) | copy-start | bytes 1179652
  64.4 2.9 %copy-start.37 = (bf16[12,63,256]{2,1,0:T(8,128)(2,1)S(1)}, bf16[12,63,256]{2,1,0:T(8,128)(2,1)}, u32[]{:S(2)}) copy-start(bf16[12,63,256]{2,1,0:T(8,128)(2,1)} %copy-done.36) | copy-start | bytes 1161220
  67.3 4.0 %copy-start.13 = (bf16[12,64,256]{2,1,0:T(8,128)(2,1)S(1)}, bf16[12,64,256]{2,1,0:T(8,128)(2,1)}, u32[]{:S(2)}) copy-start(bf16[12,64,256]{2,1,0:T(8,128)(2,1)} %copy-done.12) | copy-start | bytes 1179652
  67.4 4.0 %copy-start.33 = (bf16[12,63,256]{2,1,0:T(8,128)(2,1)S(1)}, bf16[12,63,256]{2,1,0:T(8,128)(2,1)}, u32[]{:S(2)}) copy-start(bf16[12,63,256]{2,1,0:T(8,128)(2,1)} %copy-done.32) | copy-start | bytes 1161220
  67.4 4.0 %copy-start.35 = (bf16[12,63,256]{2,1,0:T(8,128)(2,1)S(1)}, bf16[12,63,256]{2,1,0:T(8,128)(2,1)}, u32[]{:S(2)}) copy-start(bf16[12,63,256]{2,1,0:T(8,128)(2,1)} %copy-done.34) | copy-start | bytes 1161220
  71.4 1.2 copy-start.19
  89.2 24.6 %all-to-all-start = ((bf16[4,16,4096]{2,0,1:T(4,128)(2,1)}), bf16[4,16,4096]{2,0,1:T(4,128)(2,1)}, u32[]{:S(2)}, u32[]{:S(2)}) async-start(bf16[4,16,4096]{2,0,1:T(4,128)(2,1)} %copy.53), calls=%async_computation | async-start | bytes 1048576 | tf_op jit(solution)/shard_map/all_to_all | solution.py:111
  113.7 31.1 %all-to-all-start.1 = ((bf16[8,16,4096]{2,0,1:T(8,128)(2,1)}), bf16[8,16,4096]{2,0,1:T(8,128)(2,1)S(1)}, u32[]{:S(2)}, u32[]{:S(2)}) async-start(bf16[8,16,4096]{2,0,1:T(8,128)(2,1)} %copy.55), calls=%async_computation.1 | async-start | bytes 2097152 | tf_op jit(solution)/shard_map/all_to_all | solution.py:101
  119.7 66.4 %all-gather.2.cloned.1.call-start = ((), (), s32[]{:S(2)}) async-start(), calls=%async_computation.3 | async-start | bytes 2621440 | tf_op jit(solution)/shard_map/all_gather | solution.py:113
  144.8 23.3 %collective-permute-start.2 = (bf16[128,4096]{1,0:T(8,128)(2,1)S(1)}, bf16[128,4096]{1,0:T(8,128)(2,1)S(1)}, u32[]{:S(2)}, u32[]{:S(2)}) collective-permute-start(bf16[128,4096]{1,0:T(8,128)(2,1)S(1)} %bitcast.279), channel_id=1, source_target_pairs={{0,3},{1,0},{2,1},{3,2},{4,7},{5,4},{6,5},{7,6},{8,11},{9,8},{10,9... | collective-permute-start | bytes 3145736 | tf_op jit(solution)/shard_map/ppermute | solution.py:106
  147.3 24.4 %collective-permute-start = (bf16[128,4096]{1,0:T(8,128)(2,1)S(1)}, bf16[128,4096]{1,0:T(8,128)(2,1)S(1)}, u32[]{:S(2)}, u32[]{:S(2)}) collective-permute-start(bf16[128,4096]{1,0:T(8,128)(2,1)S(1)} %bitcast.280), channel_id=1, source_target_pairs={{0,1},{1,2},{2,3},{3,0},{4,5},{5,6},{6,7},{7,4},{8,9},{9,10},{10,1... | collective-permute-start | bytes 3145736 | tf_op jit(solution)/shard_map/ppermute | solution.py:105
  168.2 12.3 %collective-permute-start.3 = (bf16[64,4096]{1,0:T(8,128)(2,1)S(1)}, bf16[64,4096]{1,0:T(8,128)(2,1)S(1)}, u32[]{:S(2)}, u32[]{:S(2)}) collective-permute-start(bf16[64,4096]{1,0:T(8,128)(2,1)S(1)} %slice.345), channel_id=1, source_target_pairs={{0,3},{1,0},{2,1},{3,2},{4,7},{5,4},{6,5},{7,6},{8,11},{9,8},{10,9... | collective-permute-start | bytes 1572872 | tf_op jit(solution)/shard_map/ppermute | solution.py:109
  171.7 12.0 %collective-permute-start.1 = (bf16[64,4096]{1,0:T(8,128)(2,1)S(1)}, bf16[64,4096]{1,0:T(8,128)(2,1)S(1)}, u32[]{:S(2)}, u32[]{:S(2)}) collective-permute-start(bf16[64,4096]{1,0:T(8,128)(2,1)S(1)} %slice.344), channel_id=1, source_target_pairs={{0,1},{1,2},{2,3},{3,0},{4,5},{5,6},{6,7},{7,4},{8,9},{9,10},{10,1... | collective-permute-start | bytes 1572872 | tf_op jit(solution)/shard_map/ppermute | solution.py:108
  198.0 25.8 %all-to-all-start.2 = ((f32[16,64,128]{2,1,0:T(8,128)}), f32[16,64,128]{2,1,0:T(8,128)S(1)}, u32[]{:S(2)}, u32[]{:S(2)}) async-start(f32[16,64,128]{2,1,0:T(8,128)} %bitcast.106), calls=%async_computation.2 | async-start | bytes 1048576 | tf_op jit(solution)/shard_map/all_to_all | solution.py:122
  (4 other events, 3.0 us)
Sparse Core Ops, SparseCore 0:
  122.3 34.2 all-gather.1

commit v6 on v3

--- a/solution.py
+++ b/solution.py
@@ -98,12 +98,21 @@
     own = panel.shape[0]
     width = panel.shape[1] // n_group
     sliced = panel.reshape(own, n_group, width)
-    right_part = lax.all_to_all(sliced[left_each:], group, split_axis=1, concat_axis=0, tiled=True)
-    right_part = right_part.reshape(n_group * right_each, width)
     left_part = lax.all_to_all(sliced[:left_each], group, split_axis=1, concat_axis=0, tiled=True)
     left_part = left_part.reshape(n_group * left_each, width)
     left_tile = lax.all_gather(left_part, "pblk", axis=0, tiled=True)
-    right_tile = lax.all_gather(right_part, "y", axis=0, tiled=True)
+    left_part, right_sliced = lax.optimization_barrier((left_part, sliced[left_each:]))
+    right_part = lax.all_to_all(right_sliced, group, split_axis=1, concat_axis=0, tiled=True)
+    right_part = right_part.reshape(n_group * right_each, width)
+    up = [(j, (j + 1) % n_y) for j in range(n_y)]
+    down = [(j, (j - 1) % n_y) for j in range(n_y)]
+    from_below = lax.ppermute(right_part, "y", up)
+    from_above = lax.ppermute(right_part, "y", down)
+    half = right_part.shape[0] // 2
+    far_low = lax.ppermute(from_below[:half], "y", up)
+    far_high = lax.ppermute(from_above[half:], "y", down)
+    far = jnp.concatenate([far_low, far_high], 0)
+    right_tile = jnp.stack([far, from_below, right_part, from_above])
     left_tile = left_tile.reshape(n_blk, n_zh * n_core, n_col, left_each, width)
     left_tile = jnp.transpose(left_tile, (1, 2, 0, 3, 4)).reshape(-1, width)
     right_tile = right_tile.reshape(n_y, n_zh, n_core, n_col, right_each, width)
@@ -112,7 +121,10 @@
     chunks = partial_t.reshape(n_col, partial_t.shape[0] // n_col, n_zh * n_core, -1)
     chunks = jnp.transpose(chunks, (2, 0, 1, 3)).reshape(n_group, chunks.shape[1], chunks.shape[3])
     received = lax.all_to_all(chunks, group, split_axis=0, concat_axis=0, tiled=True)
-    return jnp.sum(received, axis=0).T
+    block = jnp.sum(received, axis=0).T
+    block = block.reshape(block.shape[0], n_zh, n_y, n_core * right_each)
+    block = jnp.roll(block, lax.axis_index("y") - 2, axis=2)
+    return block.reshape(block.shape[0], -1)
 
 
 def solution(mesh):

time: 234 us -> 218 us (0.932)
  blocking collectives: 77.7 us -> 55.6 us
  starting transfers between devices: 0.26 us -> 14.6 us
  waiting for transfers between devices: 45.1 us -> 33 us
  other arithmetic: 5.42 us -> 8.47 us
    all_gather x1, waiting for transfers between devices: 45 us -> 0.01 us  [on_device(): left_tile = lax.all_gather(left_part, 'pblk', axis=0, tiled=True)]
    all_to_all x2 -> x1, blocking collectives: 46.3 us -> 20 us  [on_device(): lax.all_to_all(right_sliced, group, split_axis=1, concat_axis=0, tiled=True)]
    ppermute x0 -> x4, waiting for transfers between devices: none -> 18.5 us  [the longest x1 10.9 us: on_device(): from_above = lax.ppermute(right_part, 'y', down)]
    all_to_all x0 -> x1, waiting for transfers between devices: none -> 14.5 us  [on_device(): lax.all_to_all(chunks, group, split_axis=0, concat_axis=0, tiled=True)]
    all_to_all x0 -> x1, starting transfers between devices: none -> 8.24 us  [on_device(): lax.all_to_all(chunks, group, split_axis=0, concat_axis=0, tiled=True)]
    ppermute x0 -> x4, starting transfers between devices: none -> 6.34 us  [the longest x1 3.52 us: on_device(): far_high = lax.ppermute(from_above[half:], 'y', down)]
    all_to_all x1, blocking collectives: 31.3 us -> 35.6 us  [on_device(): lax.all_to_all(sliced[:left_each], group, split_axis=1, concat_axis=0, ti...]
    reshape x1 -> x0, local copies, waits for them, and re-layouts: 2.73 us -> none  [on_device(): right_tile = right_tile.reshape(n_y, n_zh, n_core, n_col, right_each, width)]
  transfers between devices with their start and end apart: 2 -> 6, of which waited for: 2 -> 4; matrix products, arithmetic and copies ran while one was open for 4% -> 4% of each run, Pallas kernels for 0% -> 0%
where the time goes in v6:
time: 218 us; the launch traced here: 216 us
  blocking collectives  55.6 us (26%)
  matrix products  42.4 us (19%)
  waiting for transfers between devices  33 us (15%)
  local copies, waits for them, and re-layouts  32.6 us (15%)
  between operations  29.6 us (14%)
  starting transfers between devices  14.6 us (7%)
  other arithmetic  8.47 us (4%)
    all_to_all x1, blocking collectives, on_device(): lax.all_to_all(sliced[:left_each], group, split_axis=1, concat_axis=0, ti...  35.6 us
    all_to_all x1, blocking collectives, on_device(): lax.all_to_all(right_sliced, group, split_axis=1, concat_axis=0, tiled=True)  20 us
    dot_general x8, matrix products, panels(): jnp.einsum('esk,kt->est', wides[layer], proj_input[assign[layer]], prefer...  16.1 us
    all_to_all x1, waiting for transfers between devices, on_device(): lax.all_to_all(chunks, group, split_axis=0, concat_axis=0, tiled=True)  14.5 us
    ppermute x1, waiting for transfers between devices, on_device(): from_above = lax.ppermute(right_part, 'y', down)  10.9 us
    dot_general x8, matrix products, panels(): jnp.einsum('esc,cr->esr', delta_low, proj_delta[assign[layer]], preferred...  8.42 us
    all_to_all x1, starting transfers between devices, on_device(): lax.all_to_all(chunks, group, split_axis=0, concat_axis=0, tiled=True)  8.24 us
    dot_general x1, matrix products, panels(): jnp.einsum('bjesr,bjest->ebrt', delta_stack, input_stack, precision=lax.P...  5.48 us
  transfers between devices with their start and end apart: 6, of which 4 were waited for; matrix products, arithmetic and copies ran while one was open for 4% of the time, Pallas kernels for 0%

profile of v6, /device:TPU:1, one launch (start us, length us, event | category | flops | bytes accessed | tf_op | source)
XLA Modules:
  0.0 216.2 jit_solution(11929910012097540168)
XLA Ops:
  6.5 1.6 fusion.237
  18.3 0.9 convert_reduce_fusion
  19.2 0.8 copy.51
  20.1 0.8 copy.36
  21.5 2.9 %fusion.238 = (bf16[12,64,256]{2,1,0:T(8,128)(2,1)S(1)}, f32[12,64,256]{2,1,0:T(8,128)S(1)}) fusion(bf16[1024,256]{1,0:T(8,128)(2,1)} %param.10, s32[12,64]{1,0:T(8,128)S(1)} %bitcast.277, s32[12,64]{1,0:T(8,128)S(1)} %bitcast.278, s32[12,64]{1,0:T(8,128)S(1)} %bitcast.279, s32[12,64]{1,0:T(8,128)S(1)} %bitcast.280), kind=kOutput, calls=%fused_computation.272 | convolution fusion | flops 415432704 | bytes 1716224 | tf_op jit(solution)/shard_map/esv,vc->esc/dot_general | solution.py:30
  24.5 0.5 fusion.209
  25.5 0.7 fusion.220
  26.8 0.5 fusion.210
  27.9 0.7 fusion.219
  28.9 0.5 fusion.211
  29.9 0.7 fusion.218
  31.0 0.5 add_convert_fusion
  32.2 0.6 multiply_convert_fusion.6
  32.9 0.5 fusion.95
  34.1 0.5 fusion.98
  35.2 0.5 fusion.102
  37.7 0.5 fusion.110
  38.4 0.6 multiply_convert_fusion.1
  39.0 0.5 fusion.114
  39.7 1.3 multiply_convert_fusion
  41.0 0.7 copy-done.9
  41.8 0.5 fusion.118
  42.3 1.3 fusion.221
  44.3 2.5 %fusion.51 = f32[8,12,64,128]{3,2,1,0:T(8,128)} fusion(bf16[4,768,128]{2,1,0:T(8,128)(2,1)S(1)} %copy-done, s32[]{:T(128)S(6)} %select_n.60, bf16[12,63,256]{2,1,0:T(8,128)(2,1)} %copy-done.54, bf16[12,63,256]{2,1,0:T(8,128)(2,1)} %copy-done.53, bf16[12,64,256]{2,1,0:T(8,128)(2,1)} %copy-done.26), kind=kOutput, calls=%fused_computation.59 | convolution fusion | flops 156893184 | bytes 1757188 | tf_op jit(solution)/shard_map/esk,kt->est/dot_general | solution.py:51
  47.5 2.6 %fusion.50 = f32[8,12,64,128]{3,2,1,0:T(8,128)} fusion(f32[8,12,64,128]{3,2,1,0:T(8,128)} %fusion.51, bf16[4,768,128]{2,1,0:T(8,128)(2,1)S(1)} %copy-done, s32[]{:T(128)S(6)} %select_n.61, bf16[12,63,256]{2,1,0:T(8,128)(2,1)} %copy-done.56, bf16[12,63,256]{2,1,0:T(8,128)(2,1)} %copy-done.55, bf16[12,64,256]{2,1,0:T(8,128)(2,1)} %copy-done.27), kind=kOutput, calls=%fused_computation.57 | convolution fusion | flops 156893184 | bytes 1769476 | tf_op jit(solution)/shard_map/esk,kt->est/dot_general | solution.py:51
  50.1 1.3 fusion.59
  51.4 1.0 fusion.58
  53.0 2.6 %fusion.49 = f32[8,12,64,128]{3,2,1,0:T(8,128)} fusion(f32[8,12,64,128]{3,2,1,0:T(8,128)} %fusion.50, bf16[4,768,128]{2,1,0:T(8,128)(2,1)S(1)} %copy-done, s32[]{:T(128)S(6)} %select_n.62, bf16[12,63,256]{2,1,0:T(8,128)(2,1)} %copy-done.52, bf16[12,63,256]{2,1,0:T(8,128)(2,1)} %copy-done.51, bf16[12,64,256]{2,1,0:T(8,128)(2,1)} %copy-done.25), kind=kOutput, calls=%fused_computation.55 | convolution fusion | flops 156893184 | bytes 1769476 | tf_op jit(solution)/shard_map/esk,kt->est/dot_general | solution.py:51
  55.6 1.0 fusion.57
  57.4 1.2 fusion.48
  58.6 1.0 fusion.56
  60.5 2.4 %fusion.47 = f32[8,12,64,128]{3,2,1,0:T(8,128)} fusion(f32[8,12,64,128]{3,2,1,0:T(8,128)} %fusion.48, bf16[4,768,128]{2,1,0:T(8,128)(2,1)S(1)} %copy-done, s32[]{:T(128)S(6)} %select_n.64, bf16[12,63,256]{2,1,0:T(8,128)(2,1)} %copy-done.46, bf16[12,63,256]{2,1,0:T(8,128)(2,1)S(1)} %copy-done.45, bf16[12,64,256]{2,1,0:T(8,128)(2,1)S(1)} %copy-done.22), kind=kOutput, calls=%fused_computation.51 | convolution fusion | flops 156893184 | bytes 1769476 | tf_op jit(solution)/shard_map/esk,kt->est/dot_general | solution.py:51
  62.8 1.0 fusion.55
  64.5 1.3 fusion.46
  65.7 1.0 fusion.54
  67.4 2.3 %fusion.45 = f32[8,12,64,128]{3,2,1,0:T(8,128)} fusion(f32[8,12,64,128]{3,2,1,0:T(8,128)} %fusion.46, bf16[4,768,128]{2,1,0:T(8,128)(2,1)S(1)} %copy-done, s32[]{:T(128)S(6)} %select_n.66, bf16[12,63,256]{2,1,0:T(8,128)(2,1)} %copy-done.39, bf16[12,63,256]{2,1,0:T(8,128)(2,1)S(1)} %copy-done.38, bf16[12,64,256]{2,1,0:T(8,128)(2,1)S(1)} %copy-done.16), kind=kOutput, calls=%fused_computation.47 | convolution fusion | flops 156893184 | bytes 1769476 | tf_op jit(solution)/shard_map/esk,kt->est/dot_general | solution.py:51
  69.7 1.0 fusion.53
  71.5 1.3 fusion.44
  72.7 1.0 fusion.52
  73.7 4.3 %gather_fusion.1 = f32[8,12,64,128]{3,2,1,0:T(8,128)} fusion(f32[8,12,64,128]{3,2,1,0:T(8,128)} %fusion.44, s32[1024]{0:T(1024)S(1)} %pad_clamp_fusion), kind=kCustom, calls=%fused_computation.1 | custom fusion | bytes 6291488 | tf_op jit(solution)/shard_map/gather | solution.py:75
  78.1 4.3 %gather_fusion = f32[8,12,64,128]{3,2,1,0:T(8,128)} fusion(f32[8,12,64,128]{3,2,1,0:T(8,128)} %fusion.52, s32[1024]{0:T(1024)S(1)} %pad_clamp_fusion), kind=kCustom, calls=%fused_computation | custom fusion | bytes 6291488 | tf_op jit(solution)/shard_map/gather | solution.py:74
  82.3 5.5 %bitcast_convert_fusion = bf16[12,4,128,128]{3,2,1,0:T(8,128)(2,1)S(1)} fusion(f32[4,2,12,64,128]{4,3,2,1,0:T(8,128)} %bitcast.267, f32[4,2,12,64,128]{4,3,2,1,0:T(8,128)} %bitcast.268), kind=kOutput, calls=%fused_computation.2 | convolution fusion | flops 604766208 | bytes 7864320 | tf_op jit(solution)/shard_map/bjesr,bjest->ebrt/dot_general | solution.py:79
  87.8 1.0 slice.342
  88.9 1.5 slice.292
  90.4 0.6 copy.44
  91.0 35.6 %all_to_all.35 = bf16[8,16,4096]{2,0,1:T(8,128)(2,1)} all-to-all(bf16[8,16,4096]{2,0,1:T(8,128)(2,1)S(1)} %copy.44), channel_id=1, replica_groups=mesh['zh'=2,'y'=4,'core'=2,'col'=4,'pblk'=4] {'zh','core','col'}, dimensions={1} | all-to-all | bytes 2097152 | tf_op jit(solution)/shard_map/all_to_all | solution.py:101
  127.3 20.0 %all_to_all.36 = bf16[4,16,4096]{2,0,1:T(4,128)(2,1)S(1)} all-to-all(bf16[4,16,4096]{2,0,1:T(4,128)(2,1)S(1)} %copy.45), channel_id=1, replica_groups=mesh['zh'=2,'y'=4,'core'=2,'col'=4,'pblk'=4] {'zh','core','col'}, dimensions={1} | all-to-all | bytes 1048576 | tf_op jit(solution)/shard_map/all_to_all | solution.py:105
  147.4 2.8 %collective-permute-start.2 = (bf16[64,4096]{1,0:T(8,128)(2,1)S(1)}, bf16[64,4096]{1,0:T(8,128)(2,1)S(1)}, u32[]{:S(2)}, u32[]{:S(2)}) collective-permute-start(bf16[64,4096]{1,0:T(8,128)(2,1)S(1)} %reshape.80), channel_id=1, source_target_pairs={{0,96},{32,0},{64,32},{96,64},{1,97},{33,1},{65,33},{97,65},{2,98}... | collective-permute-start | bytes 1572872 | tf_op jit(solution)/shard_map/ppermute | solution.py:110
  150.2 10.9 %collective-permute-done.2 = bf16[64,4096]{1,0:T(8,128)(2,1)S(1)} collective-permute-done((bf16[64,4096]{1,0:T(8,128)(2,1)S(1)}, bf16[64,4096]{1,0:T(8,128)(2,1)S(1)}, u32[]{:S(2)}, u32[]{:S(2)}) %collective-permute-start.2) | collective-permute-done | bytes 524320 | tf_op jit(solution)/shard_map/ppermute | solution.py:110
  161.1 0.7 slice.345
  161.8 3.5 %collective-permute-start.3 = (bf16[32,4096]{1,0:T(8,128)(2,1)}, bf16[32,4096]{1,0:T(8,128)(2,1)}, u32[]{:S(2)}, u32[]{:S(2)}) collective-permute-start(bf16[32,4096]{1,0:T(8,128)(2,1)} %slice.345), channel_id=1, source_target_pairs={{0,96},{32,0},{64,32},{96,64},{1,97},{33,1},{65,33},{97,65},{2,98}... | collective-permute-start | bytes 786440 | tf_op jit(solution)/shard_map/ppermute | solution.py:113
  165.3 0.7 slice.344
  166.4 3.7 %collective-permute-done.3 = bf16[32,4096]{1,0:T(8,128)(2,1)} collective-permute-done((bf16[32,4096]{1,0:T(8,128)(2,1)}, bf16[32,4096]{1,0:T(8,128)(2,1)}, u32[]{:S(2)}, u32[]{:S(2)}) %collective-permute-start.3) | collective-permute-done | bytes 262176 | tf_op jit(solution)/shard_map/ppermute | solution.py:113
  170.2 3.8 %collective-permute-done.1 = bf16[32,4096]{1,0:T(8,128)(2,1)} collective-permute-done((bf16[32,4096]{1,0:T(8,128)(2,1)}, bf16[32,4096]{1,0:T(8,128)(2,1)}, u32[]{:S(2)}, u32[]{:S(2)}) %collective-permute-start.1) | collective-permute-done | bytes 262176 | tf_op jit(solution)/shard_map/ppermute | solution.py:112
  174.0 1.1 pad_maximum_fusion
  175.3 2.0 maximum_bitcast_fusion
  177.3 1.6 copy.46
  178.8 2.2 %reshape.127 = bf16[4,64,4096,1]{2,1,0,3:T(8,128)(2,1)} reshape(bf16[4,2,4,2,4,4096]{5,4,3,2,1,0:T(4,128)(2,1)S(1)} %copy.46) | data formatting | bytes 4194304 | tf_op jit(solution)/shard_map/rk,lk->rl/dot_general | solution.py:120
  181.0 2.6 %copy.47 = bf16[4,4,4,8,4096]{4,3,2,1,0:T(8,128)(2,1)S(1)} copy(bf16[4,4,4,8,4096]{4,3,1,0,2:T(8,128)(2,1)} %bitcast.271) | data formatting | bytes 8388608 | tf_op jit(solution)/shard_map/transpose | solution.py:117
  183.8 1.3 fusion.41
  185.1 0.8 copy.48
  186.0 8.2 %all-to-all-start.2 = ((f32[16,64,128]{2,1,0:T(8,128)}), f32[16,64,128]{2,1,0:T(8,128)S(1)}, u32[]{:S(2)}, u32[]{:S(2)}) async-start(f32[16,64,128]{2,1,0:T(8,128)} %bitcast.101), calls=%async_computation.2 | async-start | bytes 1048576 | tf_op jit(solution)/shard_map/all_to_all | solution.py:123
  194.2 14.5 %all-to-all-done.2 = f32[16,64,128]{2,1,0:T(8,128)S(1)} async-done(((f32[16,64,128]{2,1,0:T(8,128)}), f32[16,64,128]{2,1,0:T(8,128)S(1)}, u32[]{:S(2)}, u32[]{:S(2)}) %all-to-all-start.2) | async-done | bytes 524320 | tf_op jit(solution)/shard_map/all_to_all | solution.py:123
  208.7 0.6 fusion.172
  (166 shorter events, 9.5 us)
Async XLA Ops:
  6.5 37.7 %copy-start = (bf16[4,768,128]{2,1,0:T(8,128)(2,1)S(1)}, bf16[4,768,128]{2,1,0:T(8,128)(2,1)}, u32[]{:S(2)}) copy-start(bf16[4,768,128]{2,1,0:T(8,128)(2,1)} %param.15) | copy-start | bytes 2359300
  6.5 174.4 %all-gather.2.cloned.1.call-start = ((), (), s32[]{:S(2)}) async-start(), calls=%async_computation.3 | async-start | bytes 5242880 | tf_op jit(solution)/shard_map/all_gather | solution.py:103
  21.4 3.1 %copy-start.11 = (bf16[8,768,256]{2,1,0:T(8,128)(2,1)S(1)}, bf16[8,768,256]{2,1,0:T(8,128)(2,1)}, u32[]{:S(2)}) copy-start(bf16[8,768,256]{2,1,0:T(8,128)(2,1)} %param.11) | copy-start | bytes 9437188
  24.3 0.8 copy-start.26
  24.5 0.8 copy-start.53
  24.5 0.9 copy-start.54
  25.4 0.8 copy-start.27
  25.4 1.0 copy-start.59
  25.5 1.0 copy-start.55
  25.5 1.1 copy-start.56
  26.7 0.8 copy-start.25
  26.8 0.8 copy-start.51
  26.8 0.9 copy-start.52
  27.7 0.8 copy-start.23
  27.8 0.9 copy-start.49
  28.7 0.8 copy-start.21
  28.9 0.8 copy-start.44
  28.9 0.9 copy-start.46
  29.8 0.8 copy-start.17
  29.9 0.8 copy-start.40
  29.9 0.9 copy-start.42
  30.8 0.8 copy-start.15
  31.0 0.8 copy-start.37
  31.0 0.9 copy-start.39
  31.0 1.0 copy-start.57
  31.0 1.2 copy-start.58
  31.9 0.9 copy-start.13
  32.0 0.8 copy-start.33
  32.0 0.9 copy-start.35
  35.2 0.8 copy-start.1
  36.5 0.8 copy-start.3
  37.6 0.8 copy-start.5
  41.0 0.7 copy-start.9
  47.4 2.7 %copy-start.28 = (bf16[4,256,128]{2,1,0:T(8,128)(2,1)S(1)}, bf16[4,256,128]{2,1,0:T(8,128)(2,1)}, u32[]{:S(2)}) copy-start(bf16[4,256,128]{2,1,0:T(8,128)(2,1)} %param.14) | copy-start | bytes 786436
  47.4 2.7 %copy-start.30 = (f32[12,64,256]{2,1,0:T(8,128)S(1)}, f32[12,64,256]{2,1,0:T(8,128)}, u32[]{:S(2)}) copy-start(f32[12,64,256]{2,1,0:T(8,128)} %get-tuple-element.8) | copy-start | bytes 2359300
  47.4 2.7 %copy-start.31 = (f32[12,63,256]{2,1,0:T(8,128)S(1)}, f32[12,63,256]{2,1,0:T(8,128)}, u32[]{:S(2)}) copy-start(f32[12,63,256]{2,1,0:T(8,128)} %get-tuple-element.25) | copy-start | bytes 2322436
  47.4 2.6 %copy-start.32 = (f32[12,63,256]{2,1,0:T(8,128)S(1)}, f32[12,63,256]{2,1,0:T(8,128)}, u32[]{:S(2)}) copy-start(f32[12,63,256]{2,1,0:T(8,128)} %get-tuple-element.26) | copy-start | bytes 2322436
  47.5 2.6 %copy-start.60 = (f32[12,64,256]{2,1,0:T(8,128)S(1)}, f32[12,64,256]{2,1,0:T(8,128)}, u32[]{:S(2)}) copy-start(f32[12,64,256]{2,1,0:T(8,128)} %copy-done.59) | copy-start | bytes 2359300
  50.1 1.3 copy-start.10
  53.0 2.6 %copy-start.8 = (bf16[12,64,256]{2,1,0:T(8,128)(2,1)S(1)}, bf16[12,64,256]{2,1,0:T(8,128)(2,1)}, u32[]{:S(2)}) copy-start(bf16[12,64,256]{2,1,0:T(8,128)(2,1)} %copy-done.7) | copy-start | bytes 1179652
  53.0 2.6 %copy-start.29 = (bf16[4,256,128]{2,1,0:T(8,128)(2,1)S(1)}, bf16[4,256,128]{2,1,0:T(8,128)(2,1)}, u32[]{:S(2)}) copy-start(bf16[4,256,128]{2,1,0:T(8,128)(2,1)} %param.14) | copy-start | bytes 786436
  53.0 4.3 %copy-start.24 = (bf16[12,64,256]{2,1,0:T(8,128)(2,1)S(1)}, bf16[12,64,256]{2,1,0:T(8,128)(2,1)}, u32[]{:S(2)}) copy-start(bf16[12,64,256]{2,1,0:T(8,128)(2,1)} %copy-done.23) | copy-start | bytes 1179652
  53.0 4.3 %copy-start.48 = (bf16[12,63,256]{2,1,0:T(8,128)(2,1)S(1)}, bf16[12,63,256]{2,1,0:T(8,128)(2,1)}, u32[]{:S(2)}) copy-start(bf16[12,63,256]{2,1,0:T(8,128)(2,1)} %copy-done.47) | copy-start | bytes 1161220
  53.0 4.3 %copy-start.50 = (bf16[12,63,256]{2,1,0:T(8,128)(2,1)S(1)}, bf16[12,63,256]{2,1,0:T(8,128)(2,1)}, u32[]{:S(2)}) copy-start(bf16[12,63,256]{2,1,0:T(8,128)(2,1)} %copy-done.49) | copy-start | bytes 1161220
  57.4 1.3 copy-start.6
  57.4 3.0 %copy-start.22 = (bf16[12,64,256]{2,1,0:T(8,128)(2,1)S(1)}, bf16[12,64,256]{2,1,0:T(8,128)(2,1)}, u32[]{:S(2)}) copy-start(bf16[12,64,256]{2,1,0:T(8,128)(2,1)} %copy-done.21) | copy-start | bytes 1179652
  57.4 3.0 %copy-start.45 = (bf16[12,63,256]{2,1,0:T(8,128)(2,1)S(1)}, bf16[12,63,256]{2,1,0:T(8,128)(2,1)}, u32[]{:S(2)}) copy-start(bf16[12,63,256]{2,1,0:T(8,128)(2,1)} %copy-done.44) | copy-start | bytes 1161220
  60.4 2.4 %copy-start.4 = (bf16[12,64,256]{2,1,0:T(8,128)(2,1)S(1)}, bf16[12,64,256]{2,1,0:T(8,128)(2,1)}, u32[]{:S(2)}) copy-start(bf16[12,64,256]{2,1,0:T(8,128)(2,1)} %copy-done.3) | copy-start | bytes 1179652
  60.4 4.0 %copy-start.18 = (bf16[12,64,256]{2,1,0:T(8,128)(2,1)S(1)}, bf16[12,64,256]{2,1,0:T(8,128)(2,1)}, u32[]{:S(2)}) copy-start(bf16[12,64,256]{2,1,0:T(8,128)(2,1)} %copy-done.17) | copy-start | bytes 1179652
  60.4 4.0 %copy-start.41 = (bf16[12,63,256]{2,1,0:T(8,128)(2,1)S(1)}, bf16[12,63,256]{2,1,0:T(8,128)(2,1)}, u32[]{:S(2)}) copy-start(bf16[12,63,256]{2,1,0:T(8,128)(2,1)} %copy-done.40) | copy-start | bytes 1161220
  60.4 4.0 %copy-start.43 = (bf16[12,63,256]{2,1,0:T(8,128)(2,1)S(1)}, bf16[12,63,256]{2,1,0:T(8,128)(2,1)}, u32[]{:S(2)}) copy-start(bf16[12,63,256]{2,1,0:T(8,128)(2,1)} %copy-done.42) | copy-start | bytes 1161220
  64.4 1.3 copy-start.2
  64.4 2.9 %copy-start.16 = (bf16[12,64,256]{2,1,0:T(8,128)(2,1)S(1)}, bf16[12,64,256]{2,1,0:T(8,128)(2,1)}, u32[]{:S(2)}) copy-start(bf16[12,64,256]{2,1,0:T(8,128)(2,1)} %copy-done.15) | copy-start | bytes 1179652
  64.4 2.9 %copy-start.38 = (bf16[12,63,256]{2,1,0:T(8,128)(2,1)S(1)}, bf16[12,63,256]{2,1,0:T(8,128)(2,1)}, u32[]{:S(2)}) copy-start(bf16[12,63,256]{2,1,0:T(8,128)(2,1)} %copy-done.37) | copy-start | bytes 1161220
  67.4 4.0 %copy-start.14 = (bf16[12,64,256]{2,1,0:T(8,128)(2,1)S(1)}, bf16[12,64,256]{2,1,0:T(8,128)(2,1)}, u32[]{:S(2)}) copy-start(bf16[12,64,256]{2,1,0:T(8,128)(2,1)} %copy-done.13) | copy-start | bytes 1179652
  67.4 4.0 %copy-start.34 = (bf16[12,63,256]{2,1,0:T(8,128)(2,1)S(1)}, bf16[12,63,256]{2,1,0:T(8,128)(2,1)}, u32[]{:S(2)}) copy-start(bf16[12,63,256]{2,1,0:T(8,128)(2,1)} %copy-done.33) | copy-start | bytes 1161220
  67.4 4.0 %copy-start.36 = (bf16[12,63,256]{2,1,0:T(8,128)(2,1)S(1)}, bf16[12,63,256]{2,1,0:T(8,128)(2,1)}, u32[]{:S(2)}) copy-start(bf16[12,63,256]{2,1,0:T(8,128)(2,1)} %copy-done.35) | copy-start | bytes 1161220
  71.5 1.3 copy-start.20
  147.4 13.7 %collective-permute-start.2 = (bf16[64,4096]{1,0:T(8,128)(2,1)S(1)}, bf16[64,4096]{1,0:T(8,128)(2,1)S(1)}, u32[]{:S(2)}, u32[]{:S(2)}) collective-permute-start(bf16[64,4096]{1,0:T(8,128)(2,1)S(1)} %reshape.80), channel_id=1, source_target_pairs={{0,96},{32,0},{64,32},{96,64},{1,97},{33,1},{65,33},{97,65},{2,98}... | collective-permute-start | bytes 1572872 | tf_op jit(solution)/shard_map/ppermute | solution.py:110
  150.2 15.2 %collective-permute-start = (bf16[64,4096]{1,0:T(8,128)(2,1)S(1)}, bf16[64,4096]{1,0:T(8,128)(2,1)S(1)}, u32[]{:S(2)}, u32[]{:S(2)}) collective-permute-start(bf16[64,4096]{1,0:T(8,128)(2,1)S(1)} %reshape.80), channel_id=1, source_target_pairs={{0,32},{32,64},{64,96},{96,0},{1,33},{33,65},{65,97},{97,1},{2,34}... | collective-permute-start | bytes 1572872 | tf_op jit(solution)/shard_map/ppermute | solution.py:109
  161.8 8.4 %collective-permute-start.3 = (bf16[32,4096]{1,0:T(8,128)(2,1)}, bf16[32,4096]{1,0:T(8,128)(2,1)}, u32[]{:S(2)}, u32[]{:S(2)}) collective-permute-start(bf16[32,4096]{1,0:T(8,128)(2,1)} %slice.345), channel_id=1, source_target_pairs={{0,96},{32,0},{64,32},{96,64},{1,97},{33,1},{65,33},{97,65},{2,98}... | collective-permute-start | bytes 786440 | tf_op jit(solution)/shard_map/ppermute | solution.py:113
  166.0 8.0 %collective-permute-start.1 = (bf16[32,4096]{1,0:T(8,128)(2,1)}, bf16[32,4096]{1,0:T(8,128)(2,1)}, u32[]{:S(2)}, u32[]{:S(2)}) collective-permute-start(bf16[32,4096]{1,0:T(8,128)(2,1)} %slice.344), channel_id=1, source_target_pairs={{0,32},{32,64},{64,96},{96,0},{1,33},{33,65},{65,97},{97,1},{2,34}... | collective-permute-start | bytes 786440 | tf_op jit(solution)/shard_map/ppermute | solution.py:112
  181.0 2.9 %copy-start.12 = (bf16[4,64,4096,1]{2,1,0,3:T(8,128)(2,1)S(1)}, bf16[4,64,4096,1]{2,1,0,3:T(8,128)(2,1)}, u32[]{:S(2)}) copy-start(bf16[4,64,4096,1]{2,1,0,3:T(8,128)(2,1)} %reshape.127) | copy-start | bytes 6291460
  186.0 22.7 %all-to-all-start.2 = ((f32[16,64,128]{2,1,0:T(8,128)}), f32[16,64,128]{2,1,0:T(8,128)S(1)}, u32[]{:S(2)}, u32[]{:S(2)}) async-start(f32[16,64,128]{2,1,0:T(8,128)} %bitcast.101), calls=%async_computation.2 | async-start | bytes 1048576 | tf_op jit(solution)/shard_map/all_to_all | solution.py:123
  (3 other events, 2.2 us)
Sparse Core Ops, SparseCore 0:
  126.7 50.0 all-gather.1

commit v7 on v6

--- a/solution.py
+++ b/solution.py
@@ -82,6 +82,18 @@
     return panel.reshape(examples, blocks_here * PR * PS).astype(jnp.bfloat16)
 
 
+def spread(sliced):
+    rows, _, width = sliced.shape
+    n_core = lax.axis_size("core")
+    ring = lax.axis_size(("zh", "col"))
+    pair = lax.all_to_all(
+        sliced.reshape(rows, n_core, ring, width), "core", split_axis=1, concat_axis=0, tiled=True
+    )
+    pair = pair.reshape(n_core * rows, ring, width)
+    out = lax.all_to_all(pair, ("zh", "col"), split_axis=1, concat_axis=0, tiled=True)
+    return out.reshape(ring * n_core * rows, width)
+
+
 def on_device(left_feat, right_feat, embed, conv_w, head, assign, proj_delta, proj_input):
     group = ("zh", "core", "col")
     n_group = lax.axis_size(group)
@@ -98,12 +110,10 @@
     own = panel.shape[0]
     width = panel.shape[1] // n_group
     sliced = panel.reshape(own, n_group, width)
-    left_part = lax.all_to_all(sliced[:left_each], group, split_axis=1, concat_axis=0, tiled=True)
-    left_part = left_part.reshape(n_group * left_each, width)
+    left_part = spread(sliced[:left_each])
     left_tile = lax.all_gather(left_part, "pblk", axis=0, tiled=True)
     left_part, right_sliced = lax.optimization_barrier((left_part, sliced[left_each:]))
-    right_part = lax.all_to_all(right_sliced, group, split_axis=1, concat_axis=0, tiled=True)
-    right_part = right_part.reshape(n_group * right_each, width)
+    right_part = spread(right_sliced)
     up = [(j, (j + 1) % n_y) for j in range(n_y)]
     down = [(j, (j - 1) % n_y) for j in range(n_y)]
     from_below = lax.ppermute(right_part, "y", up)
@@ -113,10 +123,10 @@
     far_high = lax.ppermute(from_above[half:], "y", down)
     far = jnp.concatenate([far_low, far_high], 0)
     right_tile = jnp.stack([far, from_below, right_part, from_above])
-    left_tile = left_tile.reshape(n_blk, n_zh * n_core, n_col, left_each, width)
-    left_tile = jnp.transpose(left_tile, (1, 2, 0, 3, 4)).reshape(-1, width)
-    right_tile = right_tile.reshape(n_y, n_zh, n_core, n_col, right_each, width)
-    right_tile = jnp.transpose(right_tile, (3, 1, 0, 2, 4, 5)).reshape(-1, width)
+    left_tile = left_tile.reshape(n_blk, n_zh, n_col, n_core, left_each, width)
+    left_tile = jnp.transpose(left_tile, (1, 3, 2, 0, 4, 5)).reshape(-1, width)
+    right_tile = right_tile.reshape(n_y, n_zh, n_col, n_core, right_each, width)
+    right_tile = jnp.transpose(right_tile, (2, 1, 0, 3, 4, 5)).reshape(-1, width)
     partial_t = jnp.einsum("rk,lk->rl", right_tile, left_tile, preferred_element_type=jnp.float32)
     chunks = partial_t.reshape(n_col, partial_t.shape[0] // n_col, n_zh * n_core, -1)
     chunks = jnp.transpose(chunks, (2, 0, 1, 3)).reshape(n_group, chunks.shape[1], chunks.shape[3])

time: 218 us -> 227 us (1.041)
  blocking collectives: 55.6 us -> 67.7 us
  starting transfers between devices: 14.6 us -> 12 us
    all_to_all x2 -> x4, blocking collectives: 55.6 us -> 67.7 us  [the longest x2 54.7 us: spread(): lax.all_to_all(pair, ('zh', 'col'), split_axis=1, concat_axis=0, tiled=True)]
    all_to_all x1, starting transfers between devices: 8.24 us -> 5.74 us  [on_device(): lax.all_to_all(chunks, group, split_axis=0, concat_axis=0, tiled=True)]
    reshape x1 -> x5, local copies, waits for them, and re-layouts: 0.12 us -> 2.52 us  [the longest x3 1.64 us: spread(): sliced.reshape(rows, n_core, ring, width)]
where the time goes in v7:
time: 227 us; the launch traced here: 226 us
  blocking collectives  67.7 us (30%)
  matrix products  42.4 us (19%)
  local copies, waits for them, and re-layouts  32.7 us (14%)
  waiting for transfers between devices  32.7 us (14%)
  between operations  29.6 us (13%)
  starting transfers between devices  12 us (5%)
  other arithmetic  8.47 us (4%)
    all_to_all x2, blocking collectives, spread(): lax.all_to_all(pair, ('zh', 'col'), split_axis=1, concat_axis=0, tiled=True)  54.7 us
    dot_general x8, matrix products, panels(): jnp.einsum('esk,kt->est', wides[layer], proj_input[assign[layer]], prefer...  16.1 us
    all_to_all x1, waiting for transfers between devices, on_device(): lax.all_to_all(chunks, group, split_axis=0, concat_axis=0, tiled=True)  14.6 us
    all_to_all x2, blocking collectives, spread(): lax.all_to_all(sliced.reshape(rows, n_core, ring, width), 'core', split_a...  13 us
    ppermute x1, waiting for transfers between devices, on_device(): from_above = lax.ppermute(right_part, 'y', down)  10.8 us
    dot_general x8, matrix products, panels(): jnp.einsum('esc,cr->esr', delta_low, proj_delta[assign[layer]], preferred...  8.42 us
    all_to_all x1, starting transfers between devices, on_device(): lax.all_to_all(chunks, group, split_axis=0, concat_axis=0, tiled=True)  5.74 us
    dot_general x1, matrix products, panels(): jnp.einsum('bjesr,bjest->ebrt', delta_stack, input_stack, precision=lax.P...  5.48 us
  transfers between devices with their start and end apart: 6, of which 4 were waited for; matrix products, arithmetic and copies ran while one was open for 4% of the time, Pallas kernels for 0%

profile of v7, /device:TPU:1, one launch (start us, length us, event | category | flops | bytes accessed | tf_op | source)
XLA Modules:
  0.0 225.6 jit_solution(8087751025236815954)
XLA Ops:
  6.5 1.6 fusion.237
  18.3 0.9 convert_reduce_fusion
  19.2 0.8 copy.72
  20.1 0.8 copy.55
  21.5 2.9 %fusion.238 = (bf16[12,64,256]{2,1,0:T(8,128)(2,1)S(1)}, f32[12,64,256]{2,1,0:T(8,128)S(1)}) fusion(bf16[1024,256]{1,0:T(8,128)(2,1)} %param.10, s32[12,64]{1,0:T(8,128)S(1)} %bitcast.294, s32[12,64]{1,0:T(8,128)S(1)} %bitcast.295, s32[12,64]{1,0:T(8,128)S(1)} %bitcast.296, s32[12,64]{1,0:T(8,128)S(1)} %bitcast.297), kind=kOutput, calls=%fused_computation.272 | convolution fusion | flops 415432704 | bytes 1716224 | tf_op jit(solution)/shard_map/esv,vc->esc/dot_general | solution.py:30
  24.5 0.5 fusion.209
  25.5 0.7 fusion.220
  26.8 0.5 fusion.210
  27.9 0.7 fusion.219
  28.9 0.5 fusion.211
  29.9 0.7 fusion.218
  31.0 0.5 add_convert_fusion
  32.2 0.6 multiply_convert_fusion.6
  34.1 0.5 fusion.98
  35.2 0.5 fusion.102
  38.4 0.6 multiply_convert_fusion.1
  39.0 0.5 fusion.114
  39.7 1.3 multiply_convert_fusion
  41.0 0.7 copy-done.9
  41.8 0.5 fusion.118
  42.3 1.3 fusion.221
  44.3 2.5 %fusion.51 = f32[8,12,64,128]{3,2,1,0:T(8,128)} fusion(bf16[4,768,128]{2,1,0:T(8,128)(2,1)S(1)} %copy-done, s32[]{:T(128)S(6)} %select_n.60, bf16[12,63,256]{2,1,0:T(8,128)(2,1)} %copy-done.54, bf16[12,63,256]{2,1,0:T(8,128)(2,1)} %copy-done.53, bf16[12,64,256]{2,1,0:T(8,128)(2,1)} %copy-done.26), kind=kOutput, calls=%fused_computation.59 | convolution fusion | flops 156893184 | bytes 1757188 | tf_op jit(solution)/shard_map/esk,kt->est/dot_general | solution.py:51
  47.5 2.6 %fusion.50 = f32[8,12,64,128]{3,2,1,0:T(8,128)} fusion(f32[8,12,64,128]{3,2,1,0:T(8,128)} %fusion.51, bf16[4,768,128]{2,1,0:T(8,128)(2,1)S(1)} %copy-done, s32[]{:T(128)S(6)} %select_n.61, bf16[12,63,256]{2,1,0:T(8,128)(2,1)} %copy-done.56, bf16[12,63,256]{2,1,0:T(8,128)(2,1)} %copy-done.55, bf16[12,64,256]{2,1,0:T(8,128)(2,1)} %copy-done.27), kind=kOutput, calls=%fused_computation.57 | convolution fusion | flops 156893184 | bytes 1769476 | tf_op jit(solution)/shard_map/esk,kt->est/dot_general | solution.py:51
  50.1 1.3 fusion.59
  51.4 1.0 fusion.58
  53.0 2.6 %fusion.49 = f32[8,12,64,128]{3,2,1,0:T(8,128)} fusion(f32[8,12,64,128]{3,2,1,0:T(8,128)} %fusion.50, bf16[4,768,128]{2,1,0:T(8,128)(2,1)S(1)} %copy-done, s32[]{:T(128)S(6)} %select_n.62, bf16[12,63,256]{2,1,0:T(8,128)(2,1)} %copy-done.52, bf16[12,63,256]{2,1,0:T(8,128)(2,1)} %copy-done.51, bf16[12,64,256]{2,1,0:T(8,128)(2,1)} %copy-done.25), kind=kOutput, calls=%fused_computation.55 | convolution fusion | flops 156893184 | bytes 1769476 | tf_op jit(solution)/shard_map/esk,kt->est/dot_general | solution.py:51
  55.6 1.0 fusion.57
  57.4 1.2 fusion.48
  58.6 1.0 fusion.56
  60.5 2.4 %fusion.47 = f32[8,12,64,128]{3,2,1,0:T(8,128)} fusion(f32[8,12,64,128]{3,2,1,0:T(8,128)} %fusion.48, bf16[4,768,128]{2,1,0:T(8,128)(2,1)S(1)} %copy-done, s32[]{:T(128)S(6)} %select_n.64, bf16[12,63,256]{2,1,0:T(8,128)(2,1)} %copy-done.46, bf16[12,63,256]{2,1,0:T(8,128)(2,1)S(1)} %copy-done.45, bf16[12,64,256]{2,1,0:T(8,128)(2,1)S(1)} %copy-done.22), kind=kOutput, calls=%fused_computation.51 | convolution fusion | flops 156893184 | bytes 1769476 | tf_op jit(solution)/shard_map/esk,kt->est/dot_general | solution.py:51
  62.8 1.0 fusion.55
  64.5 1.3 fusion.46
  65.7 1.0 fusion.54
  67.4 2.3 %fusion.45 = f32[8,12,64,128]{3,2,1,0:T(8,128)} fusion(f32[8,12,64,128]{3,2,1,0:T(8,128)} %fusion.46, bf16[4,768,128]{2,1,0:T(8,128)(2,1)S(1)} %copy-done, s32[]{:T(128)S(6)} %select_n.66, bf16[12,63,256]{2,1,0:T(8,128)(2,1)} %copy-done.39, bf16[12,63,256]{2,1,0:T(8,128)(2,1)S(1)} %copy-done.38, bf16[12,64,256]{2,1,0:T(8,128)(2,1)S(1)} %copy-done.16), kind=kOutput, calls=%fused_computation.47 | convolution fusion | flops 156893184 | bytes 1769476 | tf_op jit(solution)/shard_map/esk,kt->est/dot_general | solution.py:51
  69.7 1.0 fusion.53
  71.5 1.3 fusion.44
  72.7 1.0 fusion.52
  73.7 4.3 %gather_fusion.1 = f32[8,12,64,128]{3,2,1,0:T(8,128)} fusion(f32[8,12,64,128]{3,2,1,0:T(8,128)} %fusion.44, s32[1024]{0:T(1024)S(1)} %pad_clamp_fusion), kind=kCustom, calls=%fused_computation.1 | custom fusion | bytes 6291488 | tf_op jit(solution)/shard_map/gather | solution.py:75
  78.1 4.3 %gather_fusion = f32[8,12,64,128]{3,2,1,0:T(8,128)} fusion(f32[8,12,64,128]{3,2,1,0:T(8,128)} %fusion.52, s32[1024]{0:T(1024)S(1)} %pad_clamp_fusion), kind=kCustom, calls=%fused_computation | custom fusion | bytes 6291488 | tf_op jit(solution)/shard_map/gather | solution.py:74
  82.3 5.5 %bitcast_convert_fusion = bf16[12,4,128,128]{3,2,1,0:T(8,128)(2,1)S(1)} fusion(f32[4,2,12,64,128]{4,3,2,1,0:T(8,128)} %bitcast.280, f32[4,2,12,64,128]{4,3,2,1,0:T(8,128)} %bitcast.281), kind=kOutput, calls=%fused_computation.2 | convolution fusion | flops 604766208 | bytes 7864320 | tf_op jit(solution)/shard_map/bjesr,bjest->ebrt/dot_general | solution.py:79
  87.8 1.0 slice.339
  88.9 1.5 reshape.94
  90.5 7.4 %all_to_all.65 = bf16[8,2,8,4096]{3,2,0,1:T(8,128)(2,1)S(1)} all-to-all(bf16[8,2,8,4096]{3,2,0,1:T(8,128)(2,1)S(1)} %copy.63), channel_id=1, replica_groups=mesh['zh'=2,'y'=4,'core'=2,'col'=4,'pblk'=4] {'core'}, dimensions={1} | all-to-all | bytes 2097152 | tf_op jit(solution)/shard_map/all_to_all | solution.py:89
  97.9 0.6 copy.64
  98.5 34.3 %all_to_all.66 = bf16[16,8,4096]{2,0,1:T(8,128)(2,1)} all-to-all(bf16[16,8,4096]{2,0,1:T(8,128)(2,1)S(1)} %copy.64), channel_id=1, replica_groups=mesh['zh'=2,'y'=4,'core'=2,'col'=4,'pblk'=4] {'zh','col'}, dimensions={1} | all-to-all | bytes 2097152 | tf_op jit(solution)/shard_map/all_to_all | solution.py:93
  133.1 5.6 %all_to_all.67 = bf16[4,2,8,4096]{3,2,0,1:T(8,128)(2,1)S(1)} all-to-all(bf16[4,2,8,4096]{3,2,0,1:T(8,128)(2,1)S(1)} %copy.65), channel_id=1, replica_groups=mesh['zh'=2,'y'=4,'core'=2,'col'=4,'pblk'=4] {'core'}, dimensions={1} | all-to-all | bytes 1048576 | tf_op jit(solution)/shard_map/all_to_all | solution.py:89
  139.0 20.4 %all_to_all.68 = bf16[8,8,4096]{2,0,1:T(8,128)(2,1)S(1)} all-to-all(bf16[8,8,4096]{2,0,1:T(8,128)(2,1)S(1)} %copy.66), channel_id=1, replica_groups=mesh['zh'=2,'y'=4,'core'=2,'col'=4,'pblk'=4] {'zh','col'}, dimensions={1} | all-to-all | bytes 1048576 | tf_op jit(solution)/shard_map/all_to_all | solution.py:93
  159.4 2.7 %collective-permute-start.2 = (bf16[64,4096]{1,0:T(8,128)(2,1)S(1)}, bf16[64,4096]{1,0:T(8,128)(2,1)S(1)}, u32[]{:S(2)}, u32[]{:S(2)}) collective-permute-start(bf16[64,4096]{1,0:T(8,128)(2,1)S(1)} %bitcast.286), channel_id=1, source_target_pairs={{0,96},{32,0},{64,32},{96,64},{1,97},{33,1},{65,33},{97,65},{2,98}... | collective-permute-start | bytes 1572872 | tf_op jit(solution)/shard_map/ppermute | solution.py:120
  162.2 10.8 %collective-permute-done.2 = bf16[64,4096]{1,0:T(8,128)(2,1)S(1)} collective-permute-done((bf16[64,4096]{1,0:T(8,128)(2,1)S(1)}, bf16[64,4096]{1,0:T(8,128)(2,1)S(1)}, u32[]{:S(2)}, u32[]{:S(2)}) %collective-permute-start.2) | collective-permute-done | bytes 524320 | tf_op jit(solution)/shard_map/ppermute | solution.py:120
  173.0 0.7 slice.342
  173.7 3.5 %collective-permute-start.3 = (bf16[32,4096]{1,0:T(8,128)(2,1)}, bf16[32,4096]{1,0:T(8,128)(2,1)}, u32[]{:S(2)}, u32[]{:S(2)}) collective-permute-start(bf16[32,4096]{1,0:T(8,128)(2,1)} %slice.342), channel_id=1, source_target_pairs={{0,96},{32,0},{64,32},{96,64},{1,97},{33,1},{65,33},{97,65},{2,98}... | collective-permute-start | bytes 786440 | tf_op jit(solution)/shard_map/ppermute | solution.py:123
  177.2 0.7 slice.341
  178.5 3.5 %collective-permute-done.3 = bf16[32,4096]{1,0:T(8,128)(2,1)} collective-permute-done((bf16[32,4096]{1,0:T(8,128)(2,1)}, bf16[32,4096]{1,0:T(8,128)(2,1)}, u32[]{:S(2)}, u32[]{:S(2)}) %collective-permute-start.3) | collective-permute-done | bytes 262176 | tf_op jit(solution)/shard_map/ppermute | solution.py:123
  182.0 3.8 %collective-permute-done.1 = bf16[32,4096]{1,0:T(8,128)(2,1)} collective-permute-done((bf16[32,4096]{1,0:T(8,128)(2,1)}, bf16[32,4096]{1,0:T(8,128)(2,1)}, u32[]{:S(2)}, u32[]{:S(2)}) %collective-permute-start.1) | collective-permute-done | bytes 262176 | tf_op jit(solution)/shard_map/ppermute | solution.py:122
  185.8 1.1 pad_maximum_fusion
  187.1 2.0 maximum_bitcast_fusion
  189.1 1.6 copy.67
  190.6 2.2 reshape.146
  192.8 2.6 %copy.68 = bf16[2,2,4,4,8,4096]{5,4,3,2,1,0:T(8,128)(2,1)S(1)} copy(bf16[2,2,4,4,8,4096]{5,4,1,2,0,3:T(8,128)(2,1)} %bitcast.282) | data formatting | bytes 8388608 | tf_op jit(solution)/shard_map/transpose | solution.py:127
  195.7 1.3 fusion.41
  196.9 0.8 copy.69
  197.8 5.7 %all-to-all-start.4 = ((f32[16,64,128]{2,1,0:T(8,128)}), f32[16,64,128]{2,1,0:T(8,128)S(1)}, u32[]{:S(2)}, u32[]{:S(2)}) async-start(f32[16,64,128]{2,1,0:T(8,128)} %bitcast.109), calls=%async_computation.4 | async-start | bytes 1048576 | tf_op jit(solution)/shard_map/all_to_all | solution.py:133
  203.5 14.6 %all-to-all-done.4 = f32[16,64,128]{2,1,0:T(8,128)S(1)} async-done(((f32[16,64,128]{2,1,0:T(8,128)}), f32[16,64,128]{2,1,0:T(8,128)S(1)}, u32[]{:S(2)}, u32[]{:S(2)}) %all-to-all-start.4) | async-done | bytes 524320 | tf_op jit(solution)/shard_map/all_to_all | solution.py:133
  218.1 0.6 fusion.172
  (170 shorter events, 10.6 us)
Async XLA Ops:
  6.5 37.7 %copy-start = (bf16[4,768,128]{2,1,0:T(8,128)(2,1)S(1)}, bf16[4,768,128]{2,1,0:T(8,128)(2,1)}, u32[]{:S(2)}) copy-start(bf16[4,768,128]{2,1,0:T(8,128)(2,1)} %param.15) | copy-start | bytes 2359300
  6.5 186.3 %all-gather.2.cloned.1.call-start = ((), (), s32[]{:S(2)}) async-start(), calls=%async_computation.5 | async-start | bytes 5242880 | tf_op jit(solution)/shard_map/all_gather | solution.py:114
  21.4 3.1 %copy-start.11 = (bf16[8,768,256]{2,1,0:T(8,128)(2,1)S(1)}, bf16[8,768,256]{2,1,0:T(8,128)(2,1)}, u32[]{:S(2)}) copy-start(bf16[8,768,256]{2,1,0:T(8,128)(2,1)} %param.11) | copy-start | bytes 9437188
  24.3 0.8 copy-start.26
  24.5 0.8 copy-start.53
  24.5 0.9 copy-start.54
  25.4 0.8 copy-start.27
  25.4 1.0 copy-start.59
  25.5 1.0 copy-start.55
  25.5 1.1 copy-start.56
  26.7 0.8 copy-start.25
  26.8 0.8 copy-start.51
  26.8 0.9 copy-start.52
  27.7 0.8 copy-start.23
  27.8 0.9 copy-start.49
  28.7 0.8 copy-start.21
  28.9 0.8 copy-start.44
  28.9 0.9 copy-start.46
  29.8 0.8 copy-start.17
  29.9 0.8 copy-start.40
  29.9 0.9 copy-start.42
  30.8 0.8 copy-start.15
  31.0 0.8 copy-start.37
  31.0 0.9 copy-start.39
  31.0 1.0 copy-start.57
  31.0 1.2 copy-start.58
  31.9 0.9 copy-start.13
  32.0 0.8 copy-start.33
  32.0 0.9 copy-start.35
  35.2 0.8 copy-start.1
  36.5 0.8 copy-start.3
  37.6 0.8 copy-start.5
  41.0 0.7 copy-start.9
  47.4 2.7 %copy-start.28 = (bf16[4,256,128]{2,1,0:T(8,128)(2,1)S(1)}, bf16[4,256,128]{2,1,0:T(8,128)(2,1)}, u32[]{:S(2)}) copy-start(bf16[4,256,128]{2,1,0:T(8,128)(2,1)} %param.14) | copy-start | bytes 786436
  47.4 2.7 %copy-start.30 = (f32[12,64,256]{2,1,0:T(8,128)S(1)}, f32[12,64,256]{2,1,0:T(8,128)}, u32[]{:S(2)}) copy-start(f32[12,64,256]{2,1,0:T(8,128)} %get-tuple-element.8) | copy-start | bytes 2359300
  47.4 2.7 %copy-start.31 = (f32[12,63,256]{2,1,0:T(8,128)S(1)}, f32[12,63,256]{2,1,0:T(8,128)}, u32[]{:S(2)}) copy-start(f32[12,63,256]{2,1,0:T(8,128)} %get-tuple-element.25) | copy-start | bytes 2322436
  47.4 2.6 %copy-start.32 = (f32[12,63,256]{2,1,0:T(8,128)S(1)}, f32[12,63,256]{2,1,0:T(8,128)}, u32[]{:S(2)}) copy-start(f32[12,63,256]{2,1,0:T(8,128)} %get-tuple-element.26) | copy-start | bytes 2322436
  47.5 2.6 %copy-start.60 = (f32[12,64,256]{2,1,0:T(8,128)S(1)}, f32[12,64,256]{2,1,0:T(8,128)}, u32[]{:S(2)}) copy-start(f32[12,64,256]{2,1,0:T(8,128)} %copy-done.59) | copy-start | bytes 2359300
  50.1 1.3 copy-start.10
  53.0 2.6 %copy-start.8 = (bf16[12,64,256]{2,1,0:T(8,128)(2,1)S(1)}, bf16[12,64,256]{2,1,0:T(8,128)(2,1)}, u32[]{:S(2)}) copy-start(bf16[12,64,256]{2,1,0:T(8,128)(2,1)} %copy-done.7) | copy-start | bytes 1179652
  53.0 2.6 %copy-start.29 = (bf16[4,256,128]{2,1,0:T(8,128)(2,1)S(1)}, bf16[4,256,128]{2,1,0:T(8,128)(2,1)}, u32[]{:S(2)}) copy-start(bf16[4,256,128]{2,1,0:T(8,128)(2,1)} %param.14) | copy-start | bytes 786436
  53.0 4.3 %copy-start.24 = (bf16[12,64,256]{2,1,0:T(8,128)(2,1)S(1)}, bf16[12,64,256]{2,1,0:T(8,128)(2,1)}, u32[]{:S(2)}) copy-start(bf16[12,64,256]{2,1,0:T(8,128)(2,1)} %copy-done.23) | copy-start | bytes 1179652
  53.0 4.3 %copy-start.48 = (bf16[12,63,256]{2,1,0:T(8,128)(2,1)S(1)}, bf16[12,63,256]{2,1,0:T(8,128)(2,1)}, u32[]{:S(2)}) copy-start(bf16[12,63,256]{2,1,0:T(8,128)(2,1)} %copy-done.47) | copy-start | bytes 1161220
  53.0 4.3 %copy-start.50 = (bf16[12,63,256]{2,1,0:T(8,128)(2,1)S(1)}, bf16[12,63,256]{2,1,0:T(8,128)(2,1)}, u32[]{:S(2)}) copy-start(bf16[12,63,256]{2,1,0:T(8,128)(2,1)} %copy-done.49) | copy-start | bytes 1161220
  57.4 1.3 copy-start.6
  57.4 3.0 %copy-start.22 = (bf16[12,64,256]{2,1,0:T(8,128)(2,1)S(1)}, bf16[12,64,256]{2,1,0:T(8,128)(2,1)}, u32[]{:S(2)}) copy-start(bf16[12,64,256]{2,1,0:T(8,128)(2,1)} %copy-done.21) | copy-start | bytes 1179652
  57.4 3.0 %copy-start.45 = (bf16[12,63,256]{2,1,0:T(8,128)(2,1)S(1)}, bf16[12,63,256]{2,1,0:T(8,128)(2,1)}, u32[]{:S(2)}) copy-start(bf16[12,63,256]{2,1,0:T(8,128)(2,1)} %copy-done.44) | copy-start | bytes 1161220
  60.4 2.4 %copy-start.4 = (bf16[12,64,256]{2,1,0:T(8,128)(2,1)S(1)}, bf16[12,64,256]{2,1,0:T(8,128)(2,1)}, u32[]{:S(2)}) copy-start(bf16[12,64,256]{2,1,0:T(8,128)(2,1)} %copy-done.3) | copy-start | bytes 1179652
  60.4 4.0 %copy-start.18 = (bf16[12,64,256]{2,1,0:T(8,128)(2,1)S(1)}, bf16[12,64,256]{2,1,0:T(8,128)(2,1)}, u32[]{:S(2)}) copy-start(bf16[12,64,256]{2,1,0:T(8,128)(2,1)} %copy-done.17) | copy-start | bytes 1179652
  60.4 4.0 %copy-start.41 = (bf16[12,63,256]{2,1,0:T(8,128)(2,1)S(1)}, bf16[12,63,256]{2,1,0:T(8,128)(2,1)}, u32[]{:S(2)}) copy-start(bf16[12,63,256]{2,1,0:T(8,128)(2,1)} %copy-done.40) | copy-start | bytes 1161220
  60.4 4.0 %copy-start.43 = (bf16[12,63,256]{2,1,0:T(8,128)(2,1)S(1)}, bf16[12,63,256]{2,1,0:T(8,128)(2,1)}, u32[]{:S(2)}) copy-start(bf16[12,63,256]{2,1,0:T(8,128)(2,1)} %copy-done.42) | copy-start | bytes 1161220
  64.4 1.3 copy-start.2
  64.4 2.9 %copy-start.16 = (bf16[12,64,256]{2,1,0:T(8,128)(2,1)S(1)}, bf16[12,64,256]{2,1,0:T(8,128)(2,1)}, u32[]{:S(2)}) copy-start(bf16[12,64,256]{2,1,0:T(8,128)(2,1)} %copy-done.15) | copy-start | bytes 1179652
  64.4 2.9 %copy-start.38 = (bf16[12,63,256]{2,1,0:T(8,128)(2,1)S(1)}, bf16[12,63,256]{2,1,0:T(8,128)(2,1)}, u32[]{:S(2)}) copy-start(bf16[12,63,256]{2,1,0:T(8,128)(2,1)} %copy-done.37) | copy-start | bytes 1161220
  67.4 4.0 %copy-start.14 = (bf16[12,64,256]{2,1,0:T(8,128)(2,1)S(1)}, bf16[12,64,256]{2,1,0:T(8,128)(2,1)}, u32[]{:S(2)}) copy-start(bf16[12,64,256]{2,1,0:T(8,128)(2,1)} %copy-done.13) | copy-start | bytes 1179652
  67.4 4.0 %copy-start.34 = (bf16[12,63,256]{2,1,0:T(8,128)(2,1)S(1)}, bf16[12,63,256]{2,1,0:T(8,128)(2,1)}, u32[]{:S(2)}) copy-start(bf16[12,63,256]{2,1,0:T(8,128)(2,1)} %copy-done.33) | copy-start | bytes 1161220
  67.4 4.0 %copy-start.36 = (bf16[12,63,256]{2,1,0:T(8,128)(2,1)S(1)}, bf16[12,63,256]{2,1,0:T(8,128)(2,1)}, u32[]{:S(2)}) copy-start(bf16[12,63,256]{2,1,0:T(8,128)(2,1)} %copy-done.35) | copy-start | bytes 1161220
  71.5 1.3 copy-start.20
  159.4 13.6 %collective-permute-start.2 = (bf16[64,4096]{1,0:T(8,128)(2,1)S(1)}, bf16[64,4096]{1,0:T(8,128)(2,1)S(1)}, u32[]{:S(2)}, u32[]{:S(2)}) collective-permute-start(bf16[64,4096]{1,0:T(8,128)(2,1)S(1)} %bitcast.286), channel_id=1, source_target_pairs={{0,96},{32,0},{64,32},{96,64},{1,97},{33,1},{65,33},{97,65},{2,98}... | collective-permute-start | bytes 1572872 | tf_op jit(solution)/shard_map/ppermute | solution.py:120
  162.2 15.1 %collective-permute-start = (bf16[64,4096]{1,0:T(8,128)(2,1)S(1)}, bf16[64,4096]{1,0:T(8,128)(2,1)S(1)}, u32[]{:S(2)}, u32[]{:S(2)}) collective-permute-start(bf16[64,4096]{1,0:T(8,128)(2,1)S(1)} %bitcast.287), channel_id=1, source_target_pairs={{0,32},{32,64},{64,96},{96,0},{1,33},{33,65},{65,97},{97,1},{2,34}... | collective-permute-start | bytes 1572872 | tf_op jit(solution)/shard_map/ppermute | solution.py:119
  173.7 8.3 %collective-permute-start.3 = (bf16[32,4096]{1,0:T(8,128)(2,1)}, bf16[32,4096]{1,0:T(8,128)(2,1)}, u32[]{:S(2)}, u32[]{:S(2)}) collective-permute-start(bf16[32,4096]{1,0:T(8,128)(2,1)} %slice.342), channel_id=1, source_target_pairs={{0,96},{32,0},{64,32},{96,64},{1,97},{33,1},{65,33},{97,65},{2,98}... | collective-permute-start | bytes 786440 | tf_op jit(solution)/shard_map/ppermute | solution.py:123
  177.9 7.9 %collective-permute-start.1 = (bf16[32,4096]{1,0:T(8,128)(2,1)}, bf16[32,4096]{1,0:T(8,128)(2,1)}, u32[]{:S(2)}, u32[]{:S(2)}) collective-permute-start(bf16[32,4096]{1,0:T(8,128)(2,1)} %slice.341), channel_id=1, source_target_pairs={{0,32},{32,64},{64,96},{96,0},{1,33},{33,65},{65,97},{97,1},{2,34}... | collective-permute-start | bytes 786440 | tf_op jit(solution)/shard_map/ppermute | solution.py:122
  192.8 2.9 %copy-start.12 = (bf16[4,64,4096,1]{2,1,0,3:T(8,128)(2,1)S(1)}, bf16[4,64,4096,1]{2,1,0,3:T(8,128)(2,1)}, u32[]{:S(2)}) copy-start(bf16[4,64,4096,1]{2,1,0,3:T(8,128)(2,1)} %reshape.146) | copy-start | bytes 6291460
  197.8 20.3 %all-to-all-start.4 = ((f32[16,64,128]{2,1,0:T(8,128)}), f32[16,64,128]{2,1,0:T(8,128)S(1)}, u32[]{:S(2)}, u32[]{:S(2)}) async-start(f32[16,64,128]{2,1,0:T(8,128)} %bitcast.109), calls=%async_computation.4 | async-start | bytes 1048576 | tf_op jit(solution)/shard_map/all_to_all | solution.py:133
  (3 other events, 2.2 us)
Sparse Core Ops, SparseCore 0:
  132.9 47.9 all-gather.1

commit v8 on v6

--- a/solution.py
+++ b/solution.py
@@ -23,11 +23,7 @@
     blocks_here = proj_delta.shape[0]
     offsets = jnp.arange(NFEAT, dtype=jnp.int32) * VOCAB
     table_rows = features.reshape(examples, SEQ, NFEAT) + offsets
-    table_ids = jnp.arange(NFEAT * VOCAB, dtype=jnp.int32)
-    onehot = (table_rows[:, :, 0:1] == table_ids).astype(jnp.bfloat16)
-    for field in range(1, NFEAT):
-        onehot = onehot + (table_rows[:, :, field : field + 1] == table_ids).astype(jnp.bfloat16)
-    hidden = jnp.einsum("esv,vc->esc", onehot, embed, preferred_element_type=jnp.float32)
+    hidden = jnp.sum(jnp.take(embed, table_rows, axis=0).astype(jnp.float32), axis=2)
     wides = []
     pres = []
     for layer in range(LAYERS):

time: 218 us -> 235 us (1.078)
  local copies, waits for them, and re-layouts: 32.6 us -> 49.5 us
  other arithmetic: 8.47 us -> 11.3 us
  matrix products: 42.4 us -> 39.7 us
    gather x0 -> x2, local copies, waits for them, and re-layouts: none -> 15.4 us  [panels(): jnp.take(embed, table_rows, axis=0).astype(jnp.float32)]
    dot_general x1 -> x0, matrix products: 2.88 us -> none  [panels(): jnp.einsum('esv,vc->esc', onehot, embed, preferred_element_type=jnp.float32)]
    reduce_sum x0 -> x1, other arithmetic: none -> 2.86 us  [panels(): jnp.sum(jnp.take(embed, table_rows, axis=0).astype(jnp.float32), axis=2)]
where the time goes in v8:
time: 235 us; the launch traced here: 234 us
  blocking collectives  55.6 us (24%)
  local copies, waits for them, and re-layouts  49.5 us (21%)
  matrix products  39.7 us (17%)
  waiting for transfers between devices  33 us (14%)
  between operations  30 us (13%)
  starting transfers between devices  14.6 us (6%)
  other arithmetic  11.3 us (5%)
    all_to_all x1, blocking collectives, on_device(): lax.all_to_all(sliced[:left_each], group, split_axis=1, concat_axis=0, ti...  35.6 us
    all_to_all x1, blocking collectives, on_device(): lax.all_to_all(right_sliced, group, split_axis=1, concat_axis=0, tiled=True)  20 us
    dot_general x8, matrix products, panels(): jnp.einsum('esk,kt->est', wides[layer], proj_input[assign[layer]], prefer...  16.3 us
    gather x2, local copies, waits for them, and re-layouts, panels(): jnp.take(embed, table_rows, axis=0).astype(jnp.float32)  15.4 us
    all_to_all x1, waiting for transfers between devices, on_device(): lax.all_to_all(chunks, group, split_axis=0, concat_axis=0, tiled=True)  14.5 us
    ppermute x1, waiting for transfers between devices, on_device(): from_above = lax.ppermute(right_part, 'y', down)  10.9 us
    dot_general x8, matrix products, panels(): jnp.einsum('esc,cr->esr', delta_low, proj_delta[assign[layer]], preferred...  8.39 us
    all_to_all x1, starting transfers between devices, on_device(): lax.all_to_all(chunks, group, split_axis=0, concat_axis=0, tiled=True)  8.24 us
  transfers between devices with their start and end apart: 6, of which 4 were waited for; matrix products, arithmetic and copies ran while one was open for 4% of the time, Pallas kernels for 0%

profile of v8, /device:TPU:1, one launch (start us, length us, event | category | flops | bytes accessed | tf_op | source)
XLA Modules:
  0.0 233.6 jit_solution(11302265891218709839)
XLA Ops:
  6.5 0.9 concatenate.149
  7.5 0.8 concatenate.146
  8.3 1.6 fusion.219
  20.3 0.9 convert_reduce_fusion.1
  21.3 0.8 copy.40
  22.8 13.0 %gather_fusion = bf16[3072,256]{1,0:T(8,128)(2,1)} fusion(bf16[1024,256]{1,0:T(8,128)(2,1)S(1)} %copy-done.1, s32[3072]{0:T(1024)S(1)} %broadcast_clamp_fusion), kind=kCustom, calls=%fused_computation | custom fusion | bytes 3158016 | tf_op jit(solution)/shard_map/jit(_take)/gather | solution.py:26
  35.8 2.4 %reshape.138 = bf16[12,64,4,256]{3,2,1,0:T(4,128)(2,1)S(1)} reshape(bf16[3072,256]{1,0:T(8,128)(2,1)} %gather_fusion) | data formatting | bytes 3145728 | tf_op jit(solution)/shard_map/jit(_take)/gather | solution.py:26
  38.8 2.9 %convert_reduce_fusion = f32[12,64,256]{2,1,0:T(8,128)S(1)} fusion(bf16[12,64,4,256]{3,2,1,0:T(4,128)(2,1)S(1)} %reshape.138, pred[12,64,4]{2,1,0:T(8,128)(4,1)S(1)} %copy.43), kind=kLoop, calls=%fused_computation.7 | loop fusion | flops 2162688 | bytes 2362368 | tf_op jit(solution)/shard_map/reduce_sum | solution.py:26
  41.9 0.5 fusion.192
  42.9 0.7 fusion.203
  44.2 0.5 fusion.193
  45.2 0.7 fusion.202
  46.2 0.5 fusion.194
  47.2 0.7 fusion.201
  48.3 0.5 add_convert_fusion
  49.5 0.6 multiply_convert_fusion.6
  50.2 0.5 fusion.78
  52.5 0.5 fusion.85
  54.9 0.5 fusion.93
  56.1 0.5 fusion.97
  56.9 1.3 multiply_convert_fusion
  58.2 0.8 copy-done.10
  59.4 1.4 fusion.204
  61.5 2.7 %fusion.35 = f32[8,12,64,128]{3,2,1,0:T(8,128)} fusion(bf16[4,768,128]{2,1,0:T(8,128)(2,1)S(1)} %copy-done, s32[]{:T(128)S(6)} %select_n.83, bf16[12,63,256]{2,1,0:T(8,128)(2,1)} %copy-done.57, bf16[12,63,256]{2,1,0:T(8,128)(2,1)} %copy-done.56, bf16[12,64,256]{2,1,0:T(8,128)(2,1)} %copy-done.12), kind=kOutput, calls=%fused_computation.45 | convolution fusion | flops 156893184 | bytes 1757188 | tf_op jit(solution)/shard_map/esk,kt->est/dot_general | solution.py:47
  64.9 2.6 %fusion.34 = f32[8,12,64,128]{3,2,1,0:T(8,128)} fusion(f32[8,12,64,128]{3,2,1,0:T(8,128)} %fusion.35, bf16[4,768,128]{2,1,0:T(8,128)(2,1)S(1)} %copy-done, s32[]{:T(128)S(6)} %select_n.84, bf16[12,63,256]{2,1,0:T(8,128)(2,1)} %copy-done.55, bf16[12,63,256]{2,1,0:T(8,128)(2,1)} %copy-done.54, bf16[12,64,256]{2,1,0:T(8,128)(2,1)} %copy-done.28), kind=kOutput, calls=%fused_computation.43 | convolution fusion | flops 156893184 | bytes 1769476 | tf_op jit(solution)/shard_map/esk,kt->est/dot_general | solution.py:47
  67.6 1.3 fusion.43
  68.9 1.0 fusion.42
  70.6 2.6 %fusion.33 = f32[8,12,64,128]{3,2,1,0:T(8,128)} fusion(f32[8,12,64,128]{3,2,1,0:T(8,128)} %fusion.34, bf16[4,768,128]{2,1,0:T(8,128)(2,1)S(1)} %copy-done, s32[]{:T(128)S(6)} %select_n.85, bf16[12,63,256]{2,1,0:T(8,128)(2,1)} %copy-done.53, bf16[12,63,256]{2,1,0:T(8,128)(2,1)} %copy-done.52, bf16[12,64,256]{2,1,0:T(8,128)(2,1)} %copy-done.27), kind=kOutput, calls=%fused_computation.41 | convolution fusion | flops 156893184 | bytes 1769476 | tf_op jit(solution)/shard_map/esk,kt->est/dot_general | solution.py:47
  73.2 1.0 fusion.41
  74.9 1.2 fusion.32
  76.2 1.0 fusion.40
  77.9 2.3 %fusion.31 = f32[8,12,64,128]{3,2,1,0:T(8,128)} fusion(f32[8,12,64,128]{3,2,1,0:T(8,128)} %fusion.32, bf16[4,768,128]{2,1,0:T(8,128)(2,1)S(1)} %copy-done, s32[]{:T(128)S(6)} %select_n.87, bf16[12,63,256]{2,1,0:T(8,128)(2,1)} %copy-done.47, bf16[12,63,256]{2,1,0:T(8,128)(2,1)S(1)} %copy-done.46, bf16[12,64,256]{2,1,0:T(8,128)(2,1)S(1)} %copy-done.24), kind=kOutput, calls=%fused_computation.37 | convolution fusion | flops 156893184 | bytes 1769476 | tf_op jit(solution)/shard_map/esk,kt->est/dot_general | solution.py:47
  80.2 1.0 fusion.39
  82.0 1.3 fusion.30
  83.2 1.0 fusion.38
  84.9 2.3 fusion.29
  87.2 1.0 fusion.37
  88.9 1.2 fusion.28
  90.2 1.0 fusion.36
  91.2 4.3 %gather_fusion.2 = f32[8,12,64,128]{3,2,1,0:T(8,128)} fusion(f32[8,12,64,128]{3,2,1,0:T(8,128)} %fusion.28, s32[1024]{0:T(1024)S(1)} %pad_clamp_fusion), kind=kCustom, calls=%fused_computation.2 | custom fusion | bytes 6291488 | tf_op jit(solution)/shard_map/gather | solution.py:71
  95.5 4.3 %gather_fusion.1 = f32[8,12,64,128]{3,2,1,0:T(8,128)} fusion(f32[8,12,64,128]{3,2,1,0:T(8,128)} %fusion.36, s32[1024]{0:T(1024)S(1)} %pad_clamp_fusion), kind=kCustom, calls=%fused_computation.1 | custom fusion | bytes 6291488 | tf_op jit(solution)/shard_map/gather | solution.py:70
  99.8 5.5 %bitcast_convert_fusion = bf16[12,4,128,128]{3,2,1,0:T(8,128)(2,1)S(1)} fusion(f32[4,2,12,64,128]{4,3,2,1,0:T(8,128)} %bitcast.262, f32[4,2,12,64,128]{4,3,2,1,0:T(8,128)} %bitcast.263), kind=kOutput, calls=%fused_computation.3 | convolution fusion | flops 604766208 | bytes 7864320 | tf_op jit(solution)/shard_map/bjesr,bjest->ebrt/dot_general | solution.py:75
  105.3 1.0 slice.324
  106.3 1.5 slice.276
  107.8 0.6 copy.50
  108.4 35.6 %all_to_all.35 = bf16[8,16,4096]{2,0,1:T(8,128)(2,1)} all-to-all(bf16[8,16,4096]{2,0,1:T(8,128)(2,1)S(1)} %copy.50), channel_id=1, replica_groups=mesh['zh'=2,'y'=4,'core'=2,'col'=4,'pblk'=4] {'zh','core','col'}, dimensions={1} | all-to-all | bytes 2097152 | tf_op jit(solution)/shard_map/all_to_all | solution.py:97
  144.7 20.0 %all_to_all.36 = bf16[4,16,4096]{2,0,1:T(4,128)(2,1)S(1)} all-to-all(bf16[4,16,4096]{2,0,1:T(4,128)(2,1)S(1)} %copy.51), channel_id=1, replica_groups=mesh['zh'=2,'y'=4,'core'=2,'col'=4,'pblk'=4] {'zh','core','col'}, dimensions={1} | all-to-all | bytes 1048576 | tf_op jit(solution)/shard_map/all_to_all | solution.py:101
  164.8 2.8 %collective-permute-start.2 = (bf16[64,4096]{1,0:T(8,128)(2,1)S(1)}, bf16[64,4096]{1,0:T(8,128)(2,1)S(1)}, u32[]{:S(2)}, u32[]{:S(2)}) collective-permute-start(bf16[64,4096]{1,0:T(8,128)(2,1)S(1)} %reshape.132), channel_id=1, source_target_pairs={{0,96},{32,0},{64,32},{96,64},{1,97},{33,1},{65,33},{97,65},{2,98}... | collective-permute-start | bytes 1572872 | tf_op jit(solution)/shard_map/ppermute | solution.py:106
  167.6 10.9 %collective-permute-done.2 = bf16[64,4096]{1,0:T(8,128)(2,1)S(1)} collective-permute-done((bf16[64,4096]{1,0:T(8,128)(2,1)S(1)}, bf16[64,4096]{1,0:T(8,128)(2,1)S(1)}, u32[]{:S(2)}, u32[]{:S(2)}) %collective-permute-start.2) | collective-permute-done | bytes 524320 | tf_op jit(solution)/shard_map/ppermute | solution.py:106
  178.5 0.7 slice.327
  179.2 3.5 %collective-permute-start.3 = (bf16[32,4096]{1,0:T(8,128)(2,1)}, bf16[32,4096]{1,0:T(8,128)(2,1)}, u32[]{:S(2)}, u32[]{:S(2)}) collective-permute-start(bf16[32,4096]{1,0:T(8,128)(2,1)} %slice.327), channel_id=1, source_target_pairs={{0,96},{32,0},{64,32},{96,64},{1,97},{33,1},{65,33},{97,65},{2,98}... | collective-permute-start | bytes 786440 | tf_op jit(solution)/shard_map/ppermute | solution.py:109
  182.8 0.7 slice.326
  183.9 3.7 %collective-permute-done.3 = bf16[32,4096]{1,0:T(8,128)(2,1)} collective-permute-done((bf16[32,4096]{1,0:T(8,128)(2,1)}, bf16[32,4096]{1,0:T(8,128)(2,1)}, u32[]{:S(2)}, u32[]{:S(2)}) %collective-permute-start.3) | collective-permute-done | bytes 262176 | tf_op jit(solution)/shard_map/ppermute | solution.py:109
  187.6 3.9 %collective-permute-done.1 = bf16[32,4096]{1,0:T(8,128)(2,1)} collective-permute-done((bf16[32,4096]{1,0:T(8,128)(2,1)}, bf16[32,4096]{1,0:T(8,128)(2,1)}, u32[]{:S(2)}, u32[]{:S(2)}) %collective-permute-start.1) | collective-permute-done | bytes 262176 | tf_op jit(solution)/shard_map/ppermute | solution.py:108
  191.5 1.1 pad_maximum_fusion
  192.7 2.0 maximum_bitcast_fusion
  194.7 1.6 copy.52
  196.3 2.1 reshape.187
  198.4 2.6 %copy.53 = bf16[4,4,4,8,4096]{4,3,2,1,0:T(8,128)(2,1)S(1)} copy(bf16[4,4,4,8,4096]{4,3,1,0,2:T(8,128)(2,1)} %bitcast.266) | data formatting | bytes 8388608 | tf_op jit(solution)/shard_map/transpose | solution.py:113
  201.2 1.3 fusion.25
  202.5 0.8 copy.54
  203.4 8.2 %all-to-all-start.2 = ((f32[16,64,128]{2,1,0:T(8,128)}), f32[16,64,128]{2,1,0:T(8,128)S(1)}, u32[]{:S(2)}, u32[]{:S(2)}) async-start(f32[16,64,128]{2,1,0:T(8,128)} %bitcast.96), calls=%async_computation.2 | async-start | bytes 1048576 | tf_op jit(solution)/shard_map/all_to_all | solution.py:119
  211.6 14.5 %all-to-all-done.2 = f32[16,64,128]{2,1,0:T(8,128)S(1)} async-done(((f32[16,64,128]{2,1,0:T(8,128)}), f32[16,64,128]{2,1,0:T(8,128)S(1)}, u32[]{:S(2)}, u32[]{:S(2)}) %all-to-all-start.2) | async-done | bytes 524320 | tf_op jit(solution)/shard_map/all_to_all | solution.py:119
  226.1 0.6 fusion.155
  (176 shorter events, 11.6 us)
Async XLA Ops:
  6.5 54.9 %copy-start = (bf16[4,768,128]{2,1,0:T(8,128)(2,1)S(1)}, bf16[4,768,128]{2,1,0:T(8,128)(2,1)}, u32[]{:S(2)}) copy-start(bf16[4,768,128]{2,1,0:T(8,128)(2,1)} %param.15) | copy-start | bytes 2359300
  6.5 16.3 %copy-start.1 = (bf16[1024,256]{1,0:T(8,128)(2,1)S(1)}, bf16[1024,256]{1,0:T(8,128)(2,1)}, u32[]{:S(2)}) copy-start(bf16[1024,256]{1,0:T(8,128)(2,1)} %param.10) | copy-start | bytes 1572868
  6.5 191.8 %all-gather.2.cloned.1.call-start = ((), (), s32[]{:S(2)}) async-start(), calls=%async_computation.3 | async-start | bytes 5242880 | tf_op jit(solution)/shard_map/all_gather | solution.py:99
  38.8 3.1 %copy-start.13 = (bf16[8,768,256]{2,1,0:T(8,128)(2,1)S(1)}, bf16[8,768,256]{2,1,0:T(8,128)(2,1)}, u32[]{:S(2)}) copy-start(bf16[8,768,256]{2,1,0:T(8,128)(2,1)} %param.11) | copy-start | bytes 9437188
  41.7 0.8 copy-start.12
  41.8 0.8 copy-start.56
  41.8 0.9 copy-start.57
  42.7 0.8 copy-start.28
  42.7 1.0 copy-start.60
  42.9 1.0 copy-start.54
  42.9 1.1 copy-start.55
  44.0 0.8 copy-start.27
  44.1 0.8 copy-start.52
  44.1 0.9 copy-start.53
  45.0 0.8 copy-start.25
  45.2 0.9 copy-start.50
  46.1 0.8 copy-start.23
  46.2 0.8 copy-start.45
  46.2 0.9 copy-start.47
  47.1 0.9 copy-start.19
  47.2 0.8 copy-start.41
  47.2 0.9 copy-start.43
  48.1 0.8 copy-start.17
  48.3 0.8 copy-start.38
  48.3 0.9 copy-start.40
  48.3 1.0 copy-start.58
  48.3 1.2 copy-start.59
  49.2 0.9 copy-start.15
  49.3 0.8 copy-start.34
  49.3 0.9 copy-start.36
  52.5 0.8 copy-start.2
  54.9 0.8 copy-start.6
  58.2 0.8 copy-start.10
  64.9 2.7 %copy-start.29 = (bf16[4,256,128]{2,1,0:T(8,128)(2,1)S(1)}, bf16[4,256,128]{2,1,0:T(8,128)(2,1)}, u32[]{:S(2)}) copy-start(bf16[4,256,128]{2,1,0:T(8,128)(2,1)} %param.14) | copy-start | bytes 786436
  64.9 2.7 %copy-start.31 = (f32[12,64,256]{2,1,0:T(8,128)S(1)}, f32[12,64,256]{2,1,0:T(8,128)}, u32[]{:S(2)}) copy-start(f32[12,64,256]{2,1,0:T(8,128)} %get-tuple-element.8) | copy-start | bytes 2359300
  64.9 2.7 %copy-start.32 = (f32[12,63,256]{2,1,0:T(8,128)S(1)}, f32[12,63,256]{2,1,0:T(8,128)}, u32[]{:S(2)}) copy-start(f32[12,63,256]{2,1,0:T(8,128)} %get-tuple-element.25) | copy-start | bytes 2322436
  64.9 2.7 %copy-start.33 = (f32[12,63,256]{2,1,0:T(8,128)S(1)}, f32[12,63,256]{2,1,0:T(8,128)}, u32[]{:S(2)}) copy-start(f32[12,63,256]{2,1,0:T(8,128)} %get-tuple-element.26) | copy-start | bytes 2322436
  64.9 2.7 %copy-start.61 = (f32[12,64,256]{2,1,0:T(8,128)S(1)}, f32[12,64,256]{2,1,0:T(8,128)}, u32[]{:S(2)}) copy-start(f32[12,64,256]{2,1,0:T(8,128)} %copy-done.60) | copy-start | bytes 2359300
  67.6 1.3 copy-start.11
  70.6 2.7 %copy-start.9 = (bf16[12,64,256]{2,1,0:T(8,128)(2,1)S(1)}, bf16[12,64,256]{2,1,0:T(8,128)(2,1)}, u32[]{:S(2)}) copy-start(bf16[12,64,256]{2,1,0:T(8,128)(2,1)} %copy-done.8) | copy-start | bytes 1179652
  70.6 2.6 %copy-start.30 = (bf16[4,256,128]{2,1,0:T(8,128)(2,1)S(1)}, bf16[4,256,128]{2,1,0:T(8,128)(2,1)}, u32[]{:S(2)}) copy-start(bf16[4,256,128]{2,1,0:T(8,128)(2,1)} %param.14) | copy-start | bytes 786436
  70.6 4.3 %copy-start.26 = (bf16[12,64,256]{2,1,0:T(8,128)(2,1)S(1)}, bf16[12,64,256]{2,1,0:T(8,128)(2,1)}, u32[]{:S(2)}) copy-start(bf16[12,64,256]{2,1,0:T(8,128)(2,1)} %copy-done.25) | copy-start | bytes 1179652
  70.6 4.3 %copy-start.49 = (bf16[12,63,256]{2,1,0:T(8,128)(2,1)S(1)}, bf16[12,63,256]{2,1,0:T(8,128)(2,1)}, u32[]{:S(2)}) copy-start(bf16[12,63,256]{2,1,0:T(8,128)(2,1)} %copy-done.48) | copy-start | bytes 1161220
  70.6 4.3 %copy-start.51 = (bf16[12,63,256]{2,1,0:T(8,128)(2,1)S(1)}, bf16[12,63,256]{2,1,0:T(8,128)(2,1)}, u32[]{:S(2)}) copy-start(bf16[12,63,256]{2,1,0:T(8,128)(2,1)} %copy-done.50) | copy-start | bytes 1161220
  74.9 1.3 copy-start.7
  74.9 2.9 %copy-start.24 = (bf16[12,64,256]{2,1,0:T(8,128)(2,1)S(1)}, bf16[12,64,256]{2,1,0:T(8,128)(2,1)}, u32[]{:S(2)}) copy-start(bf16[12,64,256]{2,1,0:T(8,128)(2,1)} %copy-done.23) | copy-start | bytes 1179652
  74.9 2.9 %copy-start.46 = (bf16[12,63,256]{2,1,0:T(8,128)(2,1)S(1)}, bf16[12,63,256]{2,1,0:T(8,128)(2,1)}, u32[]{:S(2)}) copy-start(bf16[12,63,256]{2,1,0:T(8,128)(2,1)} %copy-done.45) | copy-start | bytes 1161220
  77.9 2.4 %copy-start.5 = (bf16[12,64,256]{2,1,0:T(8,128)(2,1)S(1)}, bf16[12,64,256]{2,1,0:T(8,128)(2,1)}, u32[]{:S(2)}) copy-start(bf16[12,64,256]{2,1,0:T(8,128)(2,1)} %copy-done.4) | copy-start | bytes 1179652
  77.9 4.0 %copy-start.20 = (bf16[12,64,256]{2,1,0:T(8,128)(2,1)S(1)}, bf16[12,64,256]{2,1,0:T(8,128)(2,1)}, u32[]{:S(2)}) copy-start(bf16[12,64,256]{2,1,0:T(8,128)(2,1)} %copy-done.19) | copy-start | bytes 1179652
  77.9 4.0 %copy-start.42 = (bf16[12,63,256]{2,1,0:T(8,128)(2,1)S(1)}, bf16[12,63,256]{2,1,0:T(8,128)(2,1)}, u32[]{:S(2)}) copy-start(bf16[12,63,256]{2,1,0:T(8,128)(2,1)} %copy-done.41) | copy-start | bytes 1161220
  77.9 4.0 %copy-start.44 = (bf16[12,63,256]{2,1,0:T(8,128)(2,1)S(1)}, bf16[12,63,256]{2,1,0:T(8,128)(2,1)}, u32[]{:S(2)}) copy-start(bf16[12,63,256]{2,1,0:T(8,128)(2,1)} %copy-done.43) | copy-start | bytes 1161220
  81.9 1.3 copy-start.3
  81.9 2.9 %copy-start.18 = (bf16[12,64,256]{2,1,0:T(8,128)(2,1)S(1)}, bf16[12,64,256]{2,1,0:T(8,128)(2,1)}, u32[]{:S(2)}) copy-start(bf16[12,64,256]{2,1,0:T(8,128)(2,1)} %copy-done.17) | copy-start | bytes 1179652
  81.9 2.9 %copy-start.39 = (bf16[12,63,256]{2,1,0:T(8,128)(2,1)S(1)}, bf16[12,63,256]{2,1,0:T(8,128)(2,1)}, u32[]{:S(2)}) copy-start(bf16[12,63,256]{2,1,0:T(8,128)(2,1)} %copy-done.38) | copy-start | bytes 1161220
  84.9 4.0 %copy-start.16 = (bf16[12,64,256]{2,1,0:T(8,128)(2,1)S(1)}, bf16[12,64,256]{2,1,0:T(8,128)(2,1)}, u32[]{:S(2)}) copy-start(bf16[12,64,256]{2,1,0:T(8,128)(2,1)} %copy-done.15) | copy-start | bytes 1179652
  84.9 4.0 %copy-start.35 = (bf16[12,63,256]{2,1,0:T(8,128)(2,1)S(1)}, bf16[12,63,256]{2,1,0:T(8,128)(2,1)}, u32[]{:S(2)}) copy-start(bf16[12,63,256]{2,1,0:T(8,128)(2,1)} %copy-done.34) | copy-start | bytes 1161220
  84.9 4.0 %copy-start.37 = (bf16[12,63,256]{2,1,0:T(8,128)(2,1)S(1)}, bf16[12,63,256]{2,1,0:T(8,128)(2,1)}, u32[]{:S(2)}) copy-start(bf16[12,63,256]{2,1,0:T(8,128)(2,1)} %copy-done.36) | copy-start | bytes 1161220
  88.9 1.3 copy-start.22
  164.8 13.7 %collective-permute-start.2 = (bf16[64,4096]{1,0:T(8,128)(2,1)S(1)}, bf16[64,4096]{1,0:T(8,128)(2,1)S(1)}, u32[]{:S(2)}, u32[]{:S(2)}) collective-permute-start(bf16[64,4096]{1,0:T(8,128)(2,1)S(1)} %reshape.132), channel_id=1, source_target_pairs={{0,96},{32,0},{64,32},{96,64},{1,97},{33,1},{65,33},{97,65},{2,98}... | collective-permute-start | bytes 1572872 | tf_op jit(solution)/shard_map/ppermute | solution.py:106
  167.6 15.1 %collective-permute-start = (bf16[64,4096]{1,0:T(8,128)(2,1)S(1)}, bf16[64,4096]{1,0:T(8,128)(2,1)S(1)}, u32[]{:S(2)}, u32[]{:S(2)}) collective-permute-start(bf16[64,4096]{1,0:T(8,128)(2,1)S(1)} %reshape.132), channel_id=1, source_target_pairs={{0,32},{32,64},{64,96},{96,0},{1,33},{33,65},{65,97},{97,1},{2,34}... | collective-permute-start | bytes 1572872 | tf_op jit(solution)/shard_map/ppermute | solution.py:105
  179.2 8.4 %collective-permute-start.3 = (bf16[32,4096]{1,0:T(8,128)(2,1)}, bf16[32,4096]{1,0:T(8,128)(2,1)}, u32[]{:S(2)}, u32[]{:S(2)}) collective-permute-start(bf16[32,4096]{1,0:T(8,128)(2,1)} %slice.327), channel_id=1, source_target_pairs={{0,96},{32,0},{64,32},{96,64},{1,97},{33,1},{65,33},{97,65},{2,98}... | collective-permute-start | bytes 786440 | tf_op jit(solution)/shard_map/ppermute | solution.py:109
  183.5 8.0 %collective-permute-start.1 = (bf16[32,4096]{1,0:T(8,128)(2,1)}, bf16[32,4096]{1,0:T(8,128)(2,1)}, u32[]{:S(2)}, u32[]{:S(2)}) collective-permute-start(bf16[32,4096]{1,0:T(8,128)(2,1)} %slice.326), channel_id=1, source_target_pairs={{0,32},{32,64},{64,96},{96,0},{1,33},{33,65},{65,97},{97,1},{2,34}... | collective-permute-start | bytes 786440 | tf_op jit(solution)/shard_map/ppermute | solution.py:108
  198.4 2.9 %copy-start.14 = (bf16[4,64,4096,1]{2,1,0,3:T(8,128)(2,1)S(1)}, bf16[4,64,4096,1]{2,1,0,3:T(8,128)(2,1)}, u32[]{:S(2)}) copy-start(bf16[4,64,4096,1]{2,1,0,3:T(8,128)(2,1)} %reshape.187) | copy-start | bytes 6291460
  203.4 22.7 %all-to-all-start.2 = ((f32[16,64,128]{2,1,0:T(8,128)}), f32[16,64,128]{2,1,0:T(8,128)S(1)}, u32[]{:S(2)}, u32[]{:S(2)}) async-start(f32[16,64,128]{2,1,0:T(8,128)} %bitcast.96), calls=%async_computation.2 | async-start | bytes 1048576 | tf_op jit(solution)/shard_map/all_to_all | solution.py:119
  (4 other events, 3.0 us)
Sparse Core Ops, SparseCore 0:
  144.1 50.0 all-gather.1

commit v9 on v6

--- a/solution.py
+++ b/solution.py
@@ -120,7 +120,14 @@
     partial_t = jnp.einsum("rk,lk->rl", right_tile, left_tile, preferred_element_type=jnp.float32)
     chunks = partial_t.reshape(n_col, partial_t.shape[0] // n_col, n_zh * n_core, -1)
     chunks = jnp.transpose(chunks, (2, 0, 1, 3)).reshape(n_group, chunks.shape[1], chunks.shape[3])
-    received = lax.all_to_all(chunks, group, split_axis=0, concat_axis=0, tiled=True)
+    chunks = chunks.reshape(n_zh, n_core, n_col, chunks.shape[1], chunks.shape[2])
+    mine = lax.axis_index("core")
+    swap = [(j, (j + 1) % n_core) for j in range(n_core)]
+    for_partner = lax.dynamic_index_in_dim(chunks, 1 - mine, axis=1, keepdims=False)
+    kept = lax.dynamic_index_in_dim(chunks, mine, axis=1, keepdims=False)
+    paired = kept + lax.ppermute(for_partner, "core", swap)
+    paired = paired.reshape(n_zh * n_col, paired.shape[2], paired.shape[3])
+    received = lax.all_to_all(paired, ("zh", "col"), split_axis=0, concat_axis=0, tiled=True)
     block = jnp.sum(received, axis=0).T
     block = block.reshape(block.shape[0], n_zh, n_y, n_core * right_each)
     block = jnp.roll(block, lax.axis_index("y") - 2, axis=2)

time: 218 us -> 215 us (0.986)
  waiting for transfers between devices: 33 us -> 30.8 us
    all_to_all x1, waiting for transfers between devices: 14.5 us -> 11.1 us  [on_device(): lax.all_to_all(paired, ('zh', 'col'), split_axis=0, concat_axis=0, tiled=...]
    all_to_all x1, starting transfers between devices: 8.24 us -> 5.68 us  [on_device(): lax.all_to_all(paired, ('zh', 'col'), split_axis=0, concat_axis=0, tiled=...]
    ppermute x0 -> x1, starting transfers between devices: none -> 2.35 us  [on_device(): paired = kept + lax.ppermute(for_partner, 'core', swap)]
  transfers between devices with their start and end apart: 6 -> 7, of which waited for: 4 -> 5; matrix products, arithmetic and copies ran while one was open for 4% -> 4% of each run, Pallas kernels for 0% -> 0%
where the time goes in v9:
time: 215 us; the launch traced here: 214 us
  blocking collectives  55.5 us (26%)
  matrix products  42.4 us (20%)
  local copies, waits for them, and re-layouts  31.9 us (15%)
  waiting for transfers between devices  30.8 us (14%)
  between operations  29.3 us (14%)
  starting transfers between devices  14.4 us (7%)
  other arithmetic  9.21 us (4%)
    all_to_all x1, blocking collectives, on_device(): lax.all_to_all(sliced[:left_each], group, split_axis=1, concat_axis=0, ti...  35.6 us
    all_to_all x1, blocking collectives, on_device(): lax.all_to_all(right_sliced, group, split_axis=1, concat_axis=0, tiled=True)  20 us
    dot_general x8, matrix products, panels(): jnp.einsum('esk,kt->est', wides[layer], proj_input[assign[layer]], prefer...  16.1 us
    all_to_all x1, waiting for transfers between devices, on_device(): lax.all_to_all(paired, ('zh', 'col'), split_axis=0, concat_axis=0, tiled=...  11.1 us
    ppermute x1, waiting for transfers between devices, on_device(): from_above = lax.ppermute(right_part, 'y', down)  10.9 us
    dot_general x8, matrix products, panels(): jnp.einsum('esc,cr->esr', delta_low, proj_delta[assign[layer]], preferred...  8.43 us
    all_to_all x1, starting transfers between devices, on_device(): lax.all_to_all(paired, ('zh', 'col'), split_axis=0, concat_axis=0, tiled=...  5.68 us
    dot_general x1, matrix products, panels(): jnp.einsum('bjesr,bjest->ebrt', delta_stack, input_stack, precision=lax.P...  5.48 us
  transfers between devices with their start and end apart: 7, of which 5 were waited for; matrix products, arithmetic and copies ran while one was open for 4% of the time, Pallas kernels for 0%

profile of v9, /device:TPU:1, one launch (start us, length us, event | category | flops | bytes accessed | tf_op | source)
XLA Modules:
  0.0 213.5 jit_solution(15842210196627968603)
XLA Ops:
  6.5 1.6 fusion.234
  18.1 0.9 convert_reduce_fusion
  19.0 0.8 copy.54
  19.9 0.8 copy.38
  21.2 2.9 %fusion.235 = (bf16[12,64,256]{2,1,0:T(8,128)(2,1)S(1)}, f32[12,64,256]{2,1,0:T(8,128)S(1)}) fusion(bf16[1024,256]{1,0:T(8,128)(2,1)} %param.10, s32[12,64]{1,0:T(8,128)S(1)} %bitcast.283, s32[12,64]{1,0:T(8,128)S(1)} %bitcast.284, s32[12,64]{1,0:T(8,128)S(1)} %bitcast.285, s32[12,64]{1,0:T(8,128)S(1)} %bitcast.286), kind=kOutput, calls=%fused_computation.275 | convolution fusion | flops 415432704 | bytes 1716224 | tf_op jit(solution)/shard_map/esv,vc->esc/dot_general | solution.py:30
  24.3 0.5 fusion.206
  25.3 0.7 fusion.217
  26.6 0.5 fusion.207
  27.6 0.7 fusion.216
  28.7 0.5 fusion.208
  29.7 0.7 fusion.215
  30.8 0.5 add_convert_fusion
  32.1 0.6 multiply_convert_fusion.6
  32.8 0.5 fusion.92
  33.9 0.5 fusion.95
  35.1 0.5 fusion.99
  37.5 0.5 fusion.107
  38.3 0.6 multiply_convert_fusion.1
  39.6 1.3 multiply_convert_fusion
  40.9 0.7 copy-done.9
  42.2 1.3 fusion.218
  44.0 2.5 %fusion.48 = f32[8,12,64,128]{3,2,1,0:T(8,128)} fusion(bf16[4,768,128]{2,1,0:T(8,128)(2,1)S(1)} %copy-done, s32[]{:T(128)S(6)} %select_n.67, bf16[12,63,256]{2,1,0:T(8,128)(2,1)} %copy-done.54, bf16[12,63,256]{2,1,0:T(8,128)(2,1)} %copy-done.53, bf16[12,64,256]{2,1,0:T(8,128)(2,1)} %copy-done.26), kind=kOutput, calls=%fused_computation.58 | convolution fusion | flops 156893184 | bytes 1757188 | tf_op jit(solution)/shard_map/esk,kt->est/dot_general | solution.py:51
  47.2 2.6 %fusion.47 = f32[8,12,64,128]{3,2,1,0:T(8,128)} fusion(f32[8,12,64,128]{3,2,1,0:T(8,128)} %fusion.48, bf16[4,768,128]{2,1,0:T(8,128)(2,1)S(1)} %copy-done, s32[]{:T(128)S(6)} %select_n.68, bf16[12,63,256]{2,1,0:T(8,128)(2,1)} %copy-done.56, bf16[12,63,256]{2,1,0:T(8,128)(2,1)} %copy-done.55, bf16[12,64,256]{2,1,0:T(8,128)(2,1)} %copy-done.27), kind=kOutput, calls=%fused_computation.56 | convolution fusion | flops 156893184 | bytes 1769476 | tf_op jit(solution)/shard_map/esk,kt->est/dot_general | solution.py:51
  49.9 1.3 fusion.56
  51.2 1.0 fusion.55
  52.9 2.6 %fusion.46 = f32[8,12,64,128]{3,2,1,0:T(8,128)} fusion(f32[8,12,64,128]{3,2,1,0:T(8,128)} %fusion.47, bf16[4,768,128]{2,1,0:T(8,128)(2,1)S(1)} %copy-done, s32[]{:T(128)S(6)} %select_n.69, bf16[12,63,256]{2,1,0:T(8,128)(2,1)} %copy-done.52, bf16[12,63,256]{2,1,0:T(8,128)(2,1)} %copy-done.51, bf16[12,64,256]{2,1,0:T(8,128)(2,1)} %copy-done.25), kind=kOutput, calls=%fused_computation.54 | convolution fusion | flops 156893184 | bytes 1769476 | tf_op jit(solution)/shard_map/esk,kt->est/dot_general | solution.py:51
  55.5 1.0 fusion.54
  57.3 1.2 fusion.45
  58.5 1.0 fusion.53
  60.2 2.4 %fusion.44 = f32[8,12,64,128]{3,2,1,0:T(8,128)} fusion(f32[8,12,64,128]{3,2,1,0:T(8,128)} %fusion.45, bf16[4,768,128]{2,1,0:T(8,128)(2,1)S(1)} %copy-done, s32[]{:T(128)S(6)} %select_n.71, bf16[12,63,256]{2,1,0:T(8,128)(2,1)} %copy-done.46, bf16[12,63,256]{2,1,0:T(8,128)(2,1)S(1)} %copy-done.45, bf16[12,64,256]{2,1,0:T(8,128)(2,1)S(1)} %copy-done.22), kind=kOutput, calls=%fused_computation.50 | convolution fusion | flops 156893184 | bytes 1769476 | tf_op jit(solution)/shard_map/esk,kt->est/dot_general | solution.py:51
  62.6 1.0 fusion.52
  64.3 1.3 fusion.43
  65.6 1.0 fusion.51
  67.2 2.3 %fusion.42 = f32[8,12,64,128]{3,2,1,0:T(8,128)} fusion(f32[8,12,64,128]{3,2,1,0:T(8,128)} %fusion.43, bf16[4,768,128]{2,1,0:T(8,128)(2,1)S(1)} %copy-done, s32[]{:T(128)S(6)} %select_n.73, bf16[12,63,256]{2,1,0:T(8,128)(2,1)} %copy-done.39, bf16[12,63,256]{2,1,0:T(8,128)(2,1)S(1)} %copy-done.38, bf16[12,64,256]{2,1,0:T(8,128)(2,1)S(1)} %copy-done.16), kind=kOutput, calls=%fused_computation.46 | convolution fusion | flops 156893184 | bytes 1769476 | tf_op jit(solution)/shard_map/esk,kt->est/dot_general | solution.py:51
  69.5 1.0 fusion.50
  71.2 1.2 fusion.41
  72.5 1.0 fusion.49
  73.5 4.3 %gather_fusion.1 = f32[8,12,64,128]{3,2,1,0:T(8,128)} fusion(f32[8,12,64,128]{3,2,1,0:T(8,128)} %fusion.41, s32[1024]{0:T(1024)S(1)} %pad_clamp_fusion), kind=kCustom, calls=%fused_computation.1 | custom fusion | bytes 6291488 | tf_op jit(solution)/shard_map/gather | solution.py:75
  77.8 4.3 %gather_fusion = f32[8,12,64,128]{3,2,1,0:T(8,128)} fusion(f32[8,12,64,128]{3,2,1,0:T(8,128)} %fusion.49, s32[1024]{0:T(1024)S(1)} %pad_clamp_fusion), kind=kCustom, calls=%fused_computation | custom fusion | bytes 6291488 | tf_op jit(solution)/shard_map/gather | solution.py:74
  82.1 5.5 %bitcast_convert_fusion = bf16[12,4,128,128]{3,2,1,0:T(8,128)(2,1)S(1)} fusion(f32[4,2,12,64,128]{4,3,2,1,0:T(8,128)} %bitcast.271, f32[4,2,12,64,128]{4,3,2,1,0:T(8,128)} %bitcast.272), kind=kOutput, calls=%fused_computation.2 | convolution fusion | flops 604766208 | bytes 7864320 | tf_op jit(solution)/shard_map/bjesr,bjest->ebrt/dot_general | solution.py:79
  87.5 1.0 slice.342
  88.6 1.5 slice.292
  90.1 0.6 copy.46
  90.7 35.6 %all_to_all.35 = bf16[8,16,4096]{2,0,1:T(8,128)(2,1)} all-to-all(bf16[8,16,4096]{2,0,1:T(8,128)(2,1)S(1)} %copy.46), channel_id=1, replica_groups=mesh['zh'=2,'y'=4,'core'=2,'col'=4,'pblk'=4] {'zh','core','col'}, dimensions={1} | all-to-all | bytes 2097152 | tf_op jit(solution)/shard_map/all_to_all | solution.py:101
  127.0 20.0 %all_to_all.36 = bf16[4,16,4096]{2,0,1:T(4,128)(2,1)S(1)} all-to-all(bf16[4,16,4096]{2,0,1:T(4,128)(2,1)S(1)} %copy.47), channel_id=1, replica_groups=mesh['zh'=2,'y'=4,'core'=2,'col'=4,'pblk'=4] {'zh','core','col'}, dimensions={1} | all-to-all | bytes 1048576 | tf_op jit(solution)/shard_map/all_to_all | solution.py:105
  147.1 2.8 %collective-permute-start.2 = (bf16[64,4096]{1,0:T(8,128)(2,1)S(1)}, bf16[64,4096]{1,0:T(8,128)(2,1)S(1)}, u32[]{:S(2)}, u32[]{:S(2)}) collective-permute-start(bf16[64,4096]{1,0:T(8,128)(2,1)S(1)} %reshape.80), channel_id=1, source_target_pairs={{0,96},{32,0},{64,32},{96,64},{1,97},{33,1},{65,33},{97,65},{2,98}... | collective-permute-start | bytes 1572872 | tf_op jit(solution)/shard_map/ppermute | solution.py:110
  149.9 10.9 %collective-permute-done.2 = bf16[64,4096]{1,0:T(8,128)(2,1)S(1)} collective-permute-done((bf16[64,4096]{1,0:T(8,128)(2,1)S(1)}, bf16[64,4096]{1,0:T(8,128)(2,1)S(1)}, u32[]{:S(2)}, u32[]{:S(2)}) %collective-permute-start.2) | collective-permute-done | bytes 524320 | tf_op jit(solution)/shard_map/ppermute | solution.py:110
  160.8 0.7 slice.345
  161.6 3.5 %collective-permute-start.3 = (bf16[32,4096]{1,0:T(8,128)(2,1)}, bf16[32,4096]{1,0:T(8,128)(2,1)}, u32[]{:S(2)}, u32[]{:S(2)}) collective-permute-start(bf16[32,4096]{1,0:T(8,128)(2,1)} %slice.345), channel_id=1, source_target_pairs={{0,96},{32,0},{64,32},{96,64},{1,97},{33,1},{65,33},{97,65},{2,98}... | collective-permute-start | bytes 786440 | tf_op jit(solution)/shard_map/ppermute | solution.py:113
  165.1 0.7 slice.344
  166.2 3.7 %collective-permute-done.3 = bf16[32,4096]{1,0:T(8,128)(2,1)} collective-permute-done((bf16[32,4096]{1,0:T(8,128)(2,1)}, bf16[32,4096]{1,0:T(8,128)(2,1)}, u32[]{:S(2)}, u32[]{:S(2)}) %collective-permute-start.3) | collective-permute-done | bytes 262176 | tf_op jit(solution)/shard_map/ppermute | solution.py:113
  169.9 3.9 %collective-permute-done.1 = bf16[32,4096]{1,0:T(8,128)(2,1)} collective-permute-done((bf16[32,4096]{1,0:T(8,128)(2,1)}, bf16[32,4096]{1,0:T(8,128)(2,1)}, u32[]{:S(2)}, u32[]{:S(2)}) %collective-permute-start.1) | collective-permute-done | bytes 262176 | tf_op jit(solution)/shard_map/ppermute | solution.py:112
  173.8 1.1 pad_maximum_fusion
  175.1 2.0 maximum_bitcast_fusion
  177.0 1.6 copy.48
  178.6 2.2 %reshape.127 = bf16[4,64,4096,1]{2,1,0,3:T(8,128)(2,1)} reshape(bf16[4,2,4,2,4,4096]{5,4,3,2,1,0:T(4,128)(2,1)S(1)} %copy.48) | data formatting | bytes 4194304 | tf_op jit(solution)/shard_map/rk,lk->rl/dot_general | solution.py:120
  180.7 2.6 %copy.49 = bf16[4,4,4,8,4096]{4,3,2,1,0:T(8,128)(2,1)S(1)} copy(bf16[4,4,4,8,4096]{4,3,1,0,2:T(8,128)(2,1)} %bitcast.275) | data formatting | bytes 8388608 | tf_op jit(solution)/shard_map/transpose | solution.py:117
  183.6 1.3 fusion.23
  185.0 2.4 %collective-permute-start.4 = (f32[2,4,64,128]{3,2,1,0:T(8,128)S(1)}, f32[2,4,64,128]{3,2,1,0:T(8,128)S(1)}, u32[]{:S(2)}, u32[]{:S(2)}) collective-permute-start(f32[2,4,64,128]{3,2,1,0:T(8,128)S(1)} %bitcast.281), channel_id=1, source_target_pairs={{0,16},{16,0},{1,17},{17,1},{2,18},{18,2},{3,19},{19,3},{4,20},{20... | collective-permute-start | bytes 786440 | tf_op jit(solution)/shard_map/ppermute | solution.py:128
  187.3 1.2 collective-permute-done.4
  188.5 0.7 bitcast_add_fusion
  189.2 5.7 %all-to-all-start.2 = ((f32[8,64,128]{2,1,0:T(8,128)}), f32[8,64,128]{2,1,0:T(8,128)S(1)}, u32[]{:S(2)}, u32[]{:S(2)}) async-start(f32[8,64,128]{2,1,0:T(8,128)} %bitcast.105), calls=%async_computation.2 | async-start | bytes 524288 | tf_op jit(solution)/shard_map/all_to_all | solution.py:130
  194.9 11.1 %all-to-all-done.2 = f32[8,64,128]{2,1,0:T(8,128)S(1)} async-done(((f32[8,64,128]{2,1,0:T(8,128)}), f32[8,64,128]{2,1,0:T(8,128)S(1)}, u32[]{:S(2)}, u32[]{:S(2)}) %all-to-all-start.2) | async-done | bytes 262176 | tf_op jit(solution)/shard_map/all_to_all | solution.py:130
  206.0 0.6 fusion.169
  (170 shorter events, 10.6 us)
Async XLA Ops:
  6.5 37.5 %copy-start = (bf16[4,768,128]{2,1,0:T(8,128)(2,1)S(1)}, bf16[4,768,128]{2,1,0:T(8,128)(2,1)}, u32[]{:S(2)}) copy-start(bf16[4,768,128]{2,1,0:T(8,128)(2,1)} %param.15) | copy-start | bytes 2359300
  6.5 174.2 %all-gather.2.cloned.1.call-start = ((), (), s32[]{:S(2)}) async-start(), calls=%async_computation.3 | async-start | bytes 5242880 | tf_op jit(solution)/shard_map/all_gather | solution.py:103
  21.2 3.1 %copy-start.11 = (bf16[8,768,256]{2,1,0:T(8,128)(2,1)S(1)}, bf16[8,768,256]{2,1,0:T(8,128)(2,1)}, u32[]{:S(2)}) copy-start(bf16[8,768,256]{2,1,0:T(8,128)(2,1)} %param.11) | copy-start | bytes 9437188
  24.1 0.8 copy-start.26
  24.3 0.8 copy-start.53
  24.3 0.9 copy-start.54
  25.2 0.8 copy-start.27
  25.2 1.0 copy-start.59
  25.3 1.0 copy-start.55
  25.3 1.1 copy-start.56
  26.6 0.8 copy-start.51
  26.6 0.9 copy-start.52
  27.5 0.8 copy-start.23
  27.6 0.8 copy-start.47
  27.6 0.9 copy-start.49
  28.5 0.8 copy-start.21
  28.7 0.8 copy-start.44
  28.7 0.9 copy-start.46
  29.6 0.8 copy-start.17
  29.7 0.8 copy-start.40
  29.7 0.9 copy-start.42
  30.7 0.8 copy-start.15
  30.8 0.8 copy-start.37
  30.8 0.9 copy-start.39
  30.8 1.0 copy-start.57
  30.8 1.2 copy-start.58
  31.7 0.9 copy-start.13
  31.9 0.8 copy-start.33
  31.9 0.9 copy-start.35
  35.1 0.8 copy-start.1
  36.3 0.8 copy-start.3
  37.5 0.8 copy-start.5
  47.2 2.7 %copy-start.28 = (bf16[4,256,128]{2,1,0:T(8,128)(2,1)S(1)}, bf16[4,256,128]{2,1,0:T(8,128)(2,1)}, u32[]{:S(2)}) copy-start(bf16[4,256,128]{2,1,0:T(8,128)(2,1)} %param.14) | copy-start | bytes 786436
  47.2 2.7 %copy-start.30 = (f32[12,64,256]{2,1,0:T(8,128)S(1)}, f32[12,64,256]{2,1,0:T(8,128)}, u32[]{:S(2)}) copy-start(f32[12,64,256]{2,1,0:T(8,128)} %get-tuple-element.8) | copy-start | bytes 2359300
  47.2 2.7 %copy-start.31 = (f32[12,63,256]{2,1,0:T(8,128)S(1)}, f32[12,63,256]{2,1,0:T(8,128)}, u32[]{:S(2)}) copy-start(f32[12,63,256]{2,1,0:T(8,128)} %get-tuple-element.25) | copy-start | bytes 2322436
  47.2 2.7 %copy-start.32 = (f32[12,63,256]{2,1,0:T(8,128)S(1)}, f32[12,63,256]{2,1,0:T(8,128)}, u32[]{:S(2)}) copy-start(f32[12,63,256]{2,1,0:T(8,128)} %get-tuple-element.26) | copy-start | bytes 2322436
  47.2 2.7 %copy-start.60 = (f32[12,64,256]{2,1,0:T(8,128)S(1)}, f32[12,64,256]{2,1,0:T(8,128)}, u32[]{:S(2)}) copy-start(f32[12,64,256]{2,1,0:T(8,128)} %copy-done.59) | copy-start | bytes 2359300
  49.9 1.3 copy-start.10
  52.8 2.7 %copy-start.8 = (bf16[12,64,256]{2,1,0:T(8,128)(2,1)S(1)}, bf16[12,64,256]{2,1,0:T(8,128)(2,1)}, u32[]{:S(2)}) copy-start(bf16[12,64,256]{2,1,0:T(8,128)(2,1)} %copy-done.7) | copy-start | bytes 1179652
  52.8 2.6 %copy-start.29 = (bf16[4,256,128]{2,1,0:T(8,128)(2,1)S(1)}, bf16[4,256,128]{2,1,0:T(8,128)(2,1)}, u32[]{:S(2)}) copy-start(bf16[4,256,128]{2,1,0:T(8,128)(2,1)} %param.14) | copy-start | bytes 786436
  52.8 4.3 %copy-start.24 = (bf16[12,64,256]{2,1,0:T(8,128)(2,1)S(1)}, bf16[12,64,256]{2,1,0:T(8,128)(2,1)}, u32[]{:S(2)}) copy-start(bf16[12,64,256]{2,1,0:T(8,128)(2,1)} %copy-done.23) | copy-start | bytes 1179652
  52.9 4.3 %copy-start.48 = (bf16[12,63,256]{2,1,0:T(8,128)(2,1)S(1)}, bf16[12,63,256]{2,1,0:T(8,128)(2,1)}, u32[]{:S(2)}) copy-start(bf16[12,63,256]{2,1,0:T(8,128)(2,1)} %copy-done.47) | copy-start | bytes 1161220
  52.9 4.3 %copy-start.50 = (bf16[12,63,256]{2,1,0:T(8,128)(2,1)S(1)}, bf16[12,63,256]{2,1,0:T(8,128)(2,1)}, u32[]{:S(2)}) copy-start(bf16[12,63,256]{2,1,0:T(8,128)(2,1)} %copy-done.49) | copy-start | bytes 1161220
  57.2 1.3 copy-start.6
  57.2 2.9 %copy-start.22 = (bf16[12,64,256]{2,1,0:T(8,128)(2,1)S(1)}, bf16[12,64,256]{2,1,0:T(8,128)(2,1)}, u32[]{:S(2)}) copy-start(bf16[12,64,256]{2,1,0:T(8,128)(2,1)} %copy-done.21) | copy-start | bytes 1179652
  57.2 2.9 %copy-start.45 = (bf16[12,63,256]{2,1,0:T(8,128)(2,1)S(1)}, bf16[12,63,256]{2,1,0:T(8,128)(2,1)}, u32[]{:S(2)}) copy-start(bf16[12,63,256]{2,1,0:T(8,128)(2,1)} %copy-done.44) | copy-start | bytes 1161220
  60.2 2.4 %copy-start.4 = (bf16[12,64,256]{2,1,0:T(8,128)(2,1)S(1)}, bf16[12,64,256]{2,1,0:T(8,128)(2,1)}, u32[]{:S(2)}) copy-start(bf16[12,64,256]{2,1,0:T(8,128)(2,1)} %copy-done.3) | copy-start | bytes 1179652
  60.2 4.0 %copy-start.18 = (bf16[12,64,256]{2,1,0:T(8,128)(2,1)S(1)}, bf16[12,64,256]{2,1,0:T(8,128)(2,1)}, u32[]{:S(2)}) copy-start(bf16[12,64,256]{2,1,0:T(8,128)(2,1)} %copy-done.17) | copy-start | bytes 1179652
  60.2 4.0 %copy-start.41 = (bf16[12,63,256]{2,1,0:T(8,128)(2,1)S(1)}, bf16[12,63,256]{2,1,0:T(8,128)(2,1)}, u32[]{:S(2)}) copy-start(bf16[12,63,256]{2,1,0:T(8,128)(2,1)} %copy-done.40) | copy-start | bytes 1161220
  60.2 4.0 %copy-start.43 = (bf16[12,63,256]{2,1,0:T(8,128)(2,1)S(1)}, bf16[12,63,256]{2,1,0:T(8,128)(2,1)}, u32[]{:S(2)}) copy-start(bf16[12,63,256]{2,1,0:T(8,128)(2,1)} %copy-done.42) | copy-start | bytes 1161220
  64.3 1.3 copy-start.2
  64.3 2.9 %copy-start.16 = (bf16[12,64,256]{2,1,0:T(8,128)(2,1)S(1)}, bf16[12,64,256]{2,1,0:T(8,128)(2,1)}, u32[]{:S(2)}) copy-start(bf16[12,64,256]{2,1,0:T(8,128)(2,1)} %copy-done.15) | copy-start | bytes 1179652
  64.3 2.9 %copy-start.38 = (bf16[12,63,256]{2,1,0:T(8,128)(2,1)S(1)}, bf16[12,63,256]{2,1,0:T(8,128)(2,1)}, u32[]{:S(2)}) copy-start(bf16[12,63,256]{2,1,0:T(8,128)(2,1)} %copy-done.37) | copy-start | bytes 1161220
  67.2 4.0 %copy-start.14 = (bf16[12,64,256]{2,1,0:T(8,128)(2,1)S(1)}, bf16[12,64,256]{2,1,0:T(8,128)(2,1)}, u32[]{:S(2)}) copy-start(bf16[12,64,256]{2,1,0:T(8,128)(2,1)} %copy-done.13) | copy-start | bytes 1179652
  67.2 4.0 %copy-start.34 = (bf16[12,63,256]{2,1,0:T(8,128)(2,1)S(1)}, bf16[12,63,256]{2,1,0:T(8,128)(2,1)}, u32[]{:S(2)}) copy-start(bf16[12,63,256]{2,1,0:T(8,128)(2,1)} %copy-done.33) | copy-start | bytes 1161220
  67.2 4.0 %copy-start.36 = (bf16[12,63,256]{2,1,0:T(8,128)(2,1)S(1)}, bf16[12,63,256]{2,1,0:T(8,128)(2,1)}, u32[]{:S(2)}) copy-start(bf16[12,63,256]{2,1,0:T(8,128)(2,1)} %copy-done.35) | copy-start | bytes 1161220
  71.2 1.3 copy-start.20
  147.1 13.8 %collective-permute-start.2 = (bf16[64,4096]{1,0:T(8,128)(2,1)S(1)}, bf16[64,4096]{1,0:T(8,128)(2,1)S(1)}, u32[]{:S(2)}, u32[]{:S(2)}) collective-permute-start(bf16[64,4096]{1,0:T(8,128)(2,1)S(1)} %reshape.80), channel_id=1, source_target_pairs={{0,96},{32,0},{64,32},{96,64},{1,97},{33,1},{65,33},{97,65},{2,98}... | collective-permute-start | bytes 1572872 | tf_op jit(solution)/shard_map/ppermute | solution.py:110
  149.9 15.2 %collective-permute-start = (bf16[64,4096]{1,0:T(8,128)(2,1)S(1)}, bf16[64,4096]{1,0:T(8,128)(2,1)S(1)}, u32[]{:S(2)}, u32[]{:S(2)}) collective-permute-start(bf16[64,4096]{1,0:T(8,128)(2,1)S(1)} %reshape.80), channel_id=1, source_target_pairs={{0,32},{32,64},{64,96},{96,0},{1,33},{33,65},{65,97},{97,1},{2,34}... | collective-permute-start | bytes 1572872 | tf_op jit(solution)/shard_map/ppermute | solution.py:109
  161.6 8.4 %collective-permute-start.3 = (bf16[32,4096]{1,0:T(8,128)(2,1)}, bf16[32,4096]{1,0:T(8,128)(2,1)}, u32[]{:S(2)}, u32[]{:S(2)}) collective-permute-start(bf16[32,4096]{1,0:T(8,128)(2,1)} %slice.345), channel_id=1, source_target_pairs={{0,96},{32,0},{64,32},{96,64},{1,97},{33,1},{65,33},{97,65},{2,98}... | collective-permute-start | bytes 786440 | tf_op jit(solution)/shard_map/ppermute | solution.py:113
  165.8 8.0 %collective-permute-start.1 = (bf16[32,4096]{1,0:T(8,128)(2,1)}, bf16[32,4096]{1,0:T(8,128)(2,1)}, u32[]{:S(2)}, u32[]{:S(2)}) collective-permute-start(bf16[32,4096]{1,0:T(8,128)(2,1)} %slice.344), channel_id=1, source_target_pairs={{0,32},{32,64},{64,96},{96,0},{1,33},{33,65},{65,97},{97,1},{2,34}... | collective-permute-start | bytes 786440 | tf_op jit(solution)/shard_map/ppermute | solution.py:112
  180.7 2.9 %copy-start.12 = (bf16[4,64,4096,1]{2,1,0,3:T(8,128)(2,1)S(1)}, bf16[4,64,4096,1]{2,1,0,3:T(8,128)(2,1)}, u32[]{:S(2)}) copy-start(bf16[4,64,4096,1]{2,1,0,3:T(8,128)(2,1)} %reshape.127) | copy-start | bytes 6291460
  185.0 3.5 %collective-permute-start.4 = (f32[2,4,64,128]{3,2,1,0:T(8,128)S(1)}, f32[2,4,64,128]{3,2,1,0:T(8,128)S(1)}, u32[]{:S(2)}, u32[]{:S(2)}) collective-permute-start(f32[2,4,64,128]{3,2,1,0:T(8,128)S(1)} %bitcast.281), channel_id=1, source_target_pairs={{0,16},{16,0},{1,17},{17,1},{2,18},{18,2},{3,19},{19,3},{4,20},{20... | collective-permute-start | bytes 786440 | tf_op jit(solution)/shard_map/ppermute | solution.py:128
  189.2 16.8 %all-to-all-start.2 = ((f32[8,64,128]{2,1,0:T(8,128)}), f32[8,64,128]{2,1,0:T(8,128)S(1)}, u32[]{:S(2)}, u32[]{:S(2)}) async-start(f32[8,64,128]{2,1,0:T(8,128)} %bitcast.105), calls=%async_computation.2 | async-start | bytes 524288 | tf_op jit(solution)/shard_map/all_to_all | solution.py:130
  (4 other events, 3.0 us)
Sparse Core Ops, SparseCore 0:
  126.4 50.1 all-gather.1

commit v10 on v9

--- a/solution.py
+++ b/solution.py
@@ -126,8 +126,12 @@
     for_partner = lax.dynamic_index_in_dim(chunks, 1 - mine, axis=1, keepdims=False)
     kept = lax.dynamic_index_in_dim(chunks, mine, axis=1, keepdims=False)
     paired = kept + lax.ppermute(for_partner, "core", swap)
-    paired = paired.reshape(n_zh * n_col, paired.shape[2], paired.shape[3])
-    received = lax.all_to_all(paired, ("zh", "col"), split_axis=0, concat_axis=0, tiled=True)
+    high = lax.axis_index("zh")
+    halves = [(j, (j + 1) % n_zh) for j in range(n_zh)]
+    for_far = lax.dynamic_index_in_dim(paired, 1 - high, axis=0, keepdims=False)
+    near = lax.dynamic_index_in_dim(paired, high, axis=0, keepdims=False)
+    quads = near + lax.ppermute(for_far, "zh", halves)
+    received = lax.all_to_all(quads, "col", split_axis=0, concat_axis=0, tiled=True)
     block = jnp.sum(received, axis=0).T
     block = block.reshape(block.shape[0], n_zh, n_y, n_core * right_each)
     block = jnp.roll(block, lax.axis_index("y") - 2, axis=2)

time: 215 us -> 220 us (1.023)
  starting transfers between devices: 14.4 us -> 21.3 us
    all_to_all x1, waiting for transfers between devices: 11.1 us -> 4.77 us  [on_device(): lax.all_to_all(quads, 'col', split_axis=0, concat_axis=0, tiled=True)]
    ppermute x0 -> x1, starting transfers between devices: none -> 4.49 us  [on_device(): quads = near + lax.ppermute(for_far, 'zh', halves)]
    ppermute x0 -> x1, waiting for transfers between devices: none -> 4.18 us  [on_device(): quads = near + lax.ppermute(for_far, 'zh', halves)]
    all_to_all x1, starting transfers between devices: 5.68 us -> 8.07 us  [on_device(): lax.all_to_all(quads, 'col', split_axis=0, concat_axis=0, tiled=True)]
  transfers between devices with their start and end apart: 7 -> 8, of which waited for: 5 -> 6; matrix products, arithmetic and copies ran while one was open for 4% -> 4% of each run, Pallas kernels for 0% -> 0%
where the time goes in v10:
time: 220 us; the launch traced here: 218 us
  blocking collectives  55.5 us (25%)
  matrix products  42.4 us (19%)
  local copies, waits for them, and re-layouts  31.8 us (14%)
  between operations  29.3 us (13%)
  waiting for transfers between devices  28.6 us (13%)
  starting transfers between devices  21.3 us (10%)
  other arithmetic  9.16 us (4%)
    all_to_all x1, blocking collectives, on_device(): lax.all_to_all(sliced[:left_each], group, split_axis=1, concat_axis=0, ti...  35.6 us
    all_to_all x1, blocking collectives, on_device(): lax.all_to_all(right_sliced, group, split_axis=1, concat_axis=0, tiled=True)  20 us
    dot_general x8, matrix products, panels(): jnp.einsum('esk,kt->est', wides[layer], proj_input[assign[layer]], prefer...  16.1 us
    ppermute x1, waiting for transfers between devices, on_device(): from_above = lax.ppermute(right_part, 'y', down)  10.9 us
    dot_general x8, matrix products, panels(): jnp.einsum('esc,cr->esr', delta_low, proj_delta[assign[layer]], preferred...  8.43 us
    all_to_all x1, starting transfers between devices, on_device(): lax.all_to_all(quads, 'col', split_axis=0, concat_axis=0, tiled=True)  8.07 us
    dot_general x1, matrix products, panels(): jnp.einsum('bjesr,bjest->ebrt', delta_stack, input_stack, precision=lax.P...  5.48 us
    all_to_all x1, waiting for transfers between devices, on_device(): lax.all_to_all(quads, 'col', split_axis=0, concat_axis=0, tiled=True)  4.77 us
  transfers between devices with their start and end apart: 8, of which 6 were waited for; matrix products, arithmetic and copies ran while one was open for 4% of the time, Pallas kernels for 0%

profile of v10, /device:TPU:1, one launch (start us, length us, event | category | flops | bytes accessed | tf_op | source)
XLA Modules:
  0.0 218.2 jit_solution(12878166289278092639)
XLA Ops:
  6.5 1.6 fusion.234
  18.1 0.9 convert_reduce_fusion
  19.0 0.8 copy.48
  19.9 0.8 copy.34
  21.2 2.9 %fusion.235 = (bf16[12,64,256]{2,1,0:T(8,128)(2,1)S(1)}, f32[12,64,256]{2,1,0:T(8,128)S(1)}) fusion(bf16[1024,256]{1,0:T(8,128)(2,1)} %param.10, s32[12,64]{1,0:T(8,128)S(1)} %bitcast.285, s32[12,64]{1,0:T(8,128)S(1)} %bitcast.286, s32[12,64]{1,0:T(8,128)S(1)} %bitcast.287, s32[12,64]{1,0:T(8,128)S(1)} %bitcast.288), kind=kOutput, calls=%fused_computation.275 | convolution fusion | flops 415432704 | bytes 1716224 | tf_op jit(solution)/shard_map/esv,vc->esc/dot_general | solution.py:30
  24.3 0.5 fusion.206
  25.3 0.7 fusion.217
  26.6 0.5 fusion.207
  27.6 0.7 fusion.216
  28.7 0.5 fusion.208
  29.7 0.7 fusion.215
  30.8 0.5 add_convert_fusion
  32.1 0.6 multiply_convert_fusion.6
  33.9 0.5 fusion.95
  35.1 0.5 fusion.99
  38.3 0.6 multiply_convert_fusion.1
  39.6 1.3 multiply_convert_fusion
  40.9 0.7 copy-done.9
  42.2 1.3 fusion.218
  44.0 2.5 %fusion.48 = f32[8,12,64,128]{3,2,1,0:T(8,128)} fusion(bf16[4,768,128]{2,1,0:T(8,128)(2,1)S(1)} %copy-done, s32[]{:T(128)S(6)} %select_n.74, bf16[12,63,256]{2,1,0:T(8,128)(2,1)} %copy-done.54, bf16[12,63,256]{2,1,0:T(8,128)(2,1)} %copy-done.53, bf16[12,64,256]{2,1,0:T(8,128)(2,1)} %copy-done.26), kind=kOutput, calls=%fused_computation.58 | convolution fusion | flops 156893184 | bytes 1757188 | tf_op jit(solution)/shard_map/esk,kt->est/dot_general | solution.py:51
  47.2 2.6 %fusion.47 = f32[8,12,64,128]{3,2,1,0:T(8,128)} fusion(f32[8,12,64,128]{3,2,1,0:T(8,128)} %fusion.48, bf16[4,768,128]{2,1,0:T(8,128)(2,1)S(1)} %copy-done, s32[]{:T(128)S(6)} %select_n.75, bf16[12,63,256]{2,1,0:T(8,128)(2,1)} %copy-done.56, bf16[12,63,256]{2,1,0:T(8,128)(2,1)} %copy-done.55, bf16[12,64,256]{2,1,0:T(8,128)(2,1)} %copy-done.27), kind=kOutput, calls=%fused_computation.56 | convolution fusion | flops 156893184 | bytes 1769476 | tf_op jit(solution)/shard_map/esk,kt->est/dot_general | solution.py:51
  49.9 1.3 fusion.56
  51.2 1.0 fusion.55
  52.9 2.6 %fusion.46 = f32[8,12,64,128]{3,2,1,0:T(8,128)} fusion(f32[8,12,64,128]{3,2,1,0:T(8,128)} %fusion.47, bf16[4,768,128]{2,1,0:T(8,128)(2,1)S(1)} %copy-done, s32[]{:T(128)S(6)} %select_n.76, bf16[12,63,256]{2,1,0:T(8,128)(2,1)} %copy-done.52, bf16[12,63,256]{2,1,0:T(8,128)(2,1)} %copy-done.51, bf16[12,64,256]{2,1,0:T(8,128)(2,1)} %copy-done.25), kind=kOutput, calls=%fused_computation.54 | convolution fusion | flops 156893184 | bytes 1769476 | tf_op jit(solution)/shard_map/esk,kt->est/dot_general | solution.py:51
  55.5 1.0 fusion.54
  57.3 1.2 fusion.45
  58.5 1.0 fusion.53
  60.2 2.4 %fusion.44 = f32[8,12,64,128]{3,2,1,0:T(8,128)} fusion(f32[8,12,64,128]{3,2,1,0:T(8,128)} %fusion.45, bf16[4,768,128]{2,1,0:T(8,128)(2,1)S(1)} %copy-done, s32[]{:T(128)S(6)} %select_n.78, bf16[12,63,256]{2,1,0:T(8,128)(2,1)} %copy-done.46, bf16[12,63,256]{2,1,0:T(8,128)(2,1)S(1)} %copy-done.45, bf16[12,64,256]{2,1,0:T(8,128)(2,1)S(1)} %copy-done.22), kind=kOutput, calls=%fused_computation.50 | convolution fusion | flops 156893184 | bytes 1769476 | tf_op jit(solution)/shard_map/esk,kt->est/dot_general | solution.py:51
  62.6 1.0 fusion.52
  64.3 1.3 fusion.43
  65.6 1.0 fusion.51
  67.2 2.3 %fusion.42 = f32[8,12,64,128]{3,2,1,0:T(8,128)} fusion(f32[8,12,64,128]{3,2,1,0:T(8,128)} %fusion.43, bf16[4,768,128]{2,1,0:T(8,128)(2,1)S(1)} %copy-done, s32[]{:T(128)S(6)} %select_n.80, bf16[12,63,256]{2,1,0:T(8,128)(2,1)} %copy-done.39, bf16[12,63,256]{2,1,0:T(8,128)(2,1)S(1)} %copy-done.38, bf16[12,64,256]{2,1,0:T(8,128)(2,1)S(1)} %copy-done.16), kind=kOutput, calls=%fused_computation.46 | convolution fusion | flops 156893184 | bytes 1769476 | tf_op jit(solution)/shard_map/esk,kt->est/dot_general | solution.py:51
  69.5 1.0 fusion.50
  71.2 1.2 fusion.41
  72.5 1.0 fusion.49
  73.5 4.3 %gather_fusion.1 = f32[8,12,64,128]{3,2,1,0:T(8,128)} fusion(f32[8,12,64,128]{3,2,1,0:T(8,128)} %fusion.41, s32[1024]{0:T(1024)S(1)} %pad_clamp_fusion), kind=kCustom, calls=%fused_computation.1 | custom fusion | bytes 6291488 | tf_op jit(solution)/shard_map/gather | solution.py:75
  77.8 4.3 %gather_fusion = f32[8,12,64,128]{3,2,1,0:T(8,128)} fusion(f32[8,12,64,128]{3,2,1,0:T(8,128)} %fusion.49, s32[1024]{0:T(1024)S(1)} %pad_clamp_fusion), kind=kCustom, calls=%fused_computation | custom fusion | bytes 6291488 | tf_op jit(solution)/shard_map/gather | solution.py:74
  82.1 5.5 %bitcast_convert_fusion = bf16[12,4,128,128]{3,2,1,0:T(8,128)(2,1)S(1)} fusion(f32[4,2,12,64,128]{4,3,2,1,0:T(8,128)} %bitcast.273, f32[4,2,12,64,128]{4,3,2,1,0:T(8,128)} %bitcast.274), kind=kOutput, calls=%fused_computation.2 | convolution fusion | flops 604766208 | bytes 7864320 | tf_op jit(solution)/shard_map/bjesr,bjest->ebrt/dot_general | solution.py:79
  87.5 1.0 slice.342
  88.6 1.5 slice.292
  90.1 0.6 copy.42
  90.7 35.6 %all_to_all.35 = bf16[8,16,4096]{2,0,1:T(8,128)(2,1)} all-to-all(bf16[8,16,4096]{2,0,1:T(8,128)(2,1)S(1)} %copy.42), channel_id=1, replica_groups=mesh['zh'=2,'y'=4,'core'=2,'col'=4,'pblk'=4] {'zh','core','col'}, dimensions={1} | all-to-all | bytes 2097152 | tf_op jit(solution)/shard_map/all_to_all | solution.py:101
  127.0 20.0 %all_to_all.36 = bf16[4,16,4096]{2,0,1:T(4,128)(2,1)S(1)} all-to-all(bf16[4,16,4096]{2,0,1:T(4,128)(2,1)S(1)} %copy.43), channel_id=1, replica_groups=mesh['zh'=2,'y'=4,'core'=2,'col'=4,'pblk'=4] {'zh','core','col'}, dimensions={1} | all-to-all | bytes 1048576 | tf_op jit(solution)/shard_map/all_to_all | solution.py:105
  147.1 2.8 %collective-permute-start.2 = (bf16[64,4096]{1,0:T(8,128)(2,1)S(1)}, bf16[64,4096]{1,0:T(8,128)(2,1)S(1)}, u32[]{:S(2)}, u32[]{:S(2)}) collective-permute-start(bf16[64,4096]{1,0:T(8,128)(2,1)S(1)} %reshape.77), channel_id=1, source_target_pairs={{0,96},{32,0},{64,32},{96,64},{1,97},{33,1},{65,33},{97,65},{2,98}... | collective-permute-start | bytes 1572872 | tf_op jit(solution)/shard_map/ppermute | solution.py:110
  149.9 10.9 %collective-permute-done.2 = bf16[64,4096]{1,0:T(8,128)(2,1)S(1)} collective-permute-done((bf16[64,4096]{1,0:T(8,128)(2,1)S(1)}, bf16[64,4096]{1,0:T(8,128)(2,1)S(1)}, u32[]{:S(2)}, u32[]{:S(2)}) %collective-permute-start.2) | collective-permute-done | bytes 524320 | tf_op jit(solution)/shard_map/ppermute | solution.py:110
  160.8 0.7 slice.345
  161.6 3.5 %collective-permute-start.3 = (bf16[32,4096]{1,0:T(8,128)(2,1)}, bf16[32,4096]{1,0:T(8,128)(2,1)}, u32[]{:S(2)}, u32[]{:S(2)}) collective-permute-start(bf16[32,4096]{1,0:T(8,128)(2,1)} %slice.345), channel_id=1, source_target_pairs={{0,96},{32,0},{64,32},{96,64},{1,97},{33,1},{65,33},{97,65},{2,98}... | collective-permute-start | bytes 786440 | tf_op jit(solution)/shard_map/ppermute | solution.py:113
  165.1 0.7 slice.344
  166.2 3.7 %collective-permute-done.3 = bf16[32,4096]{1,0:T(8,128)(2,1)} collective-permute-done((bf16[32,4096]{1,0:T(8,128)(2,1)}, bf16[32,4096]{1,0:T(8,128)(2,1)}, u32[]{:S(2)}, u32[]{:S(2)}) %collective-permute-start.3) | collective-permute-done | bytes 262176 | tf_op jit(solution)/shard_map/ppermute | solution.py:113
  169.9 3.9 %collective-permute-done.1 = bf16[32,4096]{1,0:T(8,128)(2,1)} collective-permute-done((bf16[32,4096]{1,0:T(8,128)(2,1)}, bf16[32,4096]{1,0:T(8,128)(2,1)}, u32[]{:S(2)}, u32[]{:S(2)}) %collective-permute-start.1) | collective-permute-done | bytes 262176 | tf_op jit(solution)/shard_map/ppermute | solution.py:112
  173.8 1.1 pad_maximum_fusion
  175.1 2.0 maximum_bitcast_fusion
  177.0 1.6 copy.44
  178.6 2.2 reshape.123
  180.7 2.6 %copy.45 = bf16[4,4,4,8,4096]{4,3,2,1,0:T(8,128)(2,1)S(1)} copy(bf16[4,4,4,8,4096]{4,3,1,0,2:T(8,128)(2,1)} %bitcast.277) | data formatting | bytes 8388608 | tf_op jit(solution)/shard_map/transpose | solution.py:117
  183.6 1.3 fusion.23
  184.9 2.4 %collective-permute-start.4 = (f32[2,4,64,128]{3,2,0,1:T(8,128)S(1)}, f32[2,4,64,128]{3,2,0,1:T(8,128)S(1)}, u32[]{:S(2)}, u32[]{:S(2)}) collective-permute-start(f32[2,4,64,128]{3,2,0,1:T(8,128)S(1)} %dynamic-slice_bitcast_fusion), channel_id=1, source_target_pairs={{0,16},{16,0},{1,17},{17,1},{2,18},{18,2},{3,19},{19,3},{4,20},{20... | collective-permute-start | bytes 786440 | tf_op jit(solution)/shard_map/ppermute | solution.py:128
  187.3 1.2 collective-permute-done.4
  188.5 4.5 %collective-permute-start.5 = (f32[4,64,128]{2,1,0:T(8,128)S(1)}, f32[4,64,128]{2,1,0:T(8,128)S(1)}, u32[]{:S(2)}, u32[]{:S(2)}) collective-permute-start(f32[4,64,128]{2,1,0:T(8,128)S(1)} %dynamic-slice_bitcast_fusion.1), channel_id=1, source_target_pairs={{0,128},{128,0},{1,129},{129,1},{2,130},{130,2},{3,131},{131,3},{4... | collective-permute-start | bytes 393224 | tf_op jit(solution)/shard_map/ppermute | solution.py:133
  193.0 4.2 %collective-permute-done.5 = f32[4,64,128]{2,1,0:T(8,128)S(1)} collective-permute-done((f32[4,64,128]{2,1,0:T(8,128)S(1)}, f32[4,64,128]{2,1,0:T(8,128)S(1)}, u32[]{:S(2)}, u32[]{:S(2)}) %collective-permute-start.5) | collective-permute-done | bytes 131104 | tf_op jit(solution)/shard_map/ppermute | solution.py:133
  197.2 0.7 bitcast_add_fusion.1
  197.8 8.1 %all-to-all-start.2 = ((f32[4,64,128]{2,1,0:T(8,128)}), f32[4,64,128]{2,1,0:T(8,128)S(1)}, u32[]{:S(2)}, u32[]{:S(2)}) async-start(f32[4,64,128]{2,1,0:T(8,128)} %bitcast_add_fusion.1), calls=%async_computation.2 | async-start | bytes 262144 | tf_op jit(solution)/shard_map/all_to_all | solution.py:134
  205.9 4.8 %all-to-all-done.2 = f32[4,64,128]{2,1,0:T(8,128)S(1)} async-done(((f32[4,64,128]{2,1,0:T(8,128)}), f32[4,64,128]{2,1,0:T(8,128)S(1)}, u32[]{:S(2)}, u32[]{:S(2)}) %all-to-all-start.2) | async-done | bytes 131104 | tf_op jit(solution)/shard_map/all_to_all | solution.py:134
  210.7 0.6 fusion.169
  (173 shorter events, 11.6 us)
Async XLA Ops:
  6.5 37.5 %copy-start = (bf16[4,768,128]{2,1,0:T(8,128)(2,1)S(1)}, bf16[4,768,128]{2,1,0:T(8,128)(2,1)}, u32[]{:S(2)}) copy-start(bf16[4,768,128]{2,1,0:T(8,128)(2,1)} %param.15) | copy-start | bytes 2359300
  6.5 174.2 %all-gather.2.cloned.1.call-start = ((), (), s32[]{:S(2)}) async-start(), calls=%async_computation.3 | async-start | bytes 5242880 | tf_op jit(solution)/shard_map/all_gather | solution.py:103
  21.2 3.1 %copy-start.11 = (bf16[8,768,256]{2,1,0:T(8,128)(2,1)S(1)}, bf16[8,768,256]{2,1,0:T(8,128)(2,1)}, u32[]{:S(2)}) copy-start(bf16[8,768,256]{2,1,0:T(8,128)(2,1)} %param.11) | copy-start | bytes 9437188
  24.1 0.8 copy-start.26
  24.3 0.8 copy-start.53
  24.3 0.9 copy-start.54
  25.2 0.8 copy-start.27
  25.2 1.0 copy-start.59
  25.3 1.0 copy-start.55
  25.3 1.1 copy-start.56
  26.6 0.8 copy-start.51
  26.6 0.9 copy-start.52
  27.5 0.8 copy-start.23
  27.6 0.9 copy-start.49
  28.5 0.8 copy-start.21
  28.7 0.8 copy-start.44
  28.7 0.9 copy-start.46
  29.6 0.8 copy-start.17
  29.7 0.8 copy-start.40
  29.7 0.9 copy-start.42
  30.7 0.8 copy-start.15
  30.8 0.8 copy-start.37
  30.8 0.9 copy-start.39
  30.8 1.0 copy-start.57
  30.8 1.2 copy-start.58
  31.7 0.9 copy-start.13
  31.9 0.8 copy-start.33
  31.9 0.9 copy-start.35
  35.1 0.8 copy-start.1
  36.3 0.8 copy-start.3
  37.5 0.8 copy-start.5
  47.2 2.7 %copy-start.28 = (bf16[4,256,128]{2,1,0:T(8,128)(2,1)S(1)}, bf16[4,256,128]{2,1,0:T(8,128)(2,1)}, u32[]{:S(2)}) copy-start(bf16[4,256,128]{2,1,0:T(8,128)(2,1)} %param.14) | copy-start | bytes 786436
  47.2 2.7 %copy-start.30 = (f32[12,64,256]{2,1,0:T(8,128)S(1)}, f32[12,64,256]{2,1,0:T(8,128)}, u32[]{:S(2)}) copy-start(f32[12,64,256]{2,1,0:T(8,128)} %get-tuple-element.8) | copy-start | bytes 2359300
  47.2 2.7 %copy-start.31 = (f32[12,63,256]{2,1,0:T(8,128)S(1)}, f32[12,63,256]{2,1,0:T(8,128)}, u32[]{:S(2)}) copy-start(f32[12,63,256]{2,1,0:T(8,128)} %get-tuple-element.25) | copy-start | bytes 2322436
  47.2 2.7 %copy-start.32 = (f32[12,63,256]{2,1,0:T(8,128)S(1)}, f32[12,63,256]{2,1,0:T(8,128)}, u32[]{:S(2)}) copy-start(f32[12,63,256]{2,1,0:T(8,128)} %get-tuple-element.26) | copy-start | bytes 2322436
  47.2 2.7 %copy-start.60 = (f32[12,64,256]{2,1,0:T(8,128)S(1)}, f32[12,64,256]{2,1,0:T(8,128)}, u32[]{:S(2)}) copy-start(f32[12,64,256]{2,1,0:T(8,128)} %copy-done.59) | copy-start | bytes 2359300
  49.9 1.3 copy-start.10
  52.8 2.7 %copy-start.8 = (bf16[12,64,256]{2,1,0:T(8,128)(2,1)S(1)}, bf16[12,64,256]{2,1,0:T(8,128)(2,1)}, u32[]{:S(2)}) copy-start(bf16[12,64,256]{2,1,0:T(8,128)(2,1)} %copy-done.7) | copy-start | bytes 1179652
  52.8 2.6 %copy-start.29 = (bf16[4,256,128]{2,1,0:T(8,128)(2,1)S(1)}, bf16[4,256,128]{2,1,0:T(8,128)(2,1)}, u32[]{:S(2)}) copy-start(bf16[4,256,128]{2,1,0:T(8,128)(2,1)} %param.14) | copy-start | bytes 786436
  52.8 4.3 %copy-start.24 = (bf16[12,64,256]{2,1,0:T(8,128)(2,1)S(1)}, bf16[12,64,256]{2,1,0:T(8,128)(2,1)}, u32[]{:S(2)}) copy-start(bf16[12,64,256]{2,1,0:T(8,128)(2,1)} %copy-done.23) | copy-start | bytes 1179652
  52.9 4.3 %copy-start.48 = (bf16[12,63,256]{2,1,0:T(8,128)(2,1)S(1)}, bf16[12,63,256]{2,1,0:T(8,128)(2,1)}, u32[]{:S(2)}) copy-start(bf16[12,63,256]{2,1,0:T(8,128)(2,1)} %copy-done.47) | copy-start | bytes 1161220
  52.9 4.3 %copy-start.50 = (bf16[12,63,256]{2,1,0:T(8,128)(2,1)S(1)}, bf16[12,63,256]{2,1,0:T(8,128)(2,1)}, u32[]{:S(2)}) copy-start(bf16[12,63,256]{2,1,0:T(8,128)(2,1)} %copy-done.49) | copy-start | bytes 1161220
  57.2 1.3 copy-start.6
  57.2 2.9 %copy-start.22 = (bf16[12,64,256]{2,1,0:T(8,128)(2,1)S(1)}, bf16[12,64,256]{2,1,0:T(8,128)(2,1)}, u32[]{:S(2)}) copy-start(bf16[12,64,256]{2,1,0:T(8,128)(2,1)} %copy-done.21) | copy-start | bytes 1179652
  57.2 2.9 %copy-start.45 = (bf16[12,63,256]{2,1,0:T(8,128)(2,1)S(1)}, bf16[12,63,256]{2,1,0:T(8,128)(2,1)}, u32[]{:S(2)}) copy-start(bf16[12,63,256]{2,1,0:T(8,128)(2,1)} %copy-done.44) | copy-start | bytes 1161220
  60.2 2.4 %copy-start.4 = (bf16[12,64,256]{2,1,0:T(8,128)(2,1)S(1)}, bf16[12,64,256]{2,1,0:T(8,128)(2,1)}, u32[]{:S(2)}) copy-start(bf16[12,64,256]{2,1,0:T(8,128)(2,1)} %copy-done.3) | copy-start | bytes 1179652
  60.2 4.0 %copy-start.18 = (bf16[12,64,256]{2,1,0:T(8,128)(2,1)S(1)}, bf16[12,64,256]{2,1,0:T(8,128)(2,1)}, u32[]{:S(2)}) copy-start(bf16[12,64,256]{2,1,0:T(8,128)(2,1)} %copy-done.17) | copy-start | bytes 1179652
  60.2 4.0 %copy-start.41 = (bf16[12,63,256]{2,1,0:T(8,128)(2,1)S(1)}, bf16[12,63,256]{2,1,0:T(8,128)(2,1)}, u32[]{:S(2)}) copy-start(bf16[12,63,256]{2,1,0:T(8,128)(2,1)} %copy-done.40) | copy-start | bytes 1161220
  60.2 4.0 %copy-start.43 = (bf16[12,63,256]{2,1,0:T(8,128)(2,1)S(1)}, bf16[12,63,256]{2,1,0:T(8,128)(2,1)}, u32[]{:S(2)}) copy-start(bf16[12,63,256]{2,1,0:T(8,128)(2,1)} %copy-done.42) | copy-start | bytes 1161220
  64.3 1.3 copy-start.2
  64.3 2.9 %copy-start.16 = (bf16[12,64,256]{2,1,0:T(8,128)(2,1)S(1)}, bf16[12,64,256]{2,1,0:T(8,128)(2,1)}, u32[]{:S(2)}) copy-start(bf16[12,64,256]{2,1,0:T(8,128)(2,1)} %copy-done.15) | copy-start | bytes 1179652
  64.3 2.9 %copy-start.38 = (bf16[12,63,256]{2,1,0:T(8,128)(2,1)S(1)}, bf16[12,63,256]{2,1,0:T(8,128)(2,1)}, u32[]{:S(2)}) copy-start(bf16[12,63,256]{2,1,0:T(8,128)(2,1)} %copy-done.37) | copy-start | bytes 1161220
  67.2 4.0 %copy-start.14 = (bf16[12,64,256]{2,1,0:T(8,128)(2,1)S(1)}, bf16[12,64,256]{2,1,0:T(8,128)(2,1)}, u32[]{:S(2)}) copy-start(bf16[12,64,256]{2,1,0:T(8,128)(2,1)} %copy-done.13) | copy-start | bytes 1179652
  67.2 4.0 %copy-start.34 = (bf16[12,63,256]{2,1,0:T(8,128)(2,1)S(1)}, bf16[12,63,256]{2,1,0:T(8,128)(2,1)}, u32[]{:S(2)}) copy-start(bf16[12,63,256]{2,1,0:T(8,128)(2,1)} %copy-done.33) | copy-start | bytes 1161220
  67.2 4.0 %copy-start.36 = (bf16[12,63,256]{2,1,0:T(8,128)(2,1)S(1)}, bf16[12,63,256]{2,1,0:T(8,128)(2,1)}, u32[]{:S(2)}) copy-start(bf16[12,63,256]{2,1,0:T(8,128)(2,1)} %copy-done.35) | copy-start | bytes 1161220
  71.2 1.3 copy-start.20
  147.1 13.8 %collective-permute-start.2 = (bf16[64,4096]{1,0:T(8,128)(2,1)S(1)}, bf16[64,4096]{1,0:T(8,128)(2,1)S(1)}, u32[]{:S(2)}, u32[]{:S(2)}) collective-permute-start(bf16[64,4096]{1,0:T(8,128)(2,1)S(1)} %reshape.77), channel_id=1, source_target_pairs={{0,96},{32,0},{64,32},{96,64},{1,97},{33,1},{65,33},{97,65},{2,98}... | collective-permute-start | bytes 1572872 | tf_op jit(solution)/shard_map/ppermute | solution.py:110
  149.9 15.2 %collective-permute-start = (bf16[64,4096]{1,0:T(8,128)(2,1)S(1)}, bf16[64,4096]{1,0:T(8,128)(2,1)S(1)}, u32[]{:S(2)}, u32[]{:S(2)}) collective-permute-start(bf16[64,4096]{1,0:T(8,128)(2,1)S(1)} %reshape.77), channel_id=1, source_target_pairs={{0,32},{32,64},{64,96},{96,0},{1,33},{33,65},{65,97},{97,1},{2,34}... | collective-permute-start | bytes 1572872 | tf_op jit(solution)/shard_map/ppermute | solution.py:109
  161.6 8.4 %collective-permute-start.3 = (bf16[32,4096]{1,0:T(8,128)(2,1)}, bf16[32,4096]{1,0:T(8,128)(2,1)}, u32[]{:S(2)}, u32[]{:S(2)}) collective-permute-start(bf16[32,4096]{1,0:T(8,128)(2,1)} %slice.345), channel_id=1, source_target_pairs={{0,96},{32,0},{64,32},{96,64},{1,97},{33,1},{65,33},{97,65},{2,98}... | collective-permute-start | bytes 786440 | tf_op jit(solution)/shard_map/ppermute | solution.py:113
  165.8 8.0 %collective-permute-start.1 = (bf16[32,4096]{1,0:T(8,128)(2,1)}, bf16[32,4096]{1,0:T(8,128)(2,1)}, u32[]{:S(2)}, u32[]{:S(2)}) collective-permute-start(bf16[32,4096]{1,0:T(8,128)(2,1)} %slice.344), channel_id=1, source_target_pairs={{0,32},{32,64},{64,96},{96,0},{1,33},{33,65},{65,97},{97,1},{2,34}... | collective-permute-start | bytes 786440 | tf_op jit(solution)/shard_map/ppermute | solution.py:112
  180.7 2.9 %copy-start.12 = (bf16[4,64,4096,1]{2,1,0,3:T(8,128)(2,1)S(1)}, bf16[4,64,4096,1]{2,1,0,3:T(8,128)(2,1)}, u32[]{:S(2)}) copy-start(bf16[4,64,4096,1]{2,1,0,3:T(8,128)(2,1)} %reshape.123) | copy-start | bytes 6291460
  184.9 3.5 %collective-permute-start.4 = (f32[2,4,64,128]{3,2,0,1:T(8,128)S(1)}, f32[2,4,64,128]{3,2,0,1:T(8,128)S(1)}, u32[]{:S(2)}, u32[]{:S(2)}) collective-permute-start(f32[2,4,64,128]{3,2,0,1:T(8,128)S(1)} %dynamic-slice_bitcast_fusion), channel_id=1, source_target_pairs={{0,16},{16,0},{1,17},{17,1},{2,18},{18,2},{3,19},{19,3},{4,20},{20... | collective-permute-start | bytes 786440 | tf_op jit(solution)/shard_map/ppermute | solution.py:128
  188.5 8.7 %collective-permute-start.5 = (f32[4,64,128]{2,1,0:T(8,128)S(1)}, f32[4,64,128]{2,1,0:T(8,128)S(1)}, u32[]{:S(2)}, u32[]{:S(2)}) collective-permute-start(f32[4,64,128]{2,1,0:T(8,128)S(1)} %dynamic-slice_bitcast_fusion.1), channel_id=1, source_target_pairs={{0,128},{128,0},{1,129},{129,1},{2,130},{130,2},{3,131},{131,3},{4... | collective-permute-start | bytes 393224 | tf_op jit(solution)/shard_map/ppermute | solution.py:133
  197.8 12.8 %all-to-all-start.2 = ((f32[4,64,128]{2,1,0:T(8,128)}), f32[4,64,128]{2,1,0:T(8,128)S(1)}, u32[]{:S(2)}, u32[]{:S(2)}) async-start(f32[4,64,128]{2,1,0:T(8,128)} %bitcast_add_fusion.1), calls=%async_computation.2 | async-start | bytes 262144 | tf_op jit(solution)/shard_map/all_to_all | solution.py:134
  (5 other events, 3.7 us)
Sparse Core Ops, SparseCore 0:
  126.4 50.1 all-gather.1

commit v11 on v9

--- a/solution.py
+++ b/solution.py
@@ -28,16 +28,14 @@
     for field in range(1, NFEAT):
         onehot = onehot + (table_rows[:, :, field : field + 1] == table_ids).astype(jnp.bfloat16)
     hidden = jnp.einsum("esv,vc->esc", onehot, embed, preferred_element_type=jnp.float32)
-    wides = []
-    pres = []
-    for layer in range(LAYERS):
+    def forward_layer(hidden, weight):
         wide_input = shift_wide(hidden.astype(jnp.bfloat16))
-        pre_act = jnp.einsum(
-            "esk,kc->esc", wide_input, conv_w[layer], preferred_element_type=jnp.float32
-        )
-        wides.append(wide_input)
-        pres.append(pre_act)
-        hidden = hidden + jax.nn.silu(pre_act)
+        pre_act = jnp.einsum("esk,kc->esc", wide_input, weight, preferred_element_type=jnp.float32)
+        return hidden + jax.nn.silu(pre_act), (wide_input, pre_act)
+
+    hidden, (wide_stack, pre_stack) = lax.scan(forward_layer, hidden, conv_w)
+    wides = [wide_stack[layer] for layer in range(LAYERS)]
+    pres = [pre_stack[layer] for layer in range(LAYERS)]
     grad_h = jnp.broadcast_to(head / SEQ, hidden.shape)
     delta_sides = [None] * LAYERS
     input_sides = [None] * LAYERS

time: 215 us -> 246 us (1.14)
  matrix products: 42.4 us -> 59.9 us
  other arithmetic: 9.21 us -> 19.2 us
  local copies, waits for them, and re-layouts: 31.9 us -> 37.8 us
    ppermute x1, waiting for transfers between devices: 0.01 us -> 11.7 us  [on_device(): from_below = lax.ppermute(right_part, 'y', up)]
    ppermute x1, waiting for transfers between devices: 10.9 us -> 0.01 us  [on_device(): from_above = lax.ppermute(right_part, 'y', down)]
    dynamic_update_slice x0 -> x8, other arithmetic: none -> 9.78 us  [panels(): hidden, (wide_stack, pre_stack) = lax.scan(forward_layer, hidden, conv_w)]
    dot_general x8, matrix products: 4.67 us -> 12.6 us  [forward_layer(): jnp.einsum('esk,kc->esc', wide_input, weight, preferred_element_type=jnp....]
    dynamic_update_slice x0 -> x8, local copies, waits for them, and re-layouts: none -> 7.59 us  [panels(): hidden, (wide_stack, pre_stack) = lax.scan(forward_layer, hidden, conv_w)]
    dot_general x8, matrix products: 8.43 us -> 12.5 us  [panels(): jnp.einsum('esc,cr->esr', delta_low, proj_delta[assign[layer]], preferred...]
    dot_general x8, matrix products: 16.1 us -> 20.1 us  [panels(): jnp.einsum('esk,kt->est', wides[layer], proj_input[assign[layer]], prefer...]
    ppermute x1, waiting for transfers between devices: 3.72 us -> 0.01 us  [on_device(): far_high = lax.ppermute(from_above[half:], 'y', down)]
  transfers between devices with their start and end apart: 7 -> 7, of which waited for: 5 -> 4; matrix products, arithmetic and copies ran while one was open for 4% -> 4% of each run, Pallas kernels for 0% -> 0%
where the time goes in v11:
time: 246 us; the launch traced here: 244 us
  matrix products  59.9 us (24%)
  blocking collectives  55.6 us (23%)
  local copies, waits for them, and re-layouts  37.8 us (15%)
  between operations  29.5 us (12%)
  waiting for transfers between devices  28.5 us (12%)
  other arithmetic  19.2 us (8%)
  starting transfers between devices  13.3 us (5%)
    all_to_all x1, blocking collectives, on_device(): lax.all_to_all(sliced[:left_each], group, split_axis=1, concat_axis=0, ti...  35.6 us
    dot_general x8, matrix products, panels(): jnp.einsum('esk,kt->est', wides[layer], proj_input[assign[layer]], prefer...  20.1 us
    all_to_all x1, blocking collectives, on_device(): lax.all_to_all(right_sliced, group, split_axis=1, concat_axis=0, tiled=True)  20 us
    dot_general x8, matrix products, forward_layer(): jnp.einsum('esk,kc->esc', wide_input, weight, preferred_element_type=jnp....  12.6 us
    dot_general x8, matrix products, panels(): jnp.einsum('esc,cr->esr', delta_low, proj_delta[assign[layer]], preferred...  12.5 us
    ppermute x1, waiting for transfers between devices, on_device(): from_below = lax.ppermute(right_part, 'y', up)  11.7 us
    all_to_all x1, waiting for transfers between devices, on_device(): lax.all_to_all(paired, ('zh', 'col'), split_axis=0, concat_axis=0, tiled=...  11.1 us
    dynamic_update_slice x8, other arithmetic, panels(): hidden, (wide_stack, pre_stack) = lax.scan(forward_layer, hidden, conv_w)  9.78 us
  transfers between devices with their start and end apart: 7, of which 4 were waited for; matrix products, arithmetic and copies ran while one was open for 4% of the time, Pallas kernels for 0%

profile of v11, /device:TPU:1, one launch (start us, length us, event | category | flops | bytes accessed | tf_op | source)
XLA Modules:
  0.0 244.0 jit_solution(11512257539630633512)
XLA Ops:
  6.5 1.6 fusion.217
  21.7 2.7 %fusion.23 = f32[12,64,256]{2,1,0:T(8,128)S(1)} fusion(s32[12,64]{1,0:T(8,128)S(1)} %bitcast.413, s32[12,64]{1,0:T(8,128)S(1)} %bitcast.412, s32[12,64]{1,0:T(8,128)S(1)} %bitcast.411, s32[12,64]{1,0:T(8,128)S(1)} %bitcast.410, bf16[1024,256]{1,0:T(8,128)(2,1)} %param.12), kind=kOutput, calls=%fused_computation.31 | convolution fusion | flops 415236096 | bytes 1323008 | tf_op jit(solution)/shard_map/esv,vc->esc/dot_general | solution.py:30
  24.5 31.6 %while.14 = (s32[]{:T(128)}, f32[12,64,256]{2,1,0:T(8,128)S(1)}, bf16[8,12,64,768]{3,2,1,0:T(8,128)(2,1)}, f32[8,12,64,256]{3,2,1,0:T(8,128)}, bf16[8,768,256]{2,1,0:T(8,128)(2,1)}, /*index=5*/s32[]{:T(128)}) while((s32[]{:T(128)}, f32[12,64,256]{2,1,0:T(8,128)S(1)}, bf16[8,12,64,768]{3,2,1,0:T(8,128)(2,1)}, f32[8,12,64,256]{3,2,1,0:T(8,128)}, ...), condition=%wide.region_1.2_spmd, body=%wide.region_0.1_spmd.sunk | while | flops 314966016 | bytes 10569285 | solution.py:36
  24.7 1.6 multiply_add_fusion.3
  26.2 1.0 bitcast_dynamic-update-slice_fusion.5
  27.2 1.2 bitcast_dynamic-update-slice_fusion.4
  28.6 1.6 multiply_add_fusion.3
  31.1 1.2 bitcast_dynamic-update-slice_fusion.4
  32.5 1.6 multiply_add_fusion.3
  35.0 1.2 bitcast_dynamic-update-slice_fusion.4
  36.4 1.6 multiply_add_fusion.3
  38.0 1.0 bitcast_dynamic-update-slice_fusion.5
  39.0 1.2 bitcast_dynamic-update-slice_fusion.4
  40.3 1.6 multiply_add_fusion.3
  41.9 1.0 bitcast_dynamic-update-slice_fusion.5
  42.9 1.2 bitcast_dynamic-update-slice_fusion.4
  44.3 1.6 multiply_add_fusion.3
  45.9 0.9 bitcast_dynamic-update-slice_fusion.5
  46.8 1.2 bitcast_dynamic-update-slice_fusion.4
  48.2 1.6 multiply_add_fusion.3
  50.8 1.3 bitcast_dynamic-update-slice_fusion.4
  52.2 1.6 multiply_add_fusion.3
  54.8 1.3 bitcast_dynamic-update-slice_fusion.4
  56.0 2.1 fusion.137
  65.8 1.3 fusion.92
  67.7 1.4 fusion.209
  70.4 3.2 %fusion.49 = f32[8,12,64,128]{3,2,1,0:T(8,128)} fusion(f32[12,64,256]{2,1,0:T(8,128)} %get-tuple-element.48, f32[12,64,768]{2,1,0:T(8,128)S(1)} %fusion.125, f32[8,12,64,256]{3,2,1,0:T(8,128)} %get-tuple-element.34, f32[12,63,256]{2,1,0:T(8,128)} %get-tuple-element.64, f32[12,63,256]{2,1,0:T(8,128)} %get-tuple-element.63, bf16[4,256,128]{2,1,0:T(8,128)(2,1)} %param.16, ...), kind=kOutput, calls=%fused_computation.69 | convolution fusion | flops 52690944 | bytes 4390916 | tf_op jit(solution)/shard_map/esc,cr->esr/dot_general | solution.py:46
  73.6 1.9 fusion.48
  75.5 2.6 %fusion.41 = f32[8,12,64,128]{3,2,1,0:T(8,128)} fusion(bf16[8,12,64,768]{3,2,1,0:T(8,128)(2,1)} %get-tuple-element.35, bf16[4,768,128]{2,1,0:T(8,128)(2,1)S(1)} %copy-done, s32[]{:T(128)S(6)} %select_n.67), kind=kOutput, calls=%fused_computation.53 | convolution fusion | flops 150994944 | bytes 1769476 | tf_op jit(solution)/shard_map/esk,kt->est/dot_general | solution.py:49
  78.1 2.5 %fusion.40 = f32[8,12,64,128]{3,2,1,0:T(8,128)} fusion(f32[8,12,64,128]{3,2,1,0:T(8,128)} %fusion.41, bf16[8,12,64,768]{3,2,1,0:T(8,128)(2,1)} %get-tuple-element.35, bf16[4,768,128]{2,1,0:T(8,128)(2,1)S(1)} %copy-done, s32[]{:T(128)S(6)} %select_n.68), kind=kOutput, calls=%fused_computation.51 | convolution fusion | flops 150994944 | bytes 1769476 | tf_op jit(solution)/shard_map/esk,kt->est/dot_general | solution.py:49
  81.4 1.0 fusion.47
  82.4 2.5 %fusion.39 = f32[8,12,64,128]{3,2,1,0:T(8,128)} fusion(f32[8,12,64,128]{3,2,1,0:T(8,128)} %fusion.40, bf16[8,12,64,768]{3,2,1,0:T(8,128)(2,1)} %get-tuple-element.35, bf16[4,768,128]{2,1,0:T(8,128)(2,1)S(1)} %copy-done, s32[]{:T(128)S(6)} %select_n.69), kind=kOutput, calls=%fused_computation.49 | convolution fusion | flops 150994944 | bytes 1769476 | tf_op jit(solution)/shard_map/esk,kt->est/dot_general | solution.py:49
  85.6 1.0 fusion.46
  86.6 2.5 %fusion.38 = f32[8,12,64,128]{3,2,1,0:T(8,128)} fusion(f32[8,12,64,128]{3,2,1,0:T(8,128)} %fusion.39, bf16[8,12,64,768]{3,2,1,0:T(8,128)(2,1)} %get-tuple-element.35, bf16[4,768,128]{2,1,0:T(8,128)(2,1)S(1)} %copy-done, s32[]{:T(128)S(6)} %select_n.70), kind=kOutput, calls=%fused_computation.47 | convolution fusion | flops 150994944 | bytes 1769476 | tf_op jit(solution)/shard_map/esk,kt->est/dot_general | solution.py:49
  89.8 1.0 fusion.45
  90.8 2.5 %fusion.37 = f32[8,12,64,128]{3,2,1,0:T(8,128)} fusion(f32[8,12,64,128]{3,2,1,0:T(8,128)} %fusion.38, bf16[8,12,64,768]{3,2,1,0:T(8,128)(2,1)} %get-tuple-element.35, bf16[4,768,128]{2,1,0:T(8,128)(2,1)S(1)} %copy-done, s32[]{:T(128)S(6)} %select_n.71), kind=kOutput, calls=%fused_computation.45 | convolution fusion | flops 150994944 | bytes 1769476 | tf_op jit(solution)/shard_map/esk,kt->est/dot_general | solution.py:49
  94.0 1.0 fusion.44
  95.0 2.5 %fusion.36 = f32[8,12,64,128]{3,2,1,0:T(8,128)} fusion(f32[8,12,64,128]{3,2,1,0:T(8,128)} %fusion.37, bf16[8,12,64,768]{3,2,1,0:T(8,128)(2,1)} %get-tuple-element.35, bf16[4,768,128]{2,1,0:T(8,128)(2,1)S(1)} %copy-done, s32[]{:T(128)S(6)} %select_n.72), kind=kOutput, calls=%fused_computation.43 | convolution fusion | flops 150994944 | bytes 1769476 | tf_op jit(solution)/shard_map/esk,kt->est/dot_general | solution.py:49
  98.2 1.0 fusion.43
  99.2 2.5 %fusion.35 = f32[8,12,64,128]{3,2,1,0:T(8,128)} fusion(f32[8,12,64,128]{3,2,1,0:T(8,128)} %fusion.36, bf16[8,12,64,768]{3,2,1,0:T(8,128)(2,1)} %get-tuple-element.35, bf16[4,768,128]{2,1,0:T(8,128)(2,1)S(1)} %copy-done, s32[]{:T(128)S(6)} %select_n.73), kind=kOutput, calls=%fused_computation.41 | convolution fusion | flops 150994944 | bytes 1769476 | tf_op jit(solution)/shard_map/esk,kt->est/dot_general | solution.py:49
  102.3 2.3 fusion.42
  104.6 2.5 %fusion.34 = f32[8,12,64,128]{3,2,1,0:T(8,128)} fusion(f32[8,12,64,128]{3,2,1,0:T(8,128)} %fusion.35, bf16[8,12,64,768]{3,2,1,0:T(8,128)(2,1)} %get-tuple-element.35, bf16[4,768,128]{2,1,0:T(8,128)(2,1)S(1)} %copy-done, s32[]{:T(128)S(6)} %select_n.74), kind=kOutput, calls=%fused_computation.39 | convolution fusion | flops 150994944 | bytes 1769476 | tf_op jit(solution)/shard_map/esk,kt->est/dot_general | solution.py:49
  107.2 4.3 %gather_fusion = f32[8,12,64,128]{3,2,1,0:T(8,128)} fusion(f32[8,12,64,128]{3,2,1,0:T(8,128)} %fusion.42, s32[1024]{0:T(1024)S(1)} %pad_clamp_fusion), kind=kCustom, calls=%fused_computation | custom fusion | bytes 6291488 | tf_op jit(solution)/shard_map/gather | solution.py:72
  111.4 4.3 %gather_fusion.1 = f32[8,12,64,128]{3,2,1,0:T(8,128)} fusion(f32[8,12,64,128]{3,2,1,0:T(8,128)} %fusion.34, s32[1024]{0:T(1024)S(1)} %pad_clamp_fusion), kind=kCustom, calls=%fused_computation.1 | custom fusion | bytes 6291488 | tf_op jit(solution)/shard_map/gather | solution.py:73
  115.8 5.7 %bitcast_convert_fusion = bf16[12,4,128,128]{3,2,1,0:T(8,128)(2,1)S(1)} fusion(f32[4,2,12,64,128]{4,3,2,1,0:T(8,128)} %bitcast.399, f32[4,2,12,64,128]{4,3,2,1,0:T(8,128)} %bitcast.398), kind=kOutput, calls=%fused_computation.15 | convolution fusion | flops 604766208 | bytes 7864320 | tf_op jit(solution)/shard_map/bjesr,bjest->ebrt/dot_general | solution.py:77
  121.5 1.0 slice.323
  122.5 1.5 slice.287
  124.6 35.6 %all_to_all.35 = bf16[8,16,4096]{2,0,1:T(8,128)(2,1)} all-to-all(bf16[8,16,4096]{2,0,1:T(8,128)(2,1)S(1)} %copy.46), channel_id=1, replica_groups=mesh['zh'=2,'y'=4,'core'=2,'col'=4,'pblk'=4] {'zh','core','col'}, dimensions={1} | all-to-all | bytes 2097152 | tf_op jit(solution)/shard_map/all_to_all | solution.py:99
  160.9 20.0 %all_to_all.36 = bf16[4,16,4096]{2,0,1:T(4,128)(2,1)S(1)} all-to-all(bf16[4,16,4096]{2,0,1:T(4,128)(2,1)S(1)} %copy.47), channel_id=1, replica_groups=mesh['zh'=2,'y'=4,'core'=2,'col'=4,'pblk'=4] {'zh','core','col'}, dimensions={1} | all-to-all | bytes 1048576 | tf_op jit(solution)/shard_map/all_to_all | solution.py:103
  181.0 1.4 collective-permute-start
  182.4 1.5 collective-permute-start.2
  183.9 11.7 %collective-permute-done = bf16[64,4096]{1,0:T(8,128)(2,1)S(1)} collective-permute-done((bf16[64,4096]{1,0:T(8,128)(2,1)S(1)}, bf16[64,4096]{1,0:T(8,128)(2,1)S(1)}, u32[]{:S(2)}, u32[]{:S(2)}) %collective-permute-start) | collective-permute-done | bytes 524320 | tf_op jit(solution)/shard_map/ppermute | solution.py:107
  197.1 2.7 %collective-permute-start.3 = (bf16[32,4096]{1,0:T(8,128)(2,1)}, bf16[32,4096]{1,0:T(8,128)(2,1)}, u32[]{:S(2)}, u32[]{:S(2)}) collective-permute-start(bf16[32,4096]{1,0:T(8,128)(2,1)} %slice.326), channel_id=1, source_target_pairs={{0,96},{32,0},{64,32},{96,64},{1,97},{33,1},{65,33},{97,65},{2,98}... | collective-permute-start | bytes 786440 | tf_op jit(solution)/shard_map/ppermute | solution.py:111
  200.2 4.5 %collective-permute-done.1 = bf16[32,4096]{1,0:T(8,128)(2,1)} collective-permute-done((bf16[32,4096]{1,0:T(8,128)(2,1)}, bf16[32,4096]{1,0:T(8,128)(2,1)}, u32[]{:S(2)}, u32[]{:S(2)}) %collective-permute-start.1) | collective-permute-done | bytes 262176 | tf_op jit(solution)/shard_map/ppermute | solution.py:110
  204.7 1.1 pad_maximum_fusion
  206.0 2.0 maximum_bitcast_fusion
  207.9 1.6 copy.48
  209.5 2.1 reshape.129
  211.6 2.6 %copy.49 = bf16[4,4,4,8,4096]{4,3,2,1,0:T(8,128)(2,1)S(1)} copy(bf16[4,4,4,8,4096]{4,3,1,0,2:T(8,128)(2,1)} %bitcast.402) | data formatting | bytes 8388608 | tf_op jit(solution)/shard_map/transpose | solution.py:115
  214.4 1.3 fusion.16
  215.8 2.0 collective-permute-start.4
  217.8 1.2 collective-permute-done.4
  219.7 5.7 %all-to-all-start.2 = ((f32[8,64,128]{2,1,0:T(8,128)}), f32[8,64,128]{2,1,0:T(8,128)S(1)}, u32[]{:S(2)}, u32[]{:S(2)}) async-start(f32[8,64,128]{2,1,0:T(8,128)} %bitcast.123), calls=%async_computation.2 | async-start | bytes 524288 | tf_op jit(solution)/shard_map/all_to_all | solution.py:128
  225.4 11.1 %all-to-all-done.2 = f32[8,64,128]{2,1,0:T(8,128)S(1)} async-done(((f32[8,64,128]{2,1,0:T(8,128)}), f32[8,64,128]{2,1,0:T(8,128)S(1)}, u32[]{:S(2)}, u32[]{:S(2)}) %all-to-all-start.2) | async-done | bytes 262176 | tf_op jit(solution)/shard_map/all_to_all | solution.py:128
  (109 shorter events, 21.7 us)
Async XLA Ops:
  6.5 69.0 %copy-start = (bf16[4,768,128]{2,1,0:T(8,128)(2,1)S(1)}, bf16[4,768,128]{2,1,0:T(8,128)(2,1)}, u32[]{:S(2)}) copy-start(bf16[4,768,128]{2,1,0:T(8,128)(2,1)} %param.17) | copy-start | bytes 2359300
  6.5 205.1 %all-gather.2.cloned.1.call-start = ((), (), s32[]{:S(2)}) async-start(), calls=%async_computation.3 | async-start | bytes 5242880 | tf_op jit(solution)/shard_map/all_gather | solution.py:101
  24.4 31.6 %copy-start.16 = (f32[256]{0:T(256)S(1)}, f32[256]{0:T(256)}, u32[]{:S(2)}) copy-start(f32[256]{0:T(256)} %param.14) | copy-start | bytes 3076
  56.0 3.1 %copy-start.1 = (f32[8,12,64,256]{3,2,1,0:T(8,128)S(1)}, f32[8,12,64,256]{3,2,1,0:T(8,128)}, u32[]{:S(2)}) copy-start(f32[8,12,64,256]{3,2,1,0:T(8,128)} %get-tuple-element.34) | copy-start | bytes 18874372
  58.1 2.2 copy-start.13
  61.5 0.8 copy-start.2
  62.7 0.8 copy-start.4
  63.9 0.7 copy-start.6
  65.1 0.8 copy-start.8
  67.1 1.9 copy-start.10
  67.1 1.9 copy-start.15
  70.4 3.2 %copy-start.11 = (bf16[12,64,256]{2,1,0:T(8,128)(2,1)S(1)}, bf16[12,64,256]{2,1,0:T(8,128)(2,1)}, u32[]{:S(2)}) copy-start(bf16[12,64,256]{2,1,0:T(8,128)(2,1)} %copy-done.10) | copy-start | bytes 1179652
  73.6 7.7 %copy-start.9 = (bf16[12,64,256]{2,1,0:T(8,128)(2,1)S(1)}, bf16[12,64,256]{2,1,0:T(8,128)(2,1)}, u32[]{:S(2)}) copy-start(bf16[12,64,256]{2,1,0:T(8,128)(2,1)} %copy-done.8) | copy-start | bytes 1179652
  73.6 7.7 %copy-start.14 = (bf16[4,256,128]{2,1,0:T(8,128)(2,1)S(1)}, bf16[4,256,128]{2,1,0:T(8,128)(2,1)}, u32[]{:S(2)}) copy-start(bf16[4,256,128]{2,1,0:T(8,128)(2,1)} %param.16) | copy-start | bytes 786436
  75.5 10.1 %copy-start.7 = (bf16[12,64,256]{2,1,0:T(8,128)(2,1)S(1)}, bf16[12,64,256]{2,1,0:T(8,128)(2,1)}, u32[]{:S(2)}) copy-start(bf16[12,64,256]{2,1,0:T(8,128)(2,1)} %copy-done.6) | copy-start | bytes 1179652
  80.6 9.2 %copy-start.5 = (bf16[12,64,256]{2,1,0:T(8,128)(2,1)S(1)}, bf16[12,64,256]{2,1,0:T(8,128)(2,1)}, u32[]{:S(2)}) copy-start(bf16[12,64,256]{2,1,0:T(8,128)(2,1)} %copy-done.4) | copy-start | bytes 1179652
  84.9 9.1 %copy-start.3 = (bf16[12,64,256]{2,1,0:T(8,128)(2,1)S(1)}, bf16[12,64,256]{2,1,0:T(8,128)(2,1)}, u32[]{:S(2)}) copy-start(bf16[12,64,256]{2,1,0:T(8,128)(2,1)} %copy-done.2) | copy-start | bytes 1179652
  181.0 14.6 %collective-permute-start = (bf16[64,4096]{1,0:T(8,128)(2,1)S(1)}, bf16[64,4096]{1,0:T(8,128)(2,1)S(1)}, u32[]{:S(2)}, u32[]{:S(2)}) collective-permute-start(bf16[64,4096]{1,0:T(8,128)(2,1)S(1)} %reshape.82), channel_id=1, source_target_pairs={{0,32},{32,64},{64,96},{96,0},{1,33},{33,65},{65,97},{97,1},{2,34}... | collective-permute-start | bytes 1572872 | tf_op jit(solution)/shard_map/ppermute | solution.py:107
  182.4 14.0 %collective-permute-start.2 = (bf16[64,4096]{1,0:T(8,128)(2,1)S(1)}, bf16[64,4096]{1,0:T(8,128)(2,1)S(1)}, u32[]{:S(2)}, u32[]{:S(2)}) collective-permute-start(bf16[64,4096]{1,0:T(8,128)(2,1)S(1)} %reshape.82), channel_id=1, source_target_pairs={{0,96},{32,0},{64,32},{96,64},{1,97},{33,1},{65,33},{97,65},{2,98}... | collective-permute-start | bytes 1572872 | tf_op jit(solution)/shard_map/ppermute | solution.py:108
  196.4 8.3 %collective-permute-start.1 = (bf16[32,4096]{1,0:T(8,128)(2,1)}, bf16[32,4096]{1,0:T(8,128)(2,1)}, u32[]{:S(2)}, u32[]{:S(2)}) collective-permute-start(bf16[32,4096]{1,0:T(8,128)(2,1)} %slice.325), channel_id=1, source_target_pairs={{0,32},{32,64},{64,96},{96,0},{1,33},{33,65},{65,97},{97,1},{2,34}... | collective-permute-start | bytes 786440 | tf_op jit(solution)/shard_map/ppermute | solution.py:110
  197.1 7.6 %collective-permute-start.3 = (bf16[32,4096]{1,0:T(8,128)(2,1)}, bf16[32,4096]{1,0:T(8,128)(2,1)}, u32[]{:S(2)}, u32[]{:S(2)}) collective-permute-start(bf16[32,4096]{1,0:T(8,128)(2,1)} %slice.326), channel_id=1, source_target_pairs={{0,96},{32,0},{64,32},{96,64},{1,97},{33,1},{65,33},{97,65},{2,98}... | collective-permute-start | bytes 786440 | tf_op jit(solution)/shard_map/ppermute | solution.py:111
  211.6 2.9 %copy-start.12 = (bf16[4,64,4096,1]{2,1,0,3:T(8,128)(2,1)S(1)}, bf16[4,64,4096,1]{2,1,0,3:T(8,128)(2,1)}, u32[]{:S(2)}) copy-start(bf16[4,64,4096,1]{2,1,0,3:T(8,128)(2,1)} %reshape.129) | copy-start | bytes 6291460
  215.8 3.2 %collective-permute-start.4 = (f32[2,4,64,128]{3,2,1,0:T(8,128)S(1)}, f32[2,4,64,128]{3,2,1,0:T(8,128)S(1)}, u32[]{:S(2)}, u32[]{:S(2)}) collective-permute-start(f32[2,4,64,128]{3,2,1,0:T(8,128)S(1)} %bitcast.408), channel_id=1, source_target_pairs={{0,16},{16,0},{1,17},{17,1},{2,18},{18,2},{3,19},{19,3},{4,20},{20... | collective-permute-start | bytes 786440 | tf_op jit(solution)/shard_map/ppermute | solution.py:126
  219.7 16.8 %all-to-all-start.2 = ((f32[8,64,128]{2,1,0:T(8,128)}), f32[8,64,128]{2,1,0:T(8,128)S(1)}, u32[]{:S(2)}, u32[]{:S(2)}) async-start(f32[8,64,128]{2,1,0:T(8,128)} %bitcast.123), calls=%async_computation.2 | async-start | bytes 524288 | tf_op jit(solution)/shard_map/all_to_all | solution.py:128
Sparse Core Ops, SparseCore 0:
  160.3 50.0 all-gather.1

commit v12 on v9

--- a/solution.py
+++ b/solution.py
@@ -71,8 +71,11 @@
     order = jnp.sum(
         jnp.where(slot[None, :] == layer_ids[:, None], layer_ids[None, :], 0), axis=1
     )
-    delta_stack = jnp.stack(delta_sides)[order]
-    input_stack = jnp.stack(input_sides)[order]
+    delta_stack = jnp.zeros((LAYERS,) + delta_sides[0].shape, jnp.float32)
+    input_stack = jnp.zeros((LAYERS,) + input_sides[0].shape, jnp.float32)
+    for layer in range(LAYERS):
+        delta_stack = lax.dynamic_update_index_in_dim(delta_stack, delta_sides[layer], slot[layer], 0)
+        input_stack = lax.dynamic_update_index_in_dim(input_stack, input_sides[layer], slot[layer], 0)
     per_block = LAYERS // blocks_here
     delta_stack = delta_stack.reshape(blocks_here, per_block, examples, SEQ, PR)
     input_stack = input_stack.reshape(blocks_here, per_block, examples, SEQ, PS)

time: 215 us -> 221 us (1.028)
  between operations: 29.3 us -> 44 us
  matrix products: 42.4 us -> 38.6 us
  waiting for transfers between devices: 30.8 us -> 28.5 us
  local copies, waits for them, and re-layouts: 31.9 us -> 29.6 us
    ppermute x1, waiting for transfers between devices: 0.01 us -> 11.7 us  [on_device(): from_below = lax.ppermute(right_part, 'y', up)]
    ppermute x1, waiting for transfers between devices: 10.9 us -> 0.01 us  [on_device(): from_above = lax.ppermute(right_part, 'y', down)]
    gather x2 -> x0, local copies, waits for them, and re-layouts: 8.56 us -> none  [the longest x1 4.3 us: panels(): input_stack = jnp.stack(input_sides)[order]]
    dot_general x8, matrix products: 16.1 us -> 12.1 us  [panels(): jnp.einsum('esk,kt->est', wides[layer], proj_input[assign[layer]], prefer...]
    ppermute x1, waiting for transfers between devices: 3.72 us -> 0.01 us  [on_device(): far_high = lax.ppermute(from_above[half:], 'y', down)]
    unnamed x123 -> x135, local copies, waits for them, and re-layouts: 4.69 us -> 7.89 us
    another operation x0 -> x2, local copies, waits for them, and re-layouts: none -> 2.41 us
  transfers between devices with their start and end apart: 7 -> 7, of which waited for: 5 -> 4; matrix products, arithmetic and copies ran while one was open for 4% -> 4% of each run, Pallas kernels for 0% -> 0%
where the time goes in v12:
time: 221 us; the launch traced here: 219 us
  blocking collectives  55.6 us (25%)
  between operations  44 us (20%)
  matrix products  38.6 us (17%)
  local copies, waits for them, and re-layouts  29.6 us (13%)
  waiting for transfers between devices  28.5 us (13%)
  starting transfers between devices  13.3 us (6%)
  other arithmetic  9.66 us (4%)
    all_to_all x1, blocking collectives, on_device(): lax.all_to_all(sliced[:left_each], group, split_axis=1, concat_axis=0, ti...  35.6 us
    all_to_all x1, blocking collectives, on_device(): lax.all_to_all(right_sliced, group, split_axis=1, concat_axis=0, tiled=True)  20 us
    dot_general x8, matrix products, panels(): jnp.einsum('esk,kt->est', wides[layer], proj_input[assign[layer]], prefer...  12.1 us
    ppermute x1, waiting for transfers between devices, on_device(): from_below = lax.ppermute(right_part, 'y', up)  11.7 us
    all_to_all x1, waiting for transfers between devices, on_device(): lax.all_to_all(paired, ('zh', 'col'), split_axis=0, concat_axis=0, tiled=...  11.1 us
    dot_general x8, matrix products, panels(): jnp.einsum('esc,cr->esr', delta_low, proj_delta[assign[layer]], preferred...  8.62 us
    unnamed x135, local copies, waits for them, and re-layouts  7.89 us
    all_to_all x1, starting transfers between devices, on_device(): lax.all_to_all(paired, ('zh', 'col'), split_axis=0, concat_axis=0, tiled=...  5.67 us
  transfers between devices with their start and end apart: 7, of which 4 were waited for; matrix products, arithmetic and copies ran while one was open for 4% of the time, Pallas kernels for 0%

profile of v12, /device:TPU:1, one launch (start us, length us, event | category | flops | bytes accessed | tf_op | source)
XLA Modules:
  0.0 219.3 jit_solution(10545368178357410364)
XLA Ops:
  6.5 0.9 convert_reduce_fusion
  7.5 1.6 fusion.226
  9.1 0.7 multiply_add_fusion.6
  9.7 0.7 fusion.227
  30.2 0.8 copy.80
  31.0 0.8 copy.110
  32.4 2.9 %fusion.228 = (bf16[12,64,256]{2,1,0:T(8,128)(2,1)S(1)}, f32[12,64,256]{2,1,0:T(8,128)S(1)}) fusion(bf16[1024,256]{1,0:T(8,128)(2,1)} %param.10, s32[12,64]{1,0:T(8,128)S(1)} %bitcast.323, s32[12,64]{1,0:T(8,128)S(1)} %bitcast.322, s32[12,64]{1,0:T(8,128)S(1)} %bitcast.321, s32[12,64]{1,0:T(8,128)S(1)} %bitcast.320), kind=kOutput, calls=%fused_computation.266 | convolution fusion | flops 415432704 | bytes 1716224 | tf_op jit(solution)/shard_map/esv,vc->esc/dot_general | solution.py:30
  35.4 0.5 fusion.198
  36.5 0.7 fusion.209
  37.8 0.5 fusion.199
  38.8 0.7 fusion.208
  39.9 0.5 fusion.200
  40.9 0.7 fusion.207
  42.0 0.5 add_convert_fusion
  43.0 0.6 multiply_convert_fusion.6
  43.8 0.5 fusion.85
  45.0 0.5 fusion.88
  48.5 0.5 fusion.100
  50.6 1.4 multiply_convert_fusion
  52.0 0.8 copy-done.10
  53.3 1.3 fusion.210
  57.5 0.6 copy-done.28
  60.1 2.0 broadcast.90.clone
  62.1 0.8 copy-done.34
  62.9 0.8 copy-done.35
  63.8 1.3 fusion.49
  65.1 1.1 fusion.48
  67.4 2.6 %fusion.39 = f32[8,12,64,128]{3,2,0,1:T(8,128)} fusion(f32[8,12,64,128]{3,2,0,1:T(8,128)} %copy-done.1, s32[]{:T(128)S(6)} %select_n.90, bf16[4,768,128]{2,1,0:T(8,128)(2,1)S(1)} %copy-done, s32[]{:T(128)S(6)} %select_n.89, bf16[12,63,256]{2,1,0:T(8,128)(2,1)} %copy-done.55, bf16[12,63,256]{2,1,0:T(8,128)(2,1)} %copy-done.54, ...), kind=kOutput, calls=%fused_computation.49 | convolution fusion | flops 156893184 | bytes 1769480 | tf_op jit(solution)/shard_map/esk,kt->est/dot_general | solution.py:51
  70.1 1.1 fusion.47
  72.4 1.3 fusion.38
  73.7 1.0 fusion.46
  76.0 2.4 %fusion.37 = f32[8,12,64,128]{3,2,0,1:T(8,128)} fusion(f32[8,12,64,128]{3,2,0,1:T(8,128)} %fusion.38, s32[]{:T(128)S(6)} %select_n.94, bf16[4,768,128]{2,1,0:T(8,128)(2,1)S(1)} %copy-done, s32[]{:T(128)S(6)} %select_n.93, bf16[12,63,256]{2,1,0:T(8,128)(2,1)} %copy-done.49, bf16[12,63,256]{2,1,0:T(8,128)(2,1)S(1)} %copy-done.48, ...), kind=kOutput, calls=%fused_computation.45 | convolution fusion | flops 156893184 | bytes 1769480 | tf_op jit(solution)/shard_map/esk,kt->est/dot_general | solution.py:51
  78.3 1.0 fusion.45
  80.6 1.3 fusion.36
  81.9 1.0 fusion.44
  84.3 2.4 %fusion.35 = f32[8,12,64,128]{3,2,0,1:T(8,128)} fusion(f32[8,12,64,128]{3,2,0,1:T(8,128)} %fusion.36, s32[]{:T(128)S(6)} %select_n.98, bf16[4,768,128]{2,1,0:T(8,128)(2,1)S(1)} %copy-done, s32[]{:T(128)S(6)} %select_n.97, bf16[12,63,256]{2,1,0:T(8,128)(2,1)} %copy-done.42, bf16[12,63,256]{2,1,0:T(8,128)(2,1)S(1)} %copy-done.41, ...), kind=kOutput, calls=%fused_computation.41 | convolution fusion | flops 156893184 | bytes 1769480 | tf_op jit(solution)/shard_map/esk,kt->est/dot_general | solution.py:51
  86.7 1.1 fusion.43
  89.0 1.3 fusion.34
  90.3 1.1 fusion.42
  91.4 5.5 %bitcast_convert_fusion = bf16[12,4,128,128]{3,2,1,0:T(8,128)(2,1)S(1)} fusion(f32[4,2,12,64,128]{4,3,1,0,2:T(8,128)} %bitcast.71, f32[4,2,12,64,128]{4,3,1,0,2:T(8,128)} %bitcast.309), kind=kOutput, calls=%fused_computation | convolution fusion | flops 604766208 | bytes 7864320 | tf_op jit(solution)/shard_map/bjesr,bjest->ebrt/dot_general | solution.py:82
  96.8 1.0 slice.378
  97.9 1.5 slice.332
  99.4 0.6 copy.102
  100.0 35.6 %all_to_all.35 = bf16[8,16,4096]{2,0,1:T(8,128)(2,1)} all-to-all(bf16[8,16,4096]{2,0,1:T(8,128)(2,1)S(1)} %copy.102), channel_id=1, replica_groups=mesh['zh'=2,'y'=4,'core'=2,'col'=4,'pblk'=4] {'zh','core','col'}, dimensions={1} | all-to-all | bytes 2097152 | tf_op jit(solution)/shard_map/all_to_all | solution.py:104
  136.3 20.0 %all_to_all.36 = bf16[4,16,4096]{2,0,1:T(4,128)(2,1)S(1)} all-to-all(bf16[4,16,4096]{2,0,1:T(4,128)(2,1)S(1)} %copy.103), channel_id=1, replica_groups=mesh['zh'=2,'y'=4,'core'=2,'col'=4,'pblk'=4] {'zh','core','col'}, dimensions={1} | all-to-all | bytes 1048576 | tf_op jit(solution)/shard_map/all_to_all | solution.py:108
  156.4 1.3 collective-permute-start
  157.8 1.5 collective-permute-start.2
  159.3 11.7 %collective-permute-done = bf16[64,4096]{1,0:T(8,128)(2,1)S(1)} collective-permute-done((bf16[64,4096]{1,0:T(8,128)(2,1)S(1)}, bf16[64,4096]{1,0:T(8,128)(2,1)S(1)}, u32[]{:S(2)}, u32[]{:S(2)}) %collective-permute-start) | collective-permute-done | bytes 524320 | tf_op jit(solution)/shard_map/ppermute | solution.py:112
  171.0 0.7 slice.380
  171.7 0.7 slice.381
  172.5 2.7 %collective-permute-start.3 = (bf16[32,4096]{1,0:T(8,128)(2,1)}, bf16[32,4096]{1,0:T(8,128)(2,1)}, u32[]{:S(2)}, u32[]{:S(2)}) collective-permute-start(bf16[32,4096]{1,0:T(8,128)(2,1)} %slice.381), channel_id=1, source_target_pairs={{0,96},{32,0},{64,32},{96,64},{1,97},{33,1},{65,33},{97,65},{2,98}... | collective-permute-start | bytes 786440 | tf_op jit(solution)/shard_map/ppermute | solution.py:116
  175.5 4.5 %collective-permute-done.1 = bf16[32,4096]{1,0:T(8,128)(2,1)} collective-permute-done((bf16[32,4096]{1,0:T(8,128)(2,1)}, bf16[32,4096]{1,0:T(8,128)(2,1)}, u32[]{:S(2)}, u32[]{:S(2)}) %collective-permute-start.1) | collective-permute-done | bytes 262176 | tf_op jit(solution)/shard_map/ppermute | solution.py:115
  180.1 1.1 pad_maximum_fusion
  181.3 2.0 maximum_bitcast_fusion
  183.3 1.6 copy.104
  184.8 2.0 reshape.97
  186.9 2.6 %copy.105 = bf16[4,4,4,8,4096]{4,3,2,1,0:T(8,128)(2,1)S(1)} copy(bf16[4,4,4,8,4096]{4,3,1,0,2:T(8,128)(2,1)} %bitcast.312) | data formatting | bytes 8388608 | tf_op jit(solution)/shard_map/transpose | solution.py:120
  189.8 1.3 fusion.20
  191.1 2.0 collective-permute-start.4
  193.1 1.2 collective-permute-done.4
  194.3 0.7 bitcast_add_fusion
  195.0 5.7 %all-to-all-start.2 = ((f32[8,64,128]{2,1,0:T(8,128)}), f32[8,64,128]{2,1,0:T(8,128)S(1)}, u32[]{:S(2)}, u32[]{:S(2)}) async-start(f32[8,64,128]{2,1,0:T(8,128)} %bitcast.127), calls=%async_computation.2 | async-start | bytes 524288 | tf_op jit(solution)/shard_map/all_to_all | solution.py:133
  200.7 11.1 %all-to-all-done.2 = f32[8,64,128]{2,1,0:T(8,128)S(1)} async-done(((f32[8,64,128]{2,1,0:T(8,128)}), f32[8,64,128]{2,1,0:T(8,128)S(1)}, u32[]{:S(2)}, u32[]{:S(2)}) %all-to-all-start.2) | async-done | bytes 262176 | tf_op jit(solution)/shard_map/all_to_all | solution.py:133
  211.8 0.6 fusion.162
  (180 shorter events, 13.9 us)
Async XLA Ops:
  6.5 51.0 %copy-start = (bf16[4,768,128]{2,1,0:T(8,128)(2,1)S(1)}, bf16[4,768,128]{2,1,0:T(8,128)(2,1)}, u32[]{:S(2)}) copy-start(bf16[4,768,128]{2,1,0:T(8,128)(2,1)} %param.15) | copy-start | bytes 2359300
  6.5 180.4 %all-gather.2.cloned.1.call-start = ((), (), s32[]{:S(2)}) async-start(), calls=%async_computation.3 | async-start | bytes 5242880 | tf_op jit(solution)/shard_map/all_gather | solution.py:106
  32.4 3.1 %copy-start.12 = (bf16[8,768,256]{2,1,0:T(8,128)(2,1)S(1)}, bf16[8,768,256]{2,1,0:T(8,128)(2,1)}, u32[]{:S(2)}) copy-start(bf16[8,768,256]{2,1,0:T(8,128)(2,1)} %param.11) | copy-start | bytes 9437188
  35.4 0.8 copy-start.56
  35.4 0.9 copy-start.58
  36.3 0.8 copy-start.29
  36.3 1.1 copy-start.65
  36.5 1.0 copy-start.60
  36.5 1.1 copy-start.62
  37.6 1.2 copy-start.26
  37.8 0.9 copy-start.55
  38.7 0.9 copy-start.24
  38.8 0.9 copy-start.52
  39.9 0.9 copy-start.49
  40.8 0.8 copy-start.20
  40.9 0.8 copy-start.43
  40.9 0.9 copy-start.45
  42.0 0.8 copy-start.40
  42.0 1.6 copy-start.42
  42.0 0.9 copy-start.64
  42.8 0.8 copy-start.14
  42.9 0.8 copy-start.36
  42.9 0.9 copy-start.38
  48.5 0.9 copy-start.6
  49.9 0.8 copy-start.8
  57.1 1.0 copy-start.28
  57.1 1.1 copy-start.57
  57.1 1.2 copy-start.59
  58.3 1.0 copy-start.30
  58.3 1.1 copy-start.61
  58.3 1.2 copy-start.63
  59.6 2.6 %copy-start.66 = (f32[12,64,256]{2,1,0:T(8,128)S(1)}, f32[12,64,256]{2,1,0:T(8,128)}, u32[]{:S(2)}) copy-start(f32[12,64,256]{2,1,0:T(8,128)} %copy-done.65) | copy-start | bytes 2359300
  60.1 5.0 %copy-start.1 = (f32[8,12,64,128]{3,2,0,1:T(8,128)}, f32[8,12,64,128]{3,2,0,1:T(8,128)S(1)}, u32[]{:S(2)}) copy-start(f32[8,12,64,128]{3,2,0,1:T(8,128)S(1)} %fusion.40) | copy-start | bytes 9437188
  60.1 2.1 copy-start.31
  60.1 2.1 copy-start.33
  60.1 2.9 %copy-start.34 = (f32[12,63,256]{2,1,0:T(8,128)S(1)}, f32[12,63,256]{2,1,0:T(8,128)}, u32[]{:S(2)}) copy-start(f32[12,63,256]{2,1,0:T(8,128)} %get-tuple-element.25) | copy-start | bytes 2322436
  60.1 3.7 %copy-start.35 = (f32[12,63,256]{2,1,0:T(8,128)S(1)}, f32[12,63,256]{2,1,0:T(8,128)}, u32[]{:S(2)}) copy-start(f32[12,63,256]{2,1,0:T(8,128)} %get-tuple-element.26) | copy-start | bytes 2322436
  63.8 1.3 copy-start.11
  67.4 2.7 %copy-start.9 = (bf16[12,64,256]{2,1,0:T(8,128)(2,1)S(1)}, bf16[12,64,256]{2,1,0:T(8,128)(2,1)}, u32[]{:S(2)}) copy-start(bf16[12,64,256]{2,1,0:T(8,128)(2,1)} %copy-done.8) | copy-start | bytes 1179652
  67.4 2.7 %copy-start.32 = (bf16[4,256,128]{2,1,0:T(8,128)(2,1)S(1)}, bf16[4,256,128]{2,1,0:T(8,128)(2,1)}, u32[]{:S(2)}) copy-start(bf16[4,256,128]{2,1,0:T(8,128)(2,1)} %param.14) | copy-start | bytes 786436
  67.4 5.0 %copy-start.25 = (bf16[12,64,256]{2,1,0:T(8,128)(2,1)S(1)}, bf16[12,64,256]{2,1,0:T(8,128)(2,1)}, u32[]{:S(2)}) copy-start(bf16[12,64,256]{2,1,0:T(8,128)(2,1)} %copy-done.24) | copy-start | bytes 1179652
  67.4 5.0 %copy-start.51 = (bf16[12,63,256]{2,1,0:T(8,128)(2,1)S(1)}, bf16[12,63,256]{2,1,0:T(8,128)(2,1)}, u32[]{:S(2)}) copy-start(bf16[12,63,256]{2,1,0:T(8,128)(2,1)} %copy-done.50) | copy-start | bytes 1161220
  67.4 5.0 %copy-start.53 = (bf16[12,63,256]{2,1,0:T(8,128)(2,1)S(1)}, bf16[12,63,256]{2,1,0:T(8,128)(2,1)}, u32[]{:S(2)}) copy-start(bf16[12,63,256]{2,1,0:T(8,128)(2,1)} %copy-done.52) | copy-start | bytes 1161220
  72.4 1.3 copy-start.7
  72.4 3.5 %copy-start.23 = (bf16[12,64,256]{2,1,0:T(8,128)(2,1)S(1)}, bf16[12,64,256]{2,1,0:T(8,128)(2,1)}, u32[]{:S(2)}) copy-start(bf16[12,64,256]{2,1,0:T(8,128)(2,1)} %copy-done.22) | copy-start | bytes 1179652
  72.4 3.5 %copy-start.48 = (bf16[12,63,256]{2,1,0:T(8,128)(2,1)S(1)}, bf16[12,63,256]{2,1,0:T(8,128)(2,1)}, u32[]{:S(2)}) copy-start(bf16[12,63,256]{2,1,0:T(8,128)(2,1)} %copy-done.47) | copy-start | bytes 1161220
  75.9 2.4 %copy-start.5 = (bf16[12,64,256]{2,1,0:T(8,128)(2,1)S(1)}, bf16[12,64,256]{2,1,0:T(8,128)(2,1)}, u32[]{:S(2)}) copy-start(bf16[12,64,256]{2,1,0:T(8,128)(2,1)} %copy-done.4) | copy-start | bytes 1179652
  75.9 4.6 %copy-start.21 = (bf16[12,64,256]{2,1,0:T(8,128)(2,1)S(1)}, bf16[12,64,256]{2,1,0:T(8,128)(2,1)}, u32[]{:S(2)}) copy-start(bf16[12,64,256]{2,1,0:T(8,128)(2,1)} %copy-done.20) | copy-start | bytes 1179652
  76.0 4.6 %copy-start.44 = (bf16[12,63,256]{2,1,0:T(8,128)(2,1)S(1)}, bf16[12,63,256]{2,1,0:T(8,128)(2,1)}, u32[]{:S(2)}) copy-start(bf16[12,63,256]{2,1,0:T(8,128)(2,1)} %copy-done.43) | copy-start | bytes 1161220
  76.0 4.6 %copy-start.46 = (bf16[12,63,256]{2,1,0:T(8,128)(2,1)S(1)}, bf16[12,63,256]{2,1,0:T(8,128)(2,1)}, u32[]{:S(2)}) copy-start(bf16[12,63,256]{2,1,0:T(8,128)(2,1)} %copy-done.45) | copy-start | bytes 1161220
  80.6 1.3 copy-start.3
  80.6 3.6 %copy-start.19 = (bf16[12,64,256]{2,1,0:T(8,128)(2,1)S(1)}, bf16[12,64,256]{2,1,0:T(8,128)(2,1)}, u32[]{:S(2)}) copy-start(bf16[12,64,256]{2,1,0:T(8,128)(2,1)} %copy-done.18) | copy-start | bytes 1179652
  80.6 3.6 %copy-start.41 = (bf16[12,63,256]{2,1,0:T(8,128)(2,1)S(1)}, bf16[12,63,256]{2,1,0:T(8,128)(2,1)}, u32[]{:S(2)}) copy-start(bf16[12,63,256]{2,1,0:T(8,128)(2,1)} %copy-done.40) | copy-start | bytes 1161220
  84.3 4.7 %copy-start.15 = (bf16[12,64,256]{2,1,0:T(8,128)(2,1)S(1)}, bf16[12,64,256]{2,1,0:T(8,128)(2,1)}, u32[]{:S(2)}) copy-start(bf16[12,64,256]{2,1,0:T(8,128)(2,1)} %copy-done.14) | copy-start | bytes 1179652
  84.3 4.7 %copy-start.37 = (bf16[12,63,256]{2,1,0:T(8,128)(2,1)S(1)}, bf16[12,63,256]{2,1,0:T(8,128)(2,1)}, u32[]{:S(2)}) copy-start(bf16[12,63,256]{2,1,0:T(8,128)(2,1)} %copy-done.36) | copy-start | bytes 1161220
  84.3 4.7 %copy-start.39 = (bf16[12,63,256]{2,1,0:T(8,128)(2,1)S(1)}, bf16[12,63,256]{2,1,0:T(8,128)(2,1)}, u32[]{:S(2)}) copy-start(bf16[12,63,256]{2,1,0:T(8,128)(2,1)} %copy-done.38) | copy-start | bytes 1161220
  89.0 1.3 copy-start.17
  156.4 14.6 %collective-permute-start = (bf16[64,4096]{1,0:T(8,128)(2,1)S(1)}, bf16[64,4096]{1,0:T(8,128)(2,1)S(1)}, u32[]{:S(2)}, u32[]{:S(2)}) collective-permute-start(bf16[64,4096]{1,0:T(8,128)(2,1)S(1)} %reshape.66), channel_id=1, source_target_pairs={{0,32},{32,64},{64,96},{96,0},{1,33},{33,65},{65,97},{97,1},{2,34}... | collective-permute-start | bytes 1572872 | tf_op jit(solution)/shard_map/ppermute | solution.py:112
  157.8 14.0 %collective-permute-start.2 = (bf16[64,4096]{1,0:T(8,128)(2,1)S(1)}, bf16[64,4096]{1,0:T(8,128)(2,1)S(1)}, u32[]{:S(2)}, u32[]{:S(2)}) collective-permute-start(bf16[64,4096]{1,0:T(8,128)(2,1)S(1)} %reshape.66), channel_id=1, source_target_pairs={{0,96},{32,0},{64,32},{96,64},{1,97},{33,1},{65,33},{97,65},{2,98}... | collective-permute-start | bytes 1572872 | tf_op jit(solution)/shard_map/ppermute | solution.py:113
  171.7 8.3 %collective-permute-start.1 = (bf16[32,4096]{1,0:T(8,128)(2,1)}, bf16[32,4096]{1,0:T(8,128)(2,1)}, u32[]{:S(2)}, u32[]{:S(2)}) collective-permute-start(bf16[32,4096]{1,0:T(8,128)(2,1)} %slice.380), channel_id=1, source_target_pairs={{0,32},{32,64},{64,96},{96,0},{1,33},{33,65},{65,97},{97,1},{2,34}... | collective-permute-start | bytes 786440 | tf_op jit(solution)/shard_map/ppermute | solution.py:115
  172.5 7.6 %collective-permute-start.3 = (bf16[32,4096]{1,0:T(8,128)(2,1)}, bf16[32,4096]{1,0:T(8,128)(2,1)}, u32[]{:S(2)}, u32[]{:S(2)}) collective-permute-start(bf16[32,4096]{1,0:T(8,128)(2,1)} %slice.381), channel_id=1, source_target_pairs={{0,96},{32,0},{64,32},{96,64},{1,97},{33,1},{65,33},{97,65},{2,98}... | collective-permute-start | bytes 786440 | tf_op jit(solution)/shard_map/ppermute | solution.py:116
  186.9 2.9 %copy-start.13 = (bf16[4,64,4096,1]{2,1,0,3:T(8,128)(2,1)S(1)}, bf16[4,64,4096,1]{2,1,0,3:T(8,128)(2,1)}, u32[]{:S(2)}) copy-start(bf16[4,64,4096,1]{2,1,0,3:T(8,128)(2,1)} %reshape.97) | copy-start | bytes 6291460
  191.1 3.2 %collective-permute-start.4 = (f32[2,4,64,128]{3,2,1,0:T(8,128)S(1)}, f32[2,4,64,128]{3,2,1,0:T(8,128)S(1)}, u32[]{:S(2)}, u32[]{:S(2)}) collective-permute-start(f32[2,4,64,128]{3,2,1,0:T(8,128)S(1)} %bitcast.318), channel_id=1, source_target_pairs={{0,16},{16,0},{1,17},{17,1},{2,18},{18,2},{3,19},{19,3},{4,20},{20... | collective-permute-start | bytes 786440 | tf_op jit(solution)/shard_map/ppermute | solution.py:131
  195.0 16.8 %all-to-all-start.2 = ((f32[8,64,128]{2,1,0:T(8,128)}), f32[8,64,128]{2,1,0:T(8,128)S(1)}, u32[]{:S(2)}, u32[]{:S(2)}) async-start(f32[8,64,128]{2,1,0:T(8,128)} %bitcast.127), calls=%async_computation.2 | async-start | bytes 524288 | tf_op jit(solution)/shard_map/all_to_all | solution.py:133
  (10 other events, 7.6 us)
Sparse Core Ops, SparseCore 0:
  135.7 50.0 all-gather.1
